TPU v7x, 256 devices: a whole 4x4x8 slice. The times are simulated.
256 devices in a mesh: row: 16 (over y_lo, x, core), col: 16 (over y_hi, z).
Axes of the slice: x: 4, y: 4 (y_hi: 2, y_lo: 2; y = y_hi * 2 + y_lo), z: 8, core: 2. Of those that a mesh axis runs over, the one named last changes fastest.
Arguments:
- tiles: bfloat16 [16, 16, 128, 128, 128], P('row', 'col'), as said below
- coords: int32 [16, 16, 2, 128], P('row', 'col'), may hold values from 0 to 63, as said below
- counts: int32 [16, 16], P('row', 'col'), may hold values from 1 to 128, as said below
- valid: int32 [131072], P(('row', 'col')), may hold values 0 or 1
- start: float32 [8, 131072], P(None, ('row', 'col'))
- rotations: float32 [2, 8, 24], replicated, as said below
Outputs:
- eigenmaps: float32 [8, 131072], P(None, ('row', 'col'))
- ritz: float32 [8, 8], replicated
Inputs may be any that keep to these rules, and one draw needn't show every extreme that they name: coords[r, c, 0, s] is a block row from 0 to 63 and coords[r, c, 1, s] a block column from 0 to 63; the live slots of one owner name distinct blocks, each on or above the block diagonal (g_row <= g_col). The live slots of an owner are the first counts[r, c] of its list; one owner in grid row 0 has all 128 live. `tiles`: nonnegative; a tile on the block diagonal is symmetric. The Rayleigh-Ritz coefficients of the current vectors, rotations[t, :, 0 to 7], form a matrix whose diagonal dominates its rows.
All inputs are finite; a program needn't handle non-finite values. No bound on the sum of `valid` on one device may be relied on, other than what follows from the above.
Results may differ from a plain program's by a relative error of at most 0.0013.
Values may be sent and summed in bfloat16 or wider, within the bound.
No kernel may reach another device: no remote copies, remote signals or barrier semaphores. Data moves between devices by JAX's collectives and lax.ppermute only.
A program may use at most 64 MiB of HBM per device.

v0:
```python
import jax
import jax.numpy as jnp
from jax import lax
from jax.sharding import PartitionSpec as P


def matmul_high(left, right):
    return jnp.dot(left, right, precision=lax.Precision.HIGHEST)


def lower_inverse(lower_factor):
    order_size = lower_factor.shape[0]
    identity = jnp.eye(order_size, dtype=lower_factor.dtype)
    inverse_rows = []
    for row_at in range(order_size):
        partial_row = identity[row_at]
        for prior_at in range(row_at):
            partial_row = partial_row - lower_factor[row_at, prior_at] * inverse_rows[prior_at]
        inverse_rows.append(partial_row / lower_factor[row_at, row_at])
    return jnp.stack(inverse_rows)


def settle(new_vecs, new_images, new_steps, step_images, gram_x, gram_ax, node_total):
    lower_factor = jnp.linalg.cholesky(gram_x / node_total)
    inverse = lower_inverse(lower_factor)
    theta = matmul_high(matmul_high(inverse, gram_ax / node_total), inverse.T)
    return (
        matmul_high(inverse, new_vecs),
        matmul_high(inverse, new_images),
        matmul_high(inverse, new_steps),
        matmul_high(inverse, step_images),
        theta,
    )


def gram_sums(new_vecs, new_images):
    return lax.psum(
        (matmul_high(new_vecs, new_vecs.T), matmul_high(new_images, new_vecs.T)), ("row", "col")
    )


def local_terms(
    part_tiles, part_rows, part_cols, weight_direct, weight_mirror, col_blocks, row_blocks
):
    row_span = row_blocks.shape[1]
    col_span = col_blocks.shape[1]
    col_values = jnp.take(col_blocks, part_cols, axis=1)
    row_values = jnp.take(row_blocks, part_rows, axis=1)
    direct = (
        jnp.einsum("sut,cst->csu", part_tiles, col_values, preferred_element_type=jnp.float32)
        * weight_direct[None, :, None]
    )
    mirror = (
        jnp.einsum("sut,csu->cst", part_tiles, row_values, preferred_element_type=jnp.float32)
        * weight_mirror[None, :, None]
    )
    pick_rows = (part_rows[:, None] == jnp.arange(row_span, dtype=jnp.int32)[None, :]).astype(
        jnp.float32
    )
    pick_cols = (part_cols[:, None] == jnp.arange(col_span, dtype=jnp.int32)[None, :]).astype(
        jnp.float32
    )
    rows_sum = jnp.einsum("sp,csu->cpu", pick_rows, direct, precision=lax.Precision.HIGHEST)
    cols_sum = jnp.einsum("sq,cst->cqt", pick_cols, mirror, precision=lax.Precision.HIGHEST)
    return (rows_sum, cols_sum)


def body(tiles, coords, counts, valid, start, rotations):
    row_count = lax.axis_size("row")
    col_count = lax.axis_size("col")
    row_index = lax.axis_index("row")
    col_index = lax.axis_index("col")
    slot_count = tiles.shape[2]
    tile_side = tiles.shape[3]
    stretch_nodes = valid.shape[0]
    per_stretch = stretch_nodes // tile_side
    row_span = col_count * per_stretch
    col_span = row_count * per_stretch
    node_total = jnp.float32(stretch_nodes * row_count * col_count)
    vec_count = start.shape[0]
    flat_tiles = tiles.reshape(slot_count, tile_side, tile_side)
    block_rows = coords[0, 0, 0]
    block_cols = coords[0, 0, 1]
    live_count = counts[0, 0]
    global_rows = row_index * row_span + block_rows
    global_cols = (
        block_cols // per_stretch * col_count + col_index
    ) * per_stretch + block_cols % per_stretch
    live = (jnp.arange(slot_count, dtype=jnp.int32) < live_count).astype(jnp.float32)
    mirror_weight = live * (global_rows != global_cols).astype(jnp.float32)

    def graph_product(vectors):
        width = vectors.shape[0]
        short = vectors.astype(jnp.bfloat16)
        col_side = lax.all_gather(short, "row", axis=1, tiled=True)
        row_side = lax.all_gather(short, "col", axis=1, tiled=True)
        col_blocks = col_side.reshape(width, col_span, tile_side)
        row_blocks = row_side.reshape(width, row_span, tile_side)
        rows_total, cols_total = local_terms(
            flat_tiles, block_rows, block_cols, live, mirror_weight, col_blocks, row_blocks
        )
        direct_part = lax.psum_scatter(
            rows_total.reshape(width, row_span * tile_side), "col", scatter_dimension=1, tiled=True
        )
        mirror_part = lax.psum_scatter(
            cols_total.reshape(width, col_span * tile_side), "row", scatter_dimension=1, tiled=True
        )
        return direct_part + mirror_part

    node_mask = valid.astype(jnp.float32)
    first_vecs = start * node_mask[None, :]
    raw = graph_product(jnp.concatenate([node_mask[None, :], first_vecs], 0))
    degree = raw[0]
    first_images = node_mask[None, :] * (degree[None, :] * first_vecs - raw[1:])
    zero_steps = jnp.zeros_like(first_vecs)
    gram_x, gram_ax = gram_sums(first_vecs, first_images)
    vecs, images, steps, step_images, theta = settle(
        first_vecs, first_images, zero_steps, zero_steps, gram_x, gram_ax, node_total
    )
    for turn in range(rotations.shape[0]):
        resid = images - matmul_high(theta, vecs)
        resid_images = node_mask[None, :] * (degree[None, :] * resid - graph_product(resid))
        stacked = jnp.concatenate([vecs, resid, steps], 0)
        stacked_images = jnp.concatenate([images, resid_images, step_images], 0)
        rotation = rotations[turn]
        new_vecs = matmul_high(rotation, stacked)
        new_images = matmul_high(rotation, stacked_images)
        gram_x, gram_ax = gram_sums(new_vecs, new_images)
        new_steps = matmul_high(rotation[:, vec_count:], stacked[vec_count:])
        new_step_images = matmul_high(rotation[:, vec_count:], stacked_images[vec_count:])
        vecs, images, steps, step_images, theta = settle(
            new_vecs, new_images, new_steps, new_step_images, gram_x, gram_ax, node_total
        )
    return (vecs, theta)


def solution(mesh):
    in_specs = (
        P("row", "col", None, None, None),
        P("row", "col", None, None),
        P("row", "col"),
        P(("row", "col")),
        P(None, ("row", "col")),
        P(),
    )
    out_specs = (P(None, ("row", "col")), P())
    return jax.shard_map(body, mesh=mesh, in_specs=in_specs, out_specs=out_specs, check_vma=False)
```

profile of v0, /device:TPU:1, one launch (start us, length us, event | category | flops | bytes accessed | tf_op | source)
XLA Modules:
  0.0 1272.5 jit_solution(13226586753436208169)
XLA Ops:
  7.2 0.8 compare_and_fusion
  8.0 0.8 slice_bitcast_fusion.2
  9.5 0.7 multiply_convert_fusion
  10.2 39.4 %all_gather.19 = bf16[9,8192]{1,0:T(8,128)(2,1)S(1)} all-gather(bf16[9,512]{1,0:T(8,128)(2,1)S(1)} %pad_maximum_fusion.8), channel_id=1, replica_groups=mesh['row'=16,'col'=16] {'col'}, dimensions={1}, use_global_device_ids=true | all-gather | bytes 156672 | tf_op jit(solution)/shard_map/all_gather | solution.py:96
  50.5 0.7 gather_fusion.1
  51.2 3.4 fusion.8
  55.3 1.1 copy.34
  56.4 26.8 %all_gather.18 = bf16[9,8192]{1,0:T(8,128)(2,1)S(1)} all-gather(bf16[9,512]{1,0:T(8,128)(2,1)S(1)} %pad_maximum_fusion.8), channel_id=1, replica_groups=mesh['row'=16,'col'=16] {'row'}, dimensions={1}, use_global_device_ids=true | all-gather | bytes 156672 | tf_op jit(solution)/shard_map/all_gather | solution.py:95
  83.4 0.7 gather_fusion
  84.2 4.5 fusion.10
  89.3 1.1 copy.32
  90.7 26.8 %reduce-scatter.9.cloned.1.call-done = f32[9,512]{1,0:T(8,128)} async-done(((f32[9,8192]{1,0:T(8,128)}), f32[9,512]{1,0:T(8,128)}) %reduce-scatter.9.cloned.1.call-update) | async-done | bytes 18448 | tf_op jit(solution)/shard_map/reduce_scatter | solution.py:105
  117.5 198.4 %reduce-scatter.7.cloned.1.call-done = f32[9,512]{1,0:T(8,128)} async-done(((f32[9,8192]{1,0:T(8,128)}), f32[9,512]{1,0:T(8,128)}) %reduce-scatter.7.cloned.1.call-update) | async-done | bytes 18448 | tf_op jit(solution)/shard_map/reduce_scatter | solution.py:102
  315.9 0.8 add.100
  316.8 80.0 %all-reduce.2 = (f32[8,8]{0,1:T(8,128)S(1)}, f32[8,8]{0,1:T(8,128)S(1)}) all-reduce(f32[8,8]{0,1:T(8,128)S(1)} %fusion.95, f32[8,8]{0,1:T(8,128)S(1)} %fusion.87), channel_id=1, replica_groups=mesh['row'=16,'col'=16] {'row','col'}, use_global_device_ids=true, to_apply=%region_0.1 | all-reduce | flops 128 | bytes 1024 | tf_op jit(solution)/shard_map/psum | solution.py:37
  396.9 0.7 cholesky.59
  398.9 0.7 fusion.147
  399.6 0.7 fusion.148
  400.4 22.6 %subtract_divide_fusion.14 = (f32[1,8]{1,0:T(1,128)S(1)}, f32[1,8]{1,0:T(1,128)S(1)}, f32[1,8]{1,0:T(1,128)S(1)}, f32[1,8]{1,0:T(1,128)S(1)}, f32[1,8]{1,0:T(1,1...) fusion(f32[]{:T(128)} %bitcast.36, f32[]{:T(128)} %bitcast.35, f32[]{:T(128)} %bitcast.34, ...), kind=kLoop, calls=%fused_computation.199 | loop fusion | flops 512 | bytes 656 | tf_op jit(solution)/shard_map/div | solution.py:19
  423.7 31.7 %all_gather.21 = bf16[8,8192]{1,0:T(8,128)(2,1)S(1)} all-gather(bf16[8,512]{1,0:T(8,128)(2,1)S(1)} %get-tuple-element.153), channel_id=1, replica_groups=mesh['row'=16,'col'=16] {'col'}, dimensions={1}, use_global_device_ids=true | all-gather | bytes 139264 | tf_op jit(solution)/shard_map/all_gather | solution.py:96
  455.4 24.9 %all_gather.20 = bf16[8,8192]{1,0:T(8,128)(2,1)S(1)} all-gather(bf16[8,512]{1,0:T(8,128)(2,1)S(1)} %get-tuple-element.153), channel_id=1, replica_groups=mesh['row'=16,'col'=16] {'row'}, dimensions={1}, use_global_device_ids=true | all-gather | bytes 139264 | tf_op jit(solution)/shard_map/all_gather | solution.py:95
  481.0 3.4 fusion.4
  484.9 0.8 copy.69
  486.5 4.5 fusion.6
  491.5 0.9 copy.70
  493.5 45.6 %reduce-scatter.13.cloned.1.call-done = f32[8,512]{1,0:T(8,128)} async-done(((f32[8,8192]{1,0:T(8,128)}), f32[8,512]{1,0:T(8,128)}) %reduce-scatter.13.cloned.1.call-update) | async-done | bytes 16400 | tf_op jit(solution)/shard_map/reduce_scatter | solution.py:105
  539.1 197.0 %reduce-scatter.11.cloned.1.call-done = f32[8,512]{1,0:T(8,128)} async-done(((f32[8,8192]{1,0:T(8,128)}), f32[8,512]{1,0:T(8,128)}) %reduce-scatter.11.cloned.1.call-update) | async-done | bytes 16400 | tf_op jit(solution)/shard_map/reduce_scatter | solution.py:102
  736.1 0.7 subtract_multiply_fusion.1
  737.2 79.8 %all-reduce.1 = (f32[8,8]{0,1:T(8,128)S(1)}, f32[8,8]{0,1:T(8,128)S(1)}) all-reduce(f32[8,8]{0,1:T(8,128)S(1)} %fusion.152, f32[8,8]{0,1:T(8,128)S(1)} %fusion.155), channel_id=1, replica_groups=mesh['row'=16,'col'=16] {'row','col'}, use_global_device_ids=true, to_apply=%region_6.9 | all-reduce | flops 128 | bytes 1024 | tf_op jit(solution)/shard_map/psum | solution.py:37
  817.1 0.7 cholesky.70
  819.1 0.7 fusion.145
  819.8 0.7 fusion.146
  820.6 22.6 %subtract_divide_fusion.7 = (f32[1,8]{1,0:T(1,128)S(1)}, f32[1,8]{1,0:T(1,128)S(1)}, f32[1,8]{1,0:T(1,128)S(1)}, f32[1,8]{1,0:T(1,128)S(1)}, f32[1,8]{1,0:T(1,12...) fusion(f32[]{:T(128)} %bitcast.87, f32[]{:T(128)} %bitcast.86, f32[]{:T(128)} %bitcast.85, ...), kind=kLoop, calls=%fused_computation.190 | loop fusion | flops 512 | bytes 656 | tf_op jit(solution)/shard_map/div | solution.py:19
  843.9 31.8 %all_gather.23 = bf16[8,8192]{1,0:T(8,128)(2,1)S(1)} all-gather(bf16[8,512]{1,0:T(8,128)(2,1)S(1)} %get-tuple-element.155), channel_id=1, replica_groups=mesh['row'=16,'col'=16] {'col'}, dimensions={1}, use_global_device_ids=true | all-gather | bytes 139264 | tf_op jit(solution)/shard_map/all_gather | solution.py:96
  875.7 24.9 %all_gather.22 = bf16[8,8192]{1,0:T(8,128)(2,1)S(1)} all-gather(bf16[8,512]{1,0:T(8,128)(2,1)S(1)} %get-tuple-element.155), channel_id=1, replica_groups=mesh['row'=16,'col'=16] {'row'}, dimensions={1}, use_global_device_ids=true | all-gather | bytes 139264 | tf_op jit(solution)/shard_map/all_gather | solution.py:95
  901.3 3.4 fusion
  905.2 0.8 copy.67
  906.8 4.5 fusion.2
  911.8 0.9 copy.68
  914.2 45.1 %reduce-scatter.17.cloned.1.call-done = f32[8,512]{1,0:T(8,128)} async-done(((f32[8,8192]{1,0:T(8,128)}), f32[8,512]{1,0:T(8,128)}) %reduce-scatter.17.cloned.1.call-update) | async-done | bytes 16400 | tf_op jit(solution)/shard_map/reduce_scatter | solution.py:105
  959.3 197.3 %reduce-scatter.15.cloned.1.call-done = f32[8,512]{1,0:T(8,128)} async-done(((f32[8,8192]{1,0:T(8,128)}), f32[8,512]{1,0:T(8,128)}) %reduce-scatter.15.cloned.1.call-update) | async-done | bytes 16400 | tf_op jit(solution)/shard_map/reduce_scatter | solution.py:102
  1156.6 0.7 subtract_multiply_fusion
  1158.1 79.7 %all-reduce = (f32[8,8]{0,1:T(8,128)S(1)}, f32[8,8]{0,1:T(8,128)S(1)}) all-reduce(f32[8,8]{0,1:T(8,128)S(1)} %fusion.158, f32[8,8]{0,1:T(8,128)S(1)} %fusion.161), channel_id=1, replica_groups=mesh['row'=16,'col'=16] {'row','col'}, use_global_device_ids=true, to_apply=%region_10.14 | all-reduce | flops 128 | bytes 1024 | tf_op jit(solution)/shard_map/psum | solution.py:37
  1240.0 0.7 fusion.143
  1240.7 0.7 fusion.144
  1241.4 22.6 %subtract_divide_fusion = (f32[1,8]{1,0:T(1,128)S(1)}, f32[1,8]{1,0:T(1,128)S(1)}, f32[1,8]{1,0:T(1,128)S(1)}, f32[1,8]{1,0:T(1,128)S(1)}, f32[1,8]{1,0:T(1,128)...) fusion(f32[]{:T(128)} %bitcast.133, f32[]{:T(128)} %bitcast.132, f32[]{:T(128)} %bitcast.131, ...), kind=kLoop, calls=%fused_computation.183 | loop fusion | flops 512 | bytes 656 | tf_op jit(solution)/shard_map/div | solution.py:19
  1264.0 0.7 fusion.159
  1264.9 0.7 fusion.162
  (93 shorter events, 17.8 us)
Async XLA Ops:
  7.2 47.5 %copy-start.2 = (s32[1,1,2,128]{3,2,1,0:T(2,128)S(1)}, s32[1,1,2,128]{3,2,1,0:T(2,128)}, u32[]{:S(2)}) copy-start(s32[1,1,2,128]{3,2,1,0:T(2,128)} %param.12) | copy-start | bytes 3076
  7.2 110.3 %reduce-scatter.9.cloned.1.call-start = ((), (), s32[]{:S(2)}) async-start(), calls=%async_computation.7 | async-start | bytes 557056 | tf_op jit(solution)/shard_map/reduce_scatter | solution.py:105
  56.4 259.5 %reduce-scatter.7.cloned.1.call-start = ((), (), s32[]{:S(2)}) async-start(), calls=%async_computation.6 | async-start | bytes 557056 | tf_op jit(solution)/shard_map/reduce_scatter | solution.py:102
  84.1 6.4 copy-start.1
  84.2 6.4 copy-start
  90.4 448.7 %reduce-scatter.13.cloned.1.call-start = ((), (), s32[]{:S(2)}) async-start(), calls=%async_computation.9 | async-start | bytes 278528 | tf_op jit(solution)/shard_map/reduce_scatter | solution.py:105
  485.8 250.3 %reduce-scatter.11.cloned.1.call-start = ((), (), s32[]{:S(2)}) async-start(), calls=%async_computation.8 | async-start | bytes 278528 | tf_op jit(solution)/shard_map/reduce_scatter | solution.py:102
  492.5 466.8 %reduce-scatter.17.cloned.1.call-start = ((), (), s32[]{:S(2)}) async-start(), calls=%async_computation.11 | async-start | bytes 278528 | tf_op jit(solution)/shard_map/reduce_scatter | solution.py:105
  906.1 250.5 %reduce-scatter.15.cloned.1.call-start = ((), (), s32[]{:S(2)}) async-start(), calls=%async_computation.10 | async-start | bytes 278528 | tf_op jit(solution)/shard_map/reduce_scatter | solution.py:102
Sparse Core Ops, SparseCore 0:
  56.5 60.9 reduce-scatter.8
  121.8 194.0 reduce-scatter.6
  485.9 53.1 reduce-scatter.12
  543.2 192.8 reduce-scatter.10
  906.2 53.0 reduce-scatter.16
  963.4 193.1 reduce-scatter.14
where the time goes:
time: 1270 us
  waiting for transfers between devices  710 us (56%)
  blocking collectives  419 us (33%)
  other arithmetic  78.4 us (6%)
  matrix products  33.7 us (3%)
  local copies, waits for them, and re-layouts  15.6 us (1%)
  between operations  15.1 us (1%)
    reduce_scatter x3, waiting for transfers between devices, graph_product(): lax.psum_scatter(rows_total.reshape(width, row_span * tile_side), 'col',...  593 us
    psum x3, blocking collectives, gram_sums(): lax.psum((matmul_high(new_vecs, new_vecs.T), matmul_high(new_images, new_...  239 us
    reduce_scatter x3, waiting for transfers between devices, graph_product(): lax.psum_scatter(cols_total.reshape(width, col_span * tile_side), 'row',...  118 us
    all_gather x3, blocking collectives, graph_product(): row_side = lax.all_gather(short, 'col', axis=1, tiled=True)  103 us
    all_gather x3, blocking collectives, graph_product(): col_side = lax.all_gather(short, 'row', axis=1, tiled=True)  76.7 us
    div x3, other arithmetic, lower_inverse(): inverse_rows.append(partial_row / lower_factor[row_at, row_at])  67.8 us
  transfers between devices with their start and end apart: 6, of which 6 were waited for; matrix products, arithmetic and copies ran while one was open for 2% of the time, Pallas kernels for 0%

commit v1 on v0

--- a/solution.py
+++ b/solution.py
@@ -33,10 +33,28 @@
     )
 
 
+def gather_by_exchange(local, axis):
+    count = lax.axis_size(axis)
+    copies = jnp.broadcast_to(local[None], (count,) + local.shape)
+    held = lax.all_to_all(copies, axis, 0, 0, tiled=True)
+    return jnp.swapaxes(held, 0, 1).reshape(local.shape[0], count * local.shape[1])
+
+
+def scatter_sum_by_exchange(total, axis):
+    count = lax.axis_size(axis)
+    width, length = total.shape
+    chunks = jnp.swapaxes(total.reshape(width, count, length // count), 0, 1)
+    held = lax.all_to_all(chunks, axis, 0, 0, tiled=True)
+    return jnp.sum(held, axis=0)
+
+
 def gram_sums(new_vecs, new_images):
-    return lax.psum(
-        (matmul_high(new_vecs, new_vecs.T), matmul_high(new_images, new_vecs.T)), ("row", "col")
-    )
+    local = jnp.stack([matmul_high(new_vecs, new_vecs.T), matmul_high(new_images, new_vecs.T)])
+    count = lax.axis_size("row") * lax.axis_size("col")
+    copies = jnp.broadcast_to(local[None], (count,) + local.shape)
+    held = lax.all_to_all(copies, ("row", "col"), 0, 0, tiled=True)
+    total = jnp.sum(held, axis=0)
+    return total[0], total[1]
 
 
 def local_terms(
@@ -92,19 +110,15 @@
     def graph_product(vectors):
         width = vectors.shape[0]
         short = vectors.astype(jnp.bfloat16)
-        col_side = lax.all_gather(short, "row", axis=1, tiled=True)
-        row_side = lax.all_gather(short, "col", axis=1, tiled=True)
+        col_side = gather_by_exchange(short, "row")
+        row_side = gather_by_exchange(short, "col")
         col_blocks = col_side.reshape(width, col_span, tile_side)
         row_blocks = row_side.reshape(width, row_span, tile_side)
         rows_total, cols_total = local_terms(
             flat_tiles, block_rows, block_cols, live, mirror_weight, col_blocks, row_blocks
         )
-        direct_part = lax.psum_scatter(
-            rows_total.reshape(width, row_span * tile_side), "col", scatter_dimension=1, tiled=True
-        )
-        mirror_part = lax.psum_scatter(
-            cols_total.reshape(width, col_span * tile_side), "row", scatter_dimension=1, tiled=True
-        )
+        direct_part = scatter_sum_by_exchange(rows_total.reshape(width, row_span * tile_side), "col")
+        mirror_part = scatter_sum_by_exchange(cols_total.reshape(width, col_span * tile_side), "row")
         return direct_part + mirror_part
 
     node_mask = valid.astype(jnp.float32)

time: 1270 us -> 352 us (0.28)
  waiting for transfers between devices: 710 us -> 100 us
  blocking collectives: 419 us -> 32.3 us
  starting transfers between devices: 0.25 us -> 76.1 us
  between operations: 15.1 us -> 1.82 us
    reduce_scatter x6 -> x0, waiting for transfers between devices: 710 us -> none  [the longest x3 593 us: graph_product(): lax.psum_scatter(rows_total.reshape(width, row_span * tile_side), 'col',...]
    psum x3 -> x0, blocking collectives: 239 us -> none  [gram_sums(): lax.psum((matmul_high(new_vecs, new_vecs.T), matmul_high(new_images, new_...]
    all_gather x6 -> x0, blocking collectives: 180 us -> none  [the longest x3 103 us: graph_product(): row_side = lax.all_gather(short, 'col', axis=1, tiled=True)]
    all_to_all x0 -> x13, waiting for transfers between devices: none -> 100 us  [the longest x6 40.3 us: scatter_sum_by_exchange(): held = lax.all_to_all(chunks, axis, 0, 0, tiled=True)]
    all_to_all x0 -> x13, starting transfers between devices: none -> 76.1 us  [the longest x5 29.1 us: gather_by_exchange(): held = lax.all_to_all(copies, axis, 0, 0, tiled=True)]
    all_to_all x0 -> x2, blocking collectives: none -> 32.3 us  [the longest x1 21.7 us: gram_sums(): held = lax.all_to_all(copies, ('row', 'col'), 0, 0, tiled=True)]
  transfers between devices with their start and end apart: 6 -> 13, of which waited for: 6 -> 13; matrix products, arithmetic and copies ran while one was open for 2% -> 7% of each run, Pallas kernels for 0% -> 0%
where the time goes in v1:
time: 352 us; the launch traced here: 349 us
  waiting for transfers between devices  100 us (28%)
  other arithmetic  80.8 us (23%)
  starting transfers between devices  76.1 us (22%)
  blocking collectives  32.3 us (9%)
  matrix products  31.6 us (9%)
  local copies, waits for them, and re-layouts  26.7 us (8%)
    div x3, other arithmetic, lower_inverse(): inverse_rows.append(partial_row / lower_factor[row_at, row_at])  67.7 us
    all_to_all x6, waiting for transfers between devices, scatter_sum_by_exchange(): held = lax.all_to_all(chunks, axis, 0, 0, tiled=True)  40.3 us
    all_to_all x5, waiting for transfers between devices, gather_by_exchange(): held = lax.all_to_all(copies, axis, 0, 0, tiled=True)  34.6 us
    all_to_all x5, starting transfers between devices, gather_by_exchange(): held = lax.all_to_all(copies, axis, 0, 0, tiled=True)  29.1 us
    all_to_all x6, starting transfers between devices, scatter_sum_by_exchange(): held = lax.all_to_all(chunks, axis, 0, 0, tiled=True)  27.8 us
    all_to_all x2, waiting for transfers between devices, gram_sums(): held = lax.all_to_all(copies, ('row', 'col'), 0, 0, tiled=True)  25.2 us
    all_to_all x1, blocking collectives, gram_sums(): held = lax.all_to_all(copies, ('row', 'col'), 0, 0, tiled=True)  21.7 us
    all_to_all x2, starting transfers between devices, gram_sums(): held = lax.all_to_all(copies, ('row', 'col'), 0, 0, tiled=True)  19.2 us
  transfers between devices with their start and end apart: 13, of which 13 were waited for; matrix products, arithmetic and copies ran while one was open for 7% of the time, Pallas kernels for 0%

profile of v1, /device:TPU:1, one launch (start us, length us, event | category | flops | bytes accessed | tf_op | source)
XLA Modules:
  0.0 349.3 jit_solution(943247763348093600)
XLA Ops:
  2.8 6.8 %all-to-all-start = ((bf16[16,9,512]{2,1,0:T(8,128)(2,1)}), bf16[16,9,512]{2,1,0:T(8,128)(2,1)S(1)}, u32[]{:S(2)}, u32[]{:S(2)}) async-start(bf16[16,9,512]{2,1,0:T(8,128)(2,1)} %broadcast_in_dim.30), calls=%async_computation | async-start | bytes 524288 | tf_op jit(solution)/shard_map/all_to_all | solution.py:39
  11.8 5.0 %all-to-all-done = bf16[16,9,512]{2,1,0:T(8,128)(2,1)S(1)} async-done(((bf16[16,9,512]{2,1,0:T(8,128)(2,1)}), bf16[16,9,512]{2,1,0:T(8,128)(2,1)S(1)}, u32[]{:S(2)}, u32[]{:S(2)}) %all-to-all-start) | async-done | bytes 147488 | tf_op jit(solution)/shard_map/all_to_all | solution.py:39
  16.8 10.6 %all-to-all-start.2 = ((bf16[16,9,512]{2,1,0:T(8,128)(2,1)}), bf16[16,9,512]{2,1,0:T(8,128)(2,1)S(1)}, u32[]{:S(2)}, u32[]{:S(2)}) async-start(bf16[16,9,512]{2,1,0:T(8,128)(2,1)} %broadcast_in_dim.30), calls=%async_computation.2 | async-start | bytes 524288 | tf_op jit(solution)/shard_map/all_to_all | solution.py:39
  29.2 7.6 %all-to-all-done.2 = bf16[16,9,512]{2,1,0:T(8,128)(2,1)S(1)} async-done(((bf16[16,9,512]{2,1,0:T(8,128)(2,1)}), bf16[16,9,512]{2,1,0:T(8,128)(2,1)S(1)}, u32[]{:S(2)}, u32[]{:S(2)}) %all-to-all-start.2) | async-done | bytes 147488 | tf_op jit(solution)/shard_map/all_to_all | solution.py:39
  37.9 3.4 fusion.21
  41.9 1.0 copy.162
  42.9 6.4 %all-to-all-start.3 = ((f32[16,9,512]{2,1,0:T(8,128)}), f32[16,9,512]{2,1,0:T(8,128)S(1)}, u32[]{:S(2)}, u32[]{:S(2)}) async-start(f32[16,9,512]{2,1,0:T(8,128)} %bitcast.327), calls=%async_computation.3 | async-start | bytes 1048576 | tf_op jit(solution)/shard_map/all_to_all | solution.py:47
  49.3 4.5 %fusion.15 = f32[9,128,128]{2,0,1:T(8,128)S(1)} fusion(bf16[1,1,128,128,128]{4,3,2,1,0:T(8,128)(2,1)} %param.11, bf16[128,9,128]{2,1,0:T(8,128)(2,1)S(1)} %gather_fusion, f32[128]{0:T(128)S(1)} %compare_convert_fusion, pred[128]{0:T(512)(128)(4,1)S(1)} %get-tuple-element.145), kind=kOutput, calls=%fused_computation.19 | convolution fusion | flops 38043648 | bytes 5079680 | tf_op jit(solution)/shard_map/sut,cst->csu/dot_general | solution.py:68
  54.4 1.0 copy.163
  55.4 3.9 %all-to-all-done.3 = f32[16,9,512]{2,1,0:T(8,128)S(1)} async-done(((f32[16,9,512]{2,1,0:T(8,128)}), f32[16,9,512]{2,1,0:T(8,128)S(1)}, u32[]{:S(2)}, u32[]{:S(2)}) %all-to-all-start.3) | async-done | bytes 294944 | tf_op jit(solution)/shard_map/all_to_all | solution.py:47
  59.3 4.3 %all-to-all-start.1 = ((f32[16,9,512]{2,1,0:T(8,128)}), f32[16,9,512]{2,1,0:T(8,128)S(1)}, u32[]{:S(2)}, u32[]{:S(2)}) async-start(f32[16,9,512]{2,1,0:T(8,128)} %bitcast.328), calls=%async_computation.1 | async-start | bytes 1048576 | tf_op jit(solution)/shard_map/all_to_all | solution.py:47
  63.8 14.0 %all-to-all-done.1 = f32[16,9,512]{2,1,0:T(8,128)S(1)} async-done(((f32[16,9,512]{2,1,0:T(8,128)}), f32[16,9,512]{2,1,0:T(8,128)S(1)}, u32[]{:S(2)}, u32[]{:S(2)}) %all-to-all-start.1) | async-done | bytes 294944 | tf_op jit(solution)/shard_map/all_to_all | solution.py:47
  78.2 1.7 reshape.194
  79.9 9.9 %all-to-all-start.4 = ((f32[256,1,128]{2,1,0:T(1,128)}), f32[256,1,128]{2,1,0:T(1,128)S(1)}, u32[]{:S(2)}, u32[]{:S(2)}) async-start(f32[256,1,128]{2,1,0:T(1,128)} %reshape.194), calls=%async_computation.4 | async-start | bytes 262144 | tf_op jit(solution)/shard_map/all_to_all | solution.py:55
  89.8 12.6 %all-to-all-done.4 = f32[256,1,128]{2,1,0:T(1,128)S(1)} async-done(((f32[256,1,128]{2,1,0:T(1,128)}), f32[256,1,128]{2,1,0:T(1,128)S(1)}, u32[]{:S(2)}, u32[]{:S(2)}) %all-to-all-start.4) | async-done | bytes 131104 | tf_op jit(solution)/shard_map/all_to_all | solution.py:55
  102.9 0.9 reduce.4
  103.9 1.1 reshape.195
  108.9 22.6 %subtract_divide_fusion.14 = (f32[1,8]{1,0:T(1,128)S(1)}, f32[1,8]{1,0:T(1,128)S(1)}, f32[1,8]{1,0:T(1,128)S(1)}, f32[1,8]{1,0:T(1,128)S(1)}, f32[1,8]{1,0:T(1,1...) fusion(f32[]{:T(128)} %bitcast.56, f32[]{:T(128)} %bitcast.55, f32[]{:T(128)} %bitcast.54, ...), kind=kLoop, calls=%fused_computation.212 | loop fusion | flops 512 | bytes 656 | tf_op jit(solution)/shard_map/div | solution.py:19
  132.8 10.6 %all_to_all.75 = bf16[16,8,512]{2,1,0:T(8,128)(2,1)S(1)} all-to-all(bf16[16,8,512]{2,1,0:T(8,128)(2,1)} %broadcast_in_dim.33), channel_id=1, replica_groups=mesh['row'=16,'col'=16] {'row'}, dimensions={0} | all-to-all | bytes 262144 | tf_op jit(solution)/shard_map/all_to_all | solution.py:39
  143.4 3.7 %all-to-all-start.7 = ((bf16[16,8,512]{2,1,0:T(8,128)(2,1)}), bf16[16,8,512]{2,1,0:T(8,128)(2,1)S(1)}, u32[]{:S(2)}, u32[]{:S(2)}) async-start(bf16[16,8,512]{2,1,0:T(8,128)(2,1)} %broadcast_in_dim.33), calls=%async_computation.7 | async-start | bytes 262144 | tf_op jit(solution)/shard_map/all_to_all | solution.py:39
  147.8 8.1 %all-to-all-done.7 = bf16[16,8,512]{2,1,0:T(8,128)(2,1)S(1)} async-done(((bf16[16,8,512]{2,1,0:T(8,128)(2,1)}), bf16[16,8,512]{2,1,0:T(8,128)(2,1)S(1)}, u32[]{:S(2)}, u32[]{:S(2)}) %all-to-all-start.7) | async-done | bytes 131104 | tf_op jit(solution)/shard_map/all_to_all | solution.py:39
  156.6 3.4 fusion.33
  161.3 5.0 %all-to-all-start.8 = ((f32[16,8,512]{2,1,0:T(8,128)}), f32[16,8,512]{2,1,0:T(8,128)S(1)}, u32[]{:S(2)}, u32[]{:S(2)}) async-start(f32[16,8,512]{2,1,0:T(8,128)} %bitcast.331), calls=%async_computation.8 | async-start | bytes 524288 | tf_op jit(solution)/shard_map/all_to_all | solution.py:47
  166.4 4.5 %fusion.27 = f32[8,128,128]{2,0,1:T(8,128)S(1)} fusion(bf16[1,1,128,128,128]{4,3,2,1,0:T(8,128)(2,1)} %param.11, bf16[128,8,128]{2,1,0:T(8,128)(2,1)S(1)} %gather_fusion.2, f32[128]{0:T(128)S(1)} %compare_convert_fusion, pred[128]{0:T(512)(128)(4,1)S(1)} %get-tuple-element.145), kind=kOutput, calls=%fused_computation.23 | convolution fusion | flops 33816576 | bytes 4981376 | tf_op jit(solution)/shard_map/sut,cst->csu/dot_general | solution.py:68
  172.1 1.5 all-to-all-done.8
  173.6 3.5 %all-to-all-start.6 = ((f32[16,8,512]{2,1,0:T(8,128)}), f32[16,8,512]{2,1,0:T(8,128)S(1)}, u32[]{:S(2)}, u32[]{:S(2)}) async-start(f32[16,8,512]{2,1,0:T(8,128)} %bitcast.332), calls=%async_computation.6 | async-start | bytes 524288 | tf_op jit(solution)/shard_map/all_to_all | solution.py:47
  177.6 9.7 %all-to-all-done.6 = f32[16,8,512]{2,1,0:T(8,128)S(1)} async-done(((f32[16,8,512]{2,1,0:T(8,128)}), f32[16,8,512]{2,1,0:T(8,128)S(1)}, u32[]{:S(2)}, u32[]{:S(2)}) %all-to-all-start.6) | async-done | bytes 262176 | tf_op jit(solution)/shard_map/all_to_all | solution.py:47
  187.9 1.7 reshape.196
  189.6 9.3 %all-to-all-start.9 = ((f32[256,1,128]{2,1,0:T(1,128)}), f32[256,1,128]{2,1,0:T(1,128)S(1)}, u32[]{:S(2)}, u32[]{:S(2)}) async-start(f32[256,1,128]{2,1,0:T(1,128)} %reshape.196), calls=%async_computation.9 | async-start | bytes 262144 | tf_op jit(solution)/shard_map/all_to_all | solution.py:55
  198.8 12.6 %all-to-all-done.9 = f32[256,1,128]{2,1,0:T(1,128)S(1)} async-done(((f32[256,1,128]{2,1,0:T(1,128)}), f32[256,1,128]{2,1,0:T(1,128)S(1)}, u32[]{:S(2)}, u32[]{:S(2)}) %all-to-all-start.9) | async-done | bytes 131104 | tf_op jit(solution)/shard_map/all_to_all | solution.py:55
  211.4 0.9 reduce.5
  212.4 1.1 reshape.197
  217.4 22.6 %subtract_divide_fusion.7 = (f32[1,8]{1,0:T(1,128)S(1)}, f32[1,8]{1,0:T(1,128)S(1)}, f32[1,8]{1,0:T(1,128)S(1)}, f32[1,8]{1,0:T(1,128)S(1)}, f32[1,8]{1,0:T(1,12...) fusion(f32[]{:T(128)} %bitcast.110, f32[]{:T(128)} %bitcast.109, f32[]{:T(128)} %bitcast.108, ...), kind=kLoop, calls=%fused_computation.205 | loop fusion | flops 512 | bytes 656 | tf_op jit(solution)/shard_map/div | solution.py:19
  241.4 4.4 %all-to-all-start.10 = ((bf16[16,8,512]{2,1,0:T(8,128)(2,1)}), bf16[16,8,512]{2,1,0:T(8,128)(2,1)S(1)}, u32[]{:S(2)}, u32[]{:S(2)}) async-start(bf16[16,8,512]{2,1,0:T(8,128)(2,1)} %broadcast_in_dim.35), calls=%async_computation.10 | async-start | bytes 262144 | tf_op jit(solution)/shard_map/all_to_all | solution.py:39
  246.0 6.0 %all-to-all-done.10 = bf16[16,8,512]{2,1,0:T(8,128)(2,1)S(1)} async-done(((bf16[16,8,512]{2,1,0:T(8,128)(2,1)}), bf16[16,8,512]{2,1,0:T(8,128)(2,1)S(1)}, u32[]{:S(2)}, u32[]{:S(2)}) %all-to-all-start.10) | async-done | bytes 131104 | tf_op jit(solution)/shard_map/all_to_all | solution.py:39
  251.9 3.5 %all-to-all-start.12 = ((bf16[16,8,512]{2,1,0:T(8,128)(2,1)}), bf16[16,8,512]{2,1,0:T(8,128)(2,1)S(1)}, u32[]{:S(2)}, u32[]{:S(2)}) async-start(bf16[16,8,512]{2,1,0:T(8,128)(2,1)} %broadcast_in_dim.35), calls=%async_computation.12 | async-start | bytes 262144 | tf_op jit(solution)/shard_map/all_to_all | solution.py:39
  256.5 7.9 %all-to-all-done.12 = bf16[16,8,512]{2,1,0:T(8,128)(2,1)S(1)} async-done(((bf16[16,8,512]{2,1,0:T(8,128)(2,1)}), bf16[16,8,512]{2,1,0:T(8,128)(2,1)S(1)}, u32[]{:S(2)}, u32[]{:S(2)}) %all-to-all-start.12) | async-done | bytes 131104 | tf_op jit(solution)/shard_map/all_to_all | solution.py:39
  265.1 3.4 fusion.45
  269.9 5.0 %all-to-all-start.13 = ((f32[16,8,512]{2,1,0:T(8,128)}), f32[16,8,512]{2,1,0:T(8,128)S(1)}, u32[]{:S(2)}, u32[]{:S(2)}) async-start(f32[16,8,512]{2,1,0:T(8,128)} %bitcast.329), calls=%async_computation.13 | async-start | bytes 524288 | tf_op jit(solution)/shard_map/all_to_all | solution.py:47
  274.9 4.5 %fusion.39 = f32[8,128,128]{2,0,1:T(8,128)S(1)} fusion(bf16[1,1,128,128,128]{4,3,2,1,0:T(8,128)(2,1)} %param.11, bf16[128,8,128]{2,1,0:T(8,128)(2,1)S(1)} %gather_fusion.4, f32[128]{0:T(128)S(1)} %compare_convert_fusion, pred[128]{0:T(512)(128)(4,1)S(1)} %get-tuple-element.145), kind=kOutput, calls=%fused_computation.27 | convolution fusion | flops 33816576 | bytes 4981376 | tf_op jit(solution)/shard_map/sut,cst->csu/dot_general | solution.py:68
  280.7 1.5 all-to-all-done.13
  282.1 3.5 %all-to-all-start.11 = ((f32[16,8,512]{2,1,0:T(8,128)}), f32[16,8,512]{2,1,0:T(8,128)S(1)}, u32[]{:S(2)}, u32[]{:S(2)}) async-start(f32[16,8,512]{2,1,0:T(8,128)} %bitcast.330), calls=%async_computation.11 | async-start | bytes 524288 | tf_op jit(solution)/shard_map/all_to_all | solution.py:47
  286.1 9.7 %all-to-all-done.11 = f32[16,8,512]{2,1,0:T(8,128)S(1)} async-done(((f32[16,8,512]{2,1,0:T(8,128)}), f32[16,8,512]{2,1,0:T(8,128)S(1)}, u32[]{:S(2)}, u32[]{:S(2)}) %all-to-all-start.11) | async-done | bytes 262176 | tf_op jit(solution)/shard_map/all_to_all | solution.py:47
  296.4 1.1 reshape.198
  297.5 21.7 %all_to_all.76 = f32[256,1,128]{2,1,0:T(1,128)S(1)} all-to-all(f32[256,1,128]{2,1,0:T(1,128)S(1)} %reshape.198), channel_id=1, replica_groups=mesh['row'=16,'col'=16] {'row','col'}, dimensions={0} | all-to-all | bytes 262144 | tf_op jit(solution)/shard_map/all_to_all | solution.py:55
  319.2 0.9 reduce.6
  320.1 1.1 reshape.199
  325.1 22.6 %subtract_divide_fusion = (f32[1,8]{1,0:T(1,128)S(1)}, f32[1,8]{1,0:T(1,128)S(1)}, f32[1,8]{1,0:T(1,128)S(1)}, f32[1,8]{1,0:T(1,128)S(1)}, f32[1,8]{1,0:T(1,128)...) fusion(f32[]{:T(128)} %bitcast.164, f32[]{:T(128)} %bitcast.163, f32[]{:T(128)} %bitcast.162, ...), kind=kLoop, calls=%fused_computation.198 | loop fusion | flops 512 | bytes 656 | tf_op jit(solution)/shard_map/div | solution.py:19
  (124 shorter events, 34.9 us)
Async XLA Ops:
  2.8 14.0 %all-to-all-start = ((bf16[16,9,512]{2,1,0:T(8,128)(2,1)}), bf16[16,9,512]{2,1,0:T(8,128)(2,1)S(1)}, u32[]{:S(2)}, u32[]{:S(2)}) async-start(bf16[16,9,512]{2,1,0:T(8,128)(2,1)} %broadcast_in_dim.30), calls=%async_computation | async-start | bytes 524288 | tf_op jit(solution)/shard_map/all_to_all | solution.py:39
  16.8 20.0 %all-to-all-start.2 = ((bf16[16,9,512]{2,1,0:T(8,128)(2,1)}), bf16[16,9,512]{2,1,0:T(8,128)(2,1)S(1)}, u32[]{:S(2)}, u32[]{:S(2)}) async-start(bf16[16,9,512]{2,1,0:T(8,128)(2,1)} %broadcast_in_dim.30), calls=%async_computation.2 | async-start | bytes 524288 | tf_op jit(solution)/shard_map/all_to_all | solution.py:39
  42.9 16.4 %all-to-all-start.3 = ((f32[16,9,512]{2,1,0:T(8,128)}), f32[16,9,512]{2,1,0:T(8,128)S(1)}, u32[]{:S(2)}, u32[]{:S(2)}) async-start(f32[16,9,512]{2,1,0:T(8,128)} %bitcast.327), calls=%async_computation.3 | async-start | bytes 1048576 | tf_op jit(solution)/shard_map/all_to_all | solution.py:47
  49.3 14.3 %copy-start = (f32[8,512]{1,0:T(8,128)S(1)}, f32[8,512]{1,0:T(8,128)}, u32[]{:S(2)}) copy-start(f32[8,512]{1,0:T(8,128)} %param.15) | copy-start | bytes 49156
  59.3 18.5 %all-to-all-start.1 = ((f32[16,9,512]{2,1,0:T(8,128)}), f32[16,9,512]{2,1,0:T(8,128)S(1)}, u32[]{:S(2)}, u32[]{:S(2)}) async-start(f32[16,9,512]{2,1,0:T(8,128)} %bitcast.328), calls=%async_computation.1 | async-start | bytes 1048576 | tf_op jit(solution)/shard_map/all_to_all | solution.py:47
  79.9 22.5 %all-to-all-start.4 = ((f32[256,1,128]{2,1,0:T(1,128)}), f32[256,1,128]{2,1,0:T(1,128)S(1)}, u32[]{:S(2)}, u32[]{:S(2)}) async-start(f32[256,1,128]{2,1,0:T(1,128)} %reshape.194), calls=%async_computation.4 | async-start | bytes 262144 | tf_op jit(solution)/shard_map/all_to_all | solution.py:55
  143.4 12.5 %all-to-all-start.7 = ((bf16[16,8,512]{2,1,0:T(8,128)(2,1)}), bf16[16,8,512]{2,1,0:T(8,128)(2,1)S(1)}, u32[]{:S(2)}, u32[]{:S(2)}) async-start(bf16[16,8,512]{2,1,0:T(8,128)(2,1)} %broadcast_in_dim.33), calls=%async_computation.7 | async-start | bytes 262144 | tf_op jit(solution)/shard_map/all_to_all | solution.py:39
  160.5 16.8 %copy-start.1 = (f32[2,8,24]{2,1,0:T(8,128)S(1)}, f32[2,8,24]{2,1,0:T(8,128)}, u32[]{:S(2)}) copy-start(f32[2,8,24]{2,1,0:T(8,128)} %param.16) | copy-start | bytes 4612
  161.3 12.3 %all-to-all-start.8 = ((f32[16,8,512]{2,1,0:T(8,128)}), f32[16,8,512]{2,1,0:T(8,128)S(1)}, u32[]{:S(2)}, u32[]{:S(2)}) async-start(f32[16,8,512]{2,1,0:T(8,128)} %bitcast.331), calls=%async_computation.8 | async-start | bytes 524288 | tf_op jit(solution)/shard_map/all_to_all | solution.py:47
  173.6 13.8 %all-to-all-start.6 = ((f32[16,8,512]{2,1,0:T(8,128)}), f32[16,8,512]{2,1,0:T(8,128)S(1)}, u32[]{:S(2)}, u32[]{:S(2)}) async-start(f32[16,8,512]{2,1,0:T(8,128)} %bitcast.332), calls=%async_computation.6 | async-start | bytes 524288 | tf_op jit(solution)/shard_map/all_to_all | solution.py:47
  189.6 21.9 %all-to-all-start.9 = ((f32[256,1,128]{2,1,0:T(1,128)}), f32[256,1,128]{2,1,0:T(1,128)S(1)}, u32[]{:S(2)}, u32[]{:S(2)}) async-start(f32[256,1,128]{2,1,0:T(1,128)} %reshape.196), calls=%async_computation.9 | async-start | bytes 262144 | tf_op jit(solution)/shard_map/all_to_all | solution.py:55
  241.4 10.6 %all-to-all-start.10 = ((bf16[16,8,512]{2,1,0:T(8,128)(2,1)}), bf16[16,8,512]{2,1,0:T(8,128)(2,1)S(1)}, u32[]{:S(2)}, u32[]{:S(2)}) async-start(bf16[16,8,512]{2,1,0:T(8,128)(2,1)} %broadcast_in_dim.35), calls=%async_computation.10 | async-start | bytes 262144 | tf_op jit(solution)/shard_map/all_to_all | solution.py:39
  251.9 12.5 %all-to-all-start.12 = ((bf16[16,8,512]{2,1,0:T(8,128)(2,1)}), bf16[16,8,512]{2,1,0:T(8,128)(2,1)S(1)}, u32[]{:S(2)}, u32[]{:S(2)}) async-start(bf16[16,8,512]{2,1,0:T(8,128)(2,1)} %broadcast_in_dim.35), calls=%async_computation.12 | async-start | bytes 262144 | tf_op jit(solution)/shard_map/all_to_all | solution.py:39
  269.9 12.3 %all-to-all-start.13 = ((f32[16,8,512]{2,1,0:T(8,128)}), f32[16,8,512]{2,1,0:T(8,128)S(1)}, u32[]{:S(2)}, u32[]{:S(2)}) async-start(f32[16,8,512]{2,1,0:T(8,128)} %bitcast.329), calls=%async_computation.13 | async-start | bytes 524288 | tf_op jit(solution)/shard_map/all_to_all | solution.py:47
  282.1 13.8 %all-to-all-start.11 = ((f32[16,8,512]{2,1,0:T(8,128)}), f32[16,8,512]{2,1,0:T(8,128)S(1)}, u32[]{:S(2)}, u32[]{:S(2)}) async-start(f32[16,8,512]{2,1,0:T(8,128)} %bitcast.330), calls=%async_computation.11 | async-start | bytes 524288 | tf_op jit(solution)/shard_map/all_to_all | solution.py:47

commit v2 on v1

--- a/solution.py
+++ b/solution.py
@@ -10,14 +10,14 @@
 
 def lower_inverse(lower_factor):
     order_size = lower_factor.shape[0]
+    assert order_size <= 8
     identity = jnp.eye(order_size, dtype=lower_factor.dtype)
-    inverse_rows = []
-    for row_at in range(order_size):
-        partial_row = identity[row_at]
-        for prior_at in range(row_at):
-            partial_row = partial_row - lower_factor[row_at, prior_at] * inverse_rows[prior_at]
-        inverse_rows.append(partial_row / lower_factor[row_at, row_at])
-    return jnp.stack(inverse_rows)
+    diagonal = jnp.diagonal(lower_factor)
+    strict = lower_factor / diagonal[:, None] - identity
+    square = matmul_high(strict, strict)
+    fourth = matmul_high(square, square)
+    inverse = matmul_high(matmul_high(identity - strict, identity + square), identity + fourth)
+    return inverse / diagonal[None, :]
 
 
 def settle(new_vecs, new_images, new_steps, step_images, gram_x, gram_ax, node_total):

time: 352 us -> 283 us (0.80)
  other arithmetic: 80.8 us -> 13.1 us
    div x3 -> x0, other arithmetic: 67.7 us -> none  [lower_inverse(): inverse_rows.append(partial_row / lower_factor[row_at, row_at])]
    slice x6 -> x0, local copies, waits for them, and re-layouts: 4.28 us -> none  [the longest x3 2.15 us: lower_inverse(): lower_factor[row_at, prior_at] * inverse_rows[prior_at]]
    dot_general x28 -> x40, matrix products: 5.22 us -> 7.33 us  [matmul_high(): return jnp.dot(left, right, precision=lax.Precision.HIGHEST)]
  transfers between devices with their start and end apart: 13 -> 13, of which waited for: 13 -> 13; matrix products, arithmetic and copies ran while one was open for 7% -> 9% of each run, Pallas kernels for 0% -> 0%
where the time goes in v2:
time: 283 us; the launch traced here: 281 us
  waiting for transfers between devices  100 us (35%)
  starting transfers between devices  76.1 us (27%)
  matrix products  33.7 us (12%)
  blocking collectives  32.3 us (11%)
  local copies, waits for them, and re-layouts  24.2 us (9%)
  other arithmetic  13.1 us (5%)
    all_to_all x6, waiting for transfers between devices, scatter_sum_by_exchange(): held = lax.all_to_all(chunks, axis, 0, 0, tiled=True)  40.3 us
    all_to_all x5, waiting for transfers between devices, gather_by_exchange(): held = lax.all_to_all(copies, axis, 0, 0, tiled=True)  34.6 us
    all_to_all x5, starting transfers between devices, gather_by_exchange(): held = lax.all_to_all(copies, axis, 0, 0, tiled=True)  29.1 us
    all_to_all x6, starting transfers between devices, scatter_sum_by_exchange(): held = lax.all_to_all(chunks, axis, 0, 0, tiled=True)  27.8 us
    all_to_all x2, waiting for transfers between devices, gram_sums(): held = lax.all_to_all(copies, ('row', 'col'), 0, 0, tiled=True)  25.2 us
    all_to_all x1, blocking collectives, gram_sums(): held = lax.all_to_all(copies, ('row', 'col'), 0, 0, tiled=True)  21.7 us
    all_to_all x2, starting transfers between devices, gram_sums(): held = lax.all_to_all(copies, ('row', 'col'), 0, 0, tiled=True)  19.2 us
    dot_general x3, matrix products, local_terms(): jnp.einsum('sut,cst->csu', part_tiles, col_values, preferred_element_type...  13.5 us
  transfers between devices with their start and end apart: 13, of which 13 were waited for; matrix products, arithmetic and copies ran while one was open for 9% of the time, Pallas kernels for 0%

profile of v2, /device:TPU:1, one launch (start us, length us, event | category | flops | bytes accessed | tf_op | source)
XLA Modules:
  0.0 281.2 jit_solution(6054675216702237571)
XLA Ops:
  2.8 6.8 %all-to-all-start = ((bf16[16,9,512]{2,1,0:T(8,128)(2,1)}), bf16[16,9,512]{2,1,0:T(8,128)(2,1)S(1)}, u32[]{:S(2)}, u32[]{:S(2)}) async-start(bf16[16,9,512]{2,1,0:T(8,128)(2,1)} %broadcast_in_dim.38), calls=%async_computation | async-start | bytes 524288 | tf_op jit(solution)/shard_map/all_to_all | solution.py:39
  11.8 5.0 %all-to-all-done = bf16[16,9,512]{2,1,0:T(8,128)(2,1)S(1)} async-done(((bf16[16,9,512]{2,1,0:T(8,128)(2,1)}), bf16[16,9,512]{2,1,0:T(8,128)(2,1)S(1)}, u32[]{:S(2)}, u32[]{:S(2)}) %all-to-all-start) | async-done | bytes 147488 | tf_op jit(solution)/shard_map/all_to_all | solution.py:39
  16.8 10.6 %all-to-all-start.2 = ((bf16[16,9,512]{2,1,0:T(8,128)(2,1)}), bf16[16,9,512]{2,1,0:T(8,128)(2,1)S(1)}, u32[]{:S(2)}, u32[]{:S(2)}) async-start(bf16[16,9,512]{2,1,0:T(8,128)(2,1)} %broadcast_in_dim.38), calls=%async_computation.2 | async-start | bytes 524288 | tf_op jit(solution)/shard_map/all_to_all | solution.py:39
  29.2 7.6 %all-to-all-done.2 = bf16[16,9,512]{2,1,0:T(8,128)(2,1)S(1)} async-done(((bf16[16,9,512]{2,1,0:T(8,128)(2,1)}), bf16[16,9,512]{2,1,0:T(8,128)(2,1)S(1)}, u32[]{:S(2)}, u32[]{:S(2)}) %all-to-all-start.2) | async-done | bytes 147488 | tf_op jit(solution)/shard_map/all_to_all | solution.py:39
  37.9 3.4 %fusion.21 = f32[9,128,128]{2,0,1:T(8,128)S(1)} fusion(bf16[1,1,128,128,128]{4,3,2,1,0:T(8,128)(2,1)} %param.11, bf16[128,9,128]{2,1,0:T(8,128)(2,1)S(1)} %gather_fusion.4, f32[128]{0:T(128)S(1)} %compare_select_fusion.1, pred[128]{0:T(512)(128)(4,1)S(1)} %get-tuple-element.4), kind=kOutput, calls=%fused_computation.24 | convolution fusion | flops 38043648 | bytes 5079680 | tf_op jit(solution)/shard_map/sut,csu->cst/dot_general | solution.py:72
  41.9 1.0 copy.162
  42.9 6.4 %all-to-all-start.3 = ((f32[16,9,512]{2,1,0:T(8,128)}), f32[16,9,512]{2,1,0:T(8,128)S(1)}, u32[]{:S(2)}, u32[]{:S(2)}) async-start(f32[16,9,512]{2,1,0:T(8,128)} %bitcast.233), calls=%async_computation.3 | async-start | bytes 1048576 | tf_op jit(solution)/shard_map/all_to_all | solution.py:47
  49.3 4.5 %fusion.15 = f32[9,128,128]{2,0,1:T(8,128)S(1)} fusion(bf16[1,1,128,128,128]{4,3,2,1,0:T(8,128)(2,1)} %param.11, bf16[128,9,128]{2,1,0:T(8,128)(2,1)S(1)} %gather_fusion.3, f32[128]{0:T(128)S(1)} %compare_convert_fusion, pred[128]{0:T(512)(128)(4,1)S(1)} %get-tuple-element.13), kind=kOutput, calls=%fused_computation.22 | convolution fusion | flops 38043648 | bytes 5079680 | tf_op jit(solution)/shard_map/sut,cst->csu/dot_general | solution.py:68
  54.4 1.0 copy.163
  55.4 3.9 %all-to-all-done.3 = f32[16,9,512]{2,1,0:T(8,128)S(1)} async-done(((f32[16,9,512]{2,1,0:T(8,128)}), f32[16,9,512]{2,1,0:T(8,128)S(1)}, u32[]{:S(2)}, u32[]{:S(2)}) %all-to-all-start.3) | async-done | bytes 294944 | tf_op jit(solution)/shard_map/all_to_all | solution.py:47
  59.3 4.3 %all-to-all-start.1 = ((f32[16,9,512]{2,1,0:T(8,128)}), f32[16,9,512]{2,1,0:T(8,128)S(1)}, u32[]{:S(2)}, u32[]{:S(2)}) async-start(f32[16,9,512]{2,1,0:T(8,128)} %bitcast.234), calls=%async_computation.1 | async-start | bytes 1048576 | tf_op jit(solution)/shard_map/all_to_all | solution.py:47
  63.8 14.0 %all-to-all-done.1 = f32[16,9,512]{2,1,0:T(8,128)S(1)} async-done(((f32[16,9,512]{2,1,0:T(8,128)}), f32[16,9,512]{2,1,0:T(8,128)S(1)}, u32[]{:S(2)}, u32[]{:S(2)}) %all-to-all-start.1) | async-done | bytes 294944 | tf_op jit(solution)/shard_map/all_to_all | solution.py:47
  78.2 1.7 reshape.218
  79.9 9.9 %all-to-all-start.4 = ((f32[256,1,128]{2,1,0:T(1,128)}), f32[256,1,128]{2,1,0:T(1,128)S(1)}, u32[]{:S(2)}, u32[]{:S(2)}) async-start(f32[256,1,128]{2,1,0:T(1,128)} %reshape.218), calls=%async_computation.4 | async-start | bytes 262144 | tf_op jit(solution)/shard_map/all_to_all | solution.py:55
  89.8 12.6 %all-to-all-done.4 = f32[256,1,128]{2,1,0:T(1,128)S(1)} async-done(((f32[256,1,128]{2,1,0:T(1,128)}), f32[256,1,128]{2,1,0:T(1,128)S(1)}, u32[]{:S(2)}, u32[]{:S(2)}) %all-to-all-start.4) | async-done | bytes 131104 | tf_op jit(solution)/shard_map/all_to_all | solution.py:55
  102.9 0.9 reduce.4
  103.9 1.1 reshape.219
  110.1 10.6 %all_to_all.75 = bf16[16,8,512]{2,1,0:T(8,128)(2,1)S(1)} all-to-all(bf16[16,8,512]{2,1,0:T(8,128)(2,1)} %broadcast_in_dim.41), channel_id=1, replica_groups=mesh['row'=16,'col'=16] {'row'}, dimensions={0} | all-to-all | bytes 262144 | tf_op jit(solution)/shard_map/all_to_all | solution.py:39
  120.7 3.7 %all-to-all-start.7 = ((bf16[16,8,512]{2,1,0:T(8,128)(2,1)}), bf16[16,8,512]{2,1,0:T(8,128)(2,1)S(1)}, u32[]{:S(2)}, u32[]{:S(2)}) async-start(bf16[16,8,512]{2,1,0:T(8,128)(2,1)} %broadcast_in_dim.41), calls=%async_computation.7 | async-start | bytes 262144 | tf_op jit(solution)/shard_map/all_to_all | solution.py:39
  125.1 8.1 %all-to-all-done.7 = bf16[16,8,512]{2,1,0:T(8,128)(2,1)S(1)} async-done(((bf16[16,8,512]{2,1,0:T(8,128)(2,1)}), bf16[16,8,512]{2,1,0:T(8,128)(2,1)S(1)}, u32[]{:S(2)}, u32[]{:S(2)}) %all-to-all-start.7) | async-done | bytes 131104 | tf_op jit(solution)/shard_map/all_to_all | solution.py:39
  133.9 3.4 %fusion.33 = f32[8,128,128]{2,0,1:T(8,128)S(1)} fusion(bf16[1,1,128,128,128]{4,3,2,1,0:T(8,128)(2,1)} %param.11, bf16[128,8,128]{2,1,0:T(8,128)(2,1)S(1)} %gather_fusion.6, f32[128]{0:T(128)S(1)} %compare_select_fusion.1, pred[128]{0:T(512)(128)(4,1)S(1)} %get-tuple-element.4), kind=kOutput, calls=%fused_computation.28 | convolution fusion | flops 33816576 | bytes 4981376 | tf_op jit(solution)/shard_map/sut,csu->cst/dot_general | solution.py:72
  137.8 0.9 copy.166
  138.6 5.0 %all-to-all-start.8 = ((f32[16,8,512]{2,1,0:T(8,128)}), f32[16,8,512]{2,1,0:T(8,128)S(1)}, u32[]{:S(2)}, u32[]{:S(2)}) async-start(f32[16,8,512]{2,1,0:T(8,128)} %bitcast.237), calls=%async_computation.8 | async-start | bytes 524288 | tf_op jit(solution)/shard_map/all_to_all | solution.py:47
  143.7 4.5 %fusion.27 = f32[8,128,128]{2,0,1:T(8,128)S(1)} fusion(bf16[1,1,128,128,128]{4,3,2,1,0:T(8,128)(2,1)} %param.11, bf16[128,8,128]{2,1,0:T(8,128)(2,1)S(1)} %gather_fusion.5, f32[128]{0:T(128)S(1)} %compare_convert_fusion, pred[128]{0:T(512)(128)(4,1)S(1)} %get-tuple-element.13), kind=kOutput, calls=%fused_computation.26 | convolution fusion | flops 33816576 | bytes 4981376 | tf_op jit(solution)/shard_map/sut,cst->csu/dot_general | solution.py:68
  148.6 0.8 copy.167
  149.4 1.5 all-to-all-done.8
  150.9 3.5 %all-to-all-start.6 = ((f32[16,8,512]{2,1,0:T(8,128)}), f32[16,8,512]{2,1,0:T(8,128)S(1)}, u32[]{:S(2)}, u32[]{:S(2)}) async-start(f32[16,8,512]{2,1,0:T(8,128)} %bitcast.238), calls=%async_computation.6 | async-start | bytes 524288 | tf_op jit(solution)/shard_map/all_to_all | solution.py:47
  154.9 9.7 %all-to-all-done.6 = f32[16,8,512]{2,1,0:T(8,128)S(1)} async-done(((f32[16,8,512]{2,1,0:T(8,128)}), f32[16,8,512]{2,1,0:T(8,128)S(1)}, u32[]{:S(2)}, u32[]{:S(2)}) %all-to-all-start.6) | async-done | bytes 262176 | tf_op jit(solution)/shard_map/all_to_all | solution.py:47
  165.2 1.7 reshape.220
  166.9 9.3 %all-to-all-start.9 = ((f32[256,1,128]{2,1,0:T(1,128)}), f32[256,1,128]{2,1,0:T(1,128)S(1)}, u32[]{:S(2)}, u32[]{:S(2)}) async-start(f32[256,1,128]{2,1,0:T(1,128)} %reshape.220), calls=%async_computation.9 | async-start | bytes 262144 | tf_op jit(solution)/shard_map/all_to_all | solution.py:55
  176.1 12.6 %all-to-all-done.9 = f32[256,1,128]{2,1,0:T(1,128)S(1)} async-done(((f32[256,1,128]{2,1,0:T(1,128)}), f32[256,1,128]{2,1,0:T(1,128)S(1)}, u32[]{:S(2)}, u32[]{:S(2)}) %all-to-all-start.9) | async-done | bytes 131104 | tf_op jit(solution)/shard_map/all_to_all | solution.py:55
  188.7 0.9 reduce.5
  189.7 1.1 reshape.221
  196.0 4.4 %all-to-all-start.10 = ((bf16[16,8,512]{2,1,0:T(8,128)(2,1)}), bf16[16,8,512]{2,1,0:T(8,128)(2,1)S(1)}, u32[]{:S(2)}, u32[]{:S(2)}) async-start(bf16[16,8,512]{2,1,0:T(8,128)(2,1)} %broadcast_in_dim.43), calls=%async_computation.10 | async-start | bytes 262144 | tf_op jit(solution)/shard_map/all_to_all | solution.py:39
  200.6 6.0 %all-to-all-done.10 = bf16[16,8,512]{2,1,0:T(8,128)(2,1)S(1)} async-done(((bf16[16,8,512]{2,1,0:T(8,128)(2,1)}), bf16[16,8,512]{2,1,0:T(8,128)(2,1)S(1)}, u32[]{:S(2)}, u32[]{:S(2)}) %all-to-all-start.10) | async-done | bytes 131104 | tf_op jit(solution)/shard_map/all_to_all | solution.py:39
  206.5 3.5 %all-to-all-start.12 = ((bf16[16,8,512]{2,1,0:T(8,128)(2,1)}), bf16[16,8,512]{2,1,0:T(8,128)(2,1)S(1)}, u32[]{:S(2)}, u32[]{:S(2)}) async-start(bf16[16,8,512]{2,1,0:T(8,128)(2,1)} %broadcast_in_dim.43), calls=%async_computation.12 | async-start | bytes 262144 | tf_op jit(solution)/shard_map/all_to_all | solution.py:39
  211.1 7.9 %all-to-all-done.12 = bf16[16,8,512]{2,1,0:T(8,128)(2,1)S(1)} async-done(((bf16[16,8,512]{2,1,0:T(8,128)(2,1)}), bf16[16,8,512]{2,1,0:T(8,128)(2,1)S(1)}, u32[]{:S(2)}, u32[]{:S(2)}) %all-to-all-start.12) | async-done | bytes 131104 | tf_op jit(solution)/shard_map/all_to_all | solution.py:39
  219.7 3.4 %fusion.45 = f32[8,128,128]{2,0,1:T(8,128)S(1)} fusion(bf16[1,1,128,128,128]{4,3,2,1,0:T(8,128)(2,1)} %param.11, bf16[128,8,128]{2,1,0:T(8,128)(2,1)S(1)} %gather_fusion.8, f32[128]{0:T(128)S(1)} %compare_select_fusion.1, pred[128]{0:T(512)(128)(4,1)S(1)} %get-tuple-element.4), kind=kOutput, calls=%fused_computation.32 | convolution fusion | flops 33816576 | bytes 4981376 | tf_op jit(solution)/shard_map/sut,csu->cst/dot_general | solution.py:72
  223.6 0.9 copy.164
  224.5 5.0 %all-to-all-start.13 = ((f32[16,8,512]{2,1,0:T(8,128)}), f32[16,8,512]{2,1,0:T(8,128)S(1)}, u32[]{:S(2)}, u32[]{:S(2)}) async-start(f32[16,8,512]{2,1,0:T(8,128)} %bitcast.235), calls=%async_computation.13 | async-start | bytes 524288 | tf_op jit(solution)/shard_map/all_to_all | solution.py:47
  229.5 4.5 %fusion.39 = f32[8,128,128]{2,0,1:T(8,128)S(1)} fusion(bf16[1,1,128,128,128]{4,3,2,1,0:T(8,128)(2,1)} %param.11, bf16[128,8,128]{2,1,0:T(8,128)(2,1)S(1)} %gather_fusion.7, f32[128]{0:T(128)S(1)} %compare_convert_fusion, pred[128]{0:T(512)(128)(4,1)S(1)} %get-tuple-element.13), kind=kOutput, calls=%fused_computation.30 | convolution fusion | flops 33816576 | bytes 4981376 | tf_op jit(solution)/shard_map/sut,cst->csu/dot_general | solution.py:68
  235.3 1.5 all-to-all-done.13
  236.7 3.5 %all-to-all-start.11 = ((f32[16,8,512]{2,1,0:T(8,128)}), f32[16,8,512]{2,1,0:T(8,128)S(1)}, u32[]{:S(2)}, u32[]{:S(2)}) async-start(f32[16,8,512]{2,1,0:T(8,128)} %bitcast.236), calls=%async_computation.11 | async-start | bytes 524288 | tf_op jit(solution)/shard_map/all_to_all | solution.py:47
  240.7 9.7 %all-to-all-done.11 = f32[16,8,512]{2,1,0:T(8,128)S(1)} async-done(((f32[16,8,512]{2,1,0:T(8,128)}), f32[16,8,512]{2,1,0:T(8,128)S(1)}, u32[]{:S(2)}, u32[]{:S(2)}) %all-to-all-start.11) | async-done | bytes 262176 | tf_op jit(solution)/shard_map/all_to_all | solution.py:47
  251.0 1.1 reshape.222
  252.1 21.7 %all_to_all.76 = f32[256,1,128]{2,1,0:T(1,128)S(1)} all-to-all(f32[256,1,128]{2,1,0:T(1,128)S(1)} %reshape.222), channel_id=1, replica_groups=mesh['row'=16,'col'=16] {'row','col'}, dimensions={0} | all-to-all | bytes 262144 | tf_op jit(solution)/shard_map/all_to_all | solution.py:55
  273.8 0.9 reduce.6
  274.7 1.1 reshape.223
  (127 shorter events, 32.0 us)
Async XLA Ops:
  2.8 14.0 %all-to-all-start = ((bf16[16,9,512]{2,1,0:T(8,128)(2,1)}), bf16[16,9,512]{2,1,0:T(8,128)(2,1)S(1)}, u32[]{:S(2)}, u32[]{:S(2)}) async-start(bf16[16,9,512]{2,1,0:T(8,128)(2,1)} %broadcast_in_dim.38), calls=%async_computation | async-start | bytes 524288 | tf_op jit(solution)/shard_map/all_to_all | solution.py:39
  16.8 20.0 %all-to-all-start.2 = ((bf16[16,9,512]{2,1,0:T(8,128)(2,1)}), bf16[16,9,512]{2,1,0:T(8,128)(2,1)S(1)}, u32[]{:S(2)}, u32[]{:S(2)}) async-start(bf16[16,9,512]{2,1,0:T(8,128)(2,1)} %broadcast_in_dim.38), calls=%async_computation.2 | async-start | bytes 524288 | tf_op jit(solution)/shard_map/all_to_all | solution.py:39
  42.9 16.4 %all-to-all-start.3 = ((f32[16,9,512]{2,1,0:T(8,128)}), f32[16,9,512]{2,1,0:T(8,128)S(1)}, u32[]{:S(2)}, u32[]{:S(2)}) async-start(f32[16,9,512]{2,1,0:T(8,128)} %bitcast.233), calls=%async_computation.3 | async-start | bytes 1048576 | tf_op jit(solution)/shard_map/all_to_all | solution.py:47
  49.3 14.3 %copy-start = (f32[8,512]{1,0:T(8,128)S(1)}, f32[8,512]{1,0:T(8,128)}, u32[]{:S(2)}) copy-start(f32[8,512]{1,0:T(8,128)} %param.15) | copy-start | bytes 49156
  59.3 18.5 %all-to-all-start.1 = ((f32[16,9,512]{2,1,0:T(8,128)}), f32[16,9,512]{2,1,0:T(8,128)S(1)}, u32[]{:S(2)}, u32[]{:S(2)}) async-start(f32[16,9,512]{2,1,0:T(8,128)} %bitcast.234), calls=%async_computation.1 | async-start | bytes 1048576 | tf_op jit(solution)/shard_map/all_to_all | solution.py:47
  79.9 22.5 %all-to-all-start.4 = ((f32[256,1,128]{2,1,0:T(1,128)}), f32[256,1,128]{2,1,0:T(1,128)S(1)}, u32[]{:S(2)}, u32[]{:S(2)}) async-start(f32[256,1,128]{2,1,0:T(1,128)} %reshape.218), calls=%async_computation.4 | async-start | bytes 262144 | tf_op jit(solution)/shard_map/all_to_all | solution.py:55
  120.7 12.5 %all-to-all-start.7 = ((bf16[16,8,512]{2,1,0:T(8,128)(2,1)}), bf16[16,8,512]{2,1,0:T(8,128)(2,1)S(1)}, u32[]{:S(2)}, u32[]{:S(2)}) async-start(bf16[16,8,512]{2,1,0:T(8,128)(2,1)} %broadcast_in_dim.41), calls=%async_computation.7 | async-start | bytes 262144 | tf_op jit(solution)/shard_map/all_to_all | solution.py:39
  137.8 16.8 %copy-start.1 = (f32[2,8,24]{2,1,0:T(8,128)S(1)}, f32[2,8,24]{2,1,0:T(8,128)}, u32[]{:S(2)}) copy-start(f32[2,8,24]{2,1,0:T(8,128)} %param.16) | copy-start | bytes 4612
  138.6 12.3 %all-to-all-start.8 = ((f32[16,8,512]{2,1,0:T(8,128)}), f32[16,8,512]{2,1,0:T(8,128)S(1)}, u32[]{:S(2)}, u32[]{:S(2)}) async-start(f32[16,8,512]{2,1,0:T(8,128)} %bitcast.237), calls=%async_computation.8 | async-start | bytes 524288 | tf_op jit(solution)/shard_map/all_to_all | solution.py:47
  150.9 13.8 %all-to-all-start.6 = ((f32[16,8,512]{2,1,0:T(8,128)}), f32[16,8,512]{2,1,0:T(8,128)S(1)}, u32[]{:S(2)}, u32[]{:S(2)}) async-start(f32[16,8,512]{2,1,0:T(8,128)} %bitcast.238), calls=%async_computation.6 | async-start | bytes 524288 | tf_op jit(solution)/shard_map/all_to_all | solution.py:47
  166.9 21.9 %all-to-all-start.9 = ((f32[256,1,128]{2,1,0:T(1,128)}), f32[256,1,128]{2,1,0:T(1,128)S(1)}, u32[]{:S(2)}, u32[]{:S(2)}) async-start(f32[256,1,128]{2,1,0:T(1,128)} %reshape.220), calls=%async_computation.9 | async-start | bytes 262144 | tf_op jit(solution)/shard_map/all_to_all | solution.py:55
  196.0 10.6 %all-to-all-start.10 = ((bf16[16,8,512]{2,1,0:T(8,128)(2,1)}), bf16[16,8,512]{2,1,0:T(8,128)(2,1)S(1)}, u32[]{:S(2)}, u32[]{:S(2)}) async-start(bf16[16,8,512]{2,1,0:T(8,128)(2,1)} %broadcast_in_dim.43), calls=%async_computation.10 | async-start | bytes 262144 | tf_op jit(solution)/shard_map/all_to_all | solution.py:39
  206.5 12.5 %all-to-all-start.12 = ((bf16[16,8,512]{2,1,0:T(8,128)(2,1)}), bf16[16,8,512]{2,1,0:T(8,128)(2,1)S(1)}, u32[]{:S(2)}, u32[]{:S(2)}) async-start(bf16[16,8,512]{2,1,0:T(8,128)(2,1)} %broadcast_in_dim.43), calls=%async_computation.12 | async-start | bytes 262144 | tf_op jit(solution)/shard_map/all_to_all | solution.py:39
  224.5 12.3 %all-to-all-start.13 = ((f32[16,8,512]{2,1,0:T(8,128)}), f32[16,8,512]{2,1,0:T(8,128)S(1)}, u32[]{:S(2)}, u32[]{:S(2)}) async-start(f32[16,8,512]{2,1,0:T(8,128)} %bitcast.235), calls=%async_computation.13 | async-start | bytes 524288 | tf_op jit(solution)/shard_map/all_to_all | solution.py:47
  236.7 13.8 %all-to-all-start.11 = ((f32[16,8,512]{2,1,0:T(8,128)}), f32[16,8,512]{2,1,0:T(8,128)S(1)}, u32[]{:S(2)}, u32[]{:S(2)}) async-start(f32[16,8,512]{2,1,0:T(8,128)} %bitcast.236), calls=%async_computation.11 | async-start | bytes 524288 | tf_op jit(solution)/shard_map/all_to_all | solution.py:47

commit v3 on v2

--- a/solution.py
+++ b/solution.py
@@ -40,25 +40,33 @@
     return jnp.swapaxes(held, 0, 1).reshape(local.shape[0], count * local.shape[1])
 
 
-def scatter_sum_by_exchange(total, axis):
-    count = lax.axis_size(axis)
-    width, length = total.shape
-    chunks = jnp.swapaxes(total.reshape(width, count, length // count), 0, 1)
+def scatter_sum_by_exchange(chunks, axis):
     held = lax.all_to_all(chunks, axis, 0, 0, tiled=True)
     return jnp.sum(held, axis=0)
 
 
 def gram_sums(new_vecs, new_images):
-    local = jnp.stack([matmul_high(new_vecs, new_vecs.T), matmul_high(new_images, new_vecs.T)])
+    order = new_vecs.shape[0]
+    local = jnp.concatenate(
+        [matmul_high(new_vecs, new_vecs.T).reshape(-1), matmul_high(new_images, new_vecs.T).reshape(-1)]
+    )
     count = lax.axis_size("row") * lax.axis_size("col")
     copies = jnp.broadcast_to(local[None], (count,) + local.shape)
     held = lax.all_to_all(copies, ("row", "col"), 0, 0, tiled=True)
     total = jnp.sum(held, axis=0)
-    return total[0], total[1]
+    return total[: order * order].reshape(order, order), total[order * order :].reshape(order, order)
 
 
 def local_terms(
-    part_tiles, part_rows, part_cols, weight_direct, weight_mirror, col_blocks, row_blocks
+    part_tiles,
+    part_rows,
+    part_cols,
+    weight_direct,
+    weight_mirror,
+    col_blocks,
+    row_blocks,
+    row_owners,
+    col_owners,
 ):
     row_span = row_blocks.shape[1]
     col_span = col_blocks.shape[1]
@@ -78,9 +86,24 @@
     pick_cols = (part_cols[:, None] == jnp.arange(col_span, dtype=jnp.int32)[None, :]).astype(
         jnp.float32
     )
-    rows_sum = jnp.einsum("sp,csu->cpu", pick_rows, direct, precision=lax.Precision.HIGHEST)
-    cols_sum = jnp.einsum("sq,cst->cqt", pick_cols, mirror, precision=lax.Precision.HIGHEST)
-    return (rows_sum, cols_sum)
+    slots = pick_rows.shape[0]
+    rows_sum = jnp.einsum(
+        "sjb,csu->jcbu",
+        pick_rows.reshape(slots, row_owners, row_span // row_owners),
+        direct,
+        precision=lax.Precision.HIGHEST,
+    )
+    cols_sum = jnp.einsum(
+        "sjb,cst->jcbt",
+        pick_cols.reshape(slots, col_owners, col_span // col_owners),
+        mirror,
+        precision=lax.Precision.HIGHEST,
+    )
+    width = direct.shape[0]
+    return (
+        rows_sum.reshape(row_owners, width, -1),
+        cols_sum.reshape(col_owners, width, -1),
+    )
 
 
 def body(tiles, coords, counts, valid, start, rotations):
@@ -115,10 +138,18 @@
         col_blocks = col_side.reshape(width, col_span, tile_side)
         row_blocks = row_side.reshape(width, row_span, tile_side)
         rows_total, cols_total = local_terms(
-            flat_tiles, block_rows, block_cols, live, mirror_weight, col_blocks, row_blocks
+            flat_tiles,
+            block_rows,
+            block_cols,
+            live,
+            mirror_weight,
+            col_blocks,
+            row_blocks,
+            col_count,
+            row_count,
         )
-        direct_part = scatter_sum_by_exchange(rows_total.reshape(width, row_span * tile_side), "col")
-        mirror_part = scatter_sum_by_exchange(cols_total.reshape(width, col_span * tile_side), "row")
+        direct_part = scatter_sum_by_exchange(rows_total, "col")
+        mirror_part = scatter_sum_by_exchange(cols_total, "row")
         return direct_part + mirror_part
 
     node_mask = valid.astype(jnp.float32)

time: 283 us -> 273 us (0.965)
  local copies, waits for them, and re-layouts: 24.2 us -> 17.8 us
  other arithmetic: 13.1 us -> 9.97 us
    unnamed x10 -> x4, local copies, waits for them, and re-layouts: 7.87 us -> 0.01 us
    another operation x12 -> x0, local copies, waits for them, and re-layouts: 5.64 us -> none  [scatter_sum_by_exchange(): chunks = jnp.swapaxes(total.reshape(width, count, length // count), 0, 1)]
    transpose x0 -> x4, local copies, waits for them, and re-layouts: none -> 3.41 us  [the longest x2 1.71 us: local_terms(): jnp.einsum('sjb,cst->jcbt', pick_cols.reshape(slots, col_owners, col_span...]
    all_to_all x3 -> x0, other arithmetic: 2.85 us -> none  [gram_sums(): held = lax.all_to_all(copies, ('row', 'col'), 0, 0, tiled=True)]
where the time goes in v3:
time: 273 us; the launch traced here: 271 us
  waiting for transfers between devices  100 us (37%)
  starting transfers between devices  75.8 us (28%)
  matrix products  33.7 us (12%)
  blocking collectives  32.2 us (12%)
  local copies, waits for them, and re-layouts  17.8 us (7%)
  other arithmetic  9.97 us (4%)
    all_to_all x6, waiting for transfers between devices, scatter_sum_by_exchange(): held = lax.all_to_all(chunks, axis, 0, 0, tiled=True)  40.1 us
    all_to_all x5, waiting for transfers between devices, gather_by_exchange(): held = lax.all_to_all(copies, axis, 0, 0, tiled=True)  34.8 us
    all_to_all x5, starting transfers between devices, gather_by_exchange(): held = lax.all_to_all(copies, axis, 0, 0, tiled=True)  28.9 us
    all_to_all x6, starting transfers between devices, scatter_sum_by_exchange(): held = lax.all_to_all(chunks, axis, 0, 0, tiled=True)  27.8 us
    all_to_all x2, waiting for transfers between devices, gram_sums(): held = lax.all_to_all(copies, ('row', 'col'), 0, 0, tiled=True)  25.2 us
    all_to_all x1, blocking collectives, gram_sums(): held = lax.all_to_all(copies, ('row', 'col'), 0, 0, tiled=True)  21.7 us
    all_to_all x2, starting transfers between devices, gram_sums(): held = lax.all_to_all(copies, ('row', 'col'), 0, 0, tiled=True)  19.1 us
    dot_general x3, matrix products, local_terms(): jnp.einsum('sut,cst->csu', part_tiles, col_values, preferred_element_type...  13.5 us
  transfers between devices with their start and end apart: 13, of which 13 were waited for; matrix products, arithmetic and copies ran while one was open for 9% of the time, Pallas kernels for 0%

profile of v3, /device:TPU:1, one launch (start us, length us, event | category | flops | bytes accessed | tf_op | source)
XLA Modules:
  0.0 271.3 jit_solution(10276496903981217730)
XLA Ops:
  1.3 0.7 multiply_convert_fusion
  2.1 0.7 broadcast_in_dim.38
  2.8 6.8 %all-to-all-start = ((bf16[16,9,512]{2,1,0:T(8,128)(2,1)}), bf16[16,9,512]{2,1,0:T(8,128)(2,1)S(1)}, u32[]{:S(2)}, u32[]{:S(2)}) async-start(bf16[16,9,512]{2,1,0:T(8,128)(2,1)} %broadcast_in_dim.38), calls=%async_computation | async-start | bytes 524288 | tf_op jit(solution)/shard_map/all_to_all | solution.py:39
  9.6 0.8 compare_and_fusion
  11.0 0.8 compare_select_fusion.1
  11.8 5.0 %all-to-all-done = bf16[16,9,512]{2,1,0:T(8,128)(2,1)S(1)} async-done(((bf16[16,9,512]{2,1,0:T(8,128)(2,1)}), bf16[16,9,512]{2,1,0:T(8,128)(2,1)S(1)}, u32[]{:S(2)}, u32[]{:S(2)}) %all-to-all-start) | async-done | bytes 147488 | tf_op jit(solution)/shard_map/all_to_all | solution.py:39
  16.8 10.6 %all-to-all-start.2 = ((bf16[16,9,512]{2,1,0:T(8,128)(2,1)}), bf16[16,9,512]{2,1,0:T(8,128)(2,1)S(1)}, u32[]{:S(2)}, u32[]{:S(2)}) async-start(bf16[16,9,512]{2,1,0:T(8,128)(2,1)} %broadcast_in_dim.38), calls=%async_computation.2 | async-start | bytes 524288 | tf_op jit(solution)/shard_map/all_to_all | solution.py:39
  27.4 0.8 slice_bitcast_fusion.2
  29.2 7.6 %all-to-all-done.2 = bf16[16,9,512]{2,1,0:T(8,128)(2,1)S(1)} async-done(((bf16[16,9,512]{2,1,0:T(8,128)(2,1)}), bf16[16,9,512]{2,1,0:T(8,128)(2,1)S(1)}, u32[]{:S(2)}, u32[]{:S(2)}) %all-to-all-start.2) | async-done | bytes 147488 | tf_op jit(solution)/shard_map/all_to_all | solution.py:39
  37.9 3.4 %fusion.21 = f32[9,128,128,1]{2,0,1,3:T(8,128)S(1)} fusion(bf16[1,1,128,128,128]{4,3,2,1,0:T(8,128)(2,1)} %param.11, bf16[128,9,128]{2,1,0:T(8,128)(2,1)S(1)} %gather_fusion.4, f32[128]{0:T(128)S(1)} %compare_select_fusion.1, pred[128]{0:T(512)(128)(4,1)S(1)} %get-tuple-element.4), kind=kOutput, calls=%fused_computation.24 | convolution fusion | flops 38043648 | bytes 5079680 | tf_op jit(solution)/shard_map/sut,csu->cst/dot_general | solution.py:80
  42.0 0.9 reshape.370
  42.9 6.4 %all-to-all-start.3 = ((f32[16,9,512]{2,1,0:T(8,128)}), f32[16,9,512]{2,1,0:T(8,128)S(1)}, u32[]{:S(2)}, u32[]{:S(2)}) async-start(f32[16,9,512]{2,1,0:T(8,128)} %reshape.370), calls=%async_computation.3 | async-start | bytes 1048576 | tf_op jit(solution)/shard_map/all_to_all | solution.py:44
  49.3 4.5 %fusion.15 = f32[9,128,128,1]{2,0,1,3:T(8,128)S(1)} fusion(bf16[1,1,128,128,128]{4,3,2,1,0:T(8,128)(2,1)} %param.11, bf16[128,9,128]{2,1,0:T(8,128)(2,1)S(1)} %gather_fusion.3, f32[128]{0:T(128)S(1)} %compare_convert_fusion, pred[128]{0:T(512)(128)(4,1)S(1)} %get-tuple-element.13), kind=kOutput, calls=%fused_computation.22 | convolution fusion | flops 38043648 | bytes 5079680 | tf_op jit(solution)/shard_map/sut,cst->csu/dot_general | solution.py:76
  54.5 0.9 reshape.369
  55.4 3.9 %all-to-all-done.3 = f32[16,9,512]{2,1,0:T(8,128)S(1)} async-done(((f32[16,9,512]{2,1,0:T(8,128)}), f32[16,9,512]{2,1,0:T(8,128)S(1)}, u32[]{:S(2)}, u32[]{:S(2)}) %all-to-all-start.3) | async-done | bytes 294944 | tf_op jit(solution)/shard_map/all_to_all | solution.py:44
  59.3 4.3 %all-to-all-start.1 = ((f32[16,9,512]{2,1,0:T(8,128)}), f32[16,9,512]{2,1,0:T(8,128)S(1)}, u32[]{:S(2)}, u32[]{:S(2)}) async-start(f32[16,9,512]{2,1,0:T(8,128)} %reshape.369), calls=%async_computation.1 | async-start | bytes 1048576 | tf_op jit(solution)/shard_map/all_to_all | solution.py:44
  63.9 13.9 %all-to-all-done.1 = f32[16,9,512]{2,1,0:T(8,128)S(1)} async-done(((f32[16,9,512]{2,1,0:T(8,128)}), f32[16,9,512]{2,1,0:T(8,128)S(1)}, u32[]{:S(2)}, u32[]{:S(2)}) %all-to-all-start.1) | async-done | bytes 294944 | tf_op jit(solution)/shard_map/all_to_all | solution.py:44
  78.2 0.7 broadcast_in_dim.39
  78.9 9.9 %all-to-all-start.4 = ((f32[256,1,128]{2,1,0:T(1,128)}), f32[256,1,128]{2,1,0:T(1,128)S(1)}, u32[]{:S(2)}, u32[]{:S(2)}) async-start(f32[256,1,128]{2,1,0:T(1,128)} %broadcast_in_dim.39), calls=%async_computation.4 | async-start | bytes 262144 | tf_op jit(solution)/shard_map/all_to_all | solution.py:55
  88.8 12.6 %all-to-all-done.4 = f32[256,1,128]{2,1,0:T(1,128)S(1)} async-done(((f32[256,1,128]{2,1,0:T(1,128)}), f32[256,1,128]{2,1,0:T(1,128)S(1)}, u32[]{:S(2)}, u32[]{:S(2)}) %all-to-all-start.4) | async-done | bytes 131104 | tf_op jit(solution)/shard_map/all_to_all | solution.py:55
  106.6 10.6 %all_to_all.78 = bf16[16,8,512]{2,1,0:T(8,128)(2,1)S(1)} all-to-all(bf16[16,8,512]{2,1,0:T(8,128)(2,1)} %broadcast_in_dim.41), channel_id=1, replica_groups=mesh['row'=16,'col'=16] {'row'}, dimensions={0} | all-to-all | bytes 262144 | tf_op jit(solution)/shard_map/all_to_all | solution.py:39
  117.1 3.5 %all-to-all-start.7 = ((bf16[16,8,512]{2,1,0:T(8,128)(2,1)}), bf16[16,8,512]{2,1,0:T(8,128)(2,1)S(1)}, u32[]{:S(2)}, u32[]{:S(2)}) async-start(bf16[16,8,512]{2,1,0:T(8,128)(2,1)} %broadcast_in_dim.41), calls=%async_computation.7 | async-start | bytes 262144 | tf_op jit(solution)/shard_map/all_to_all | solution.py:39
  121.3 8.3 %all-to-all-done.7 = bf16[16,8,512]{2,1,0:T(8,128)(2,1)S(1)} async-done(((bf16[16,8,512]{2,1,0:T(8,128)(2,1)}), bf16[16,8,512]{2,1,0:T(8,128)(2,1)S(1)}, u32[]{:S(2)}, u32[]{:S(2)}) %all-to-all-start.7) | async-done | bytes 131104 | tf_op jit(solution)/shard_map/all_to_all | solution.py:39
  130.3 3.4 %fusion.33 = f32[8,128,128,1]{2,0,1,3:T(8,128)S(1)} fusion(bf16[1,1,128,128,128]{4,3,2,1,0:T(8,128)(2,1)} %param.11, bf16[128,8,128]{2,1,0:T(8,128)(2,1)S(1)} %gather_fusion.6, f32[128]{0:T(128)S(1)} %compare_select_fusion.1, pred[128]{0:T(512)(128)(4,1)S(1)} %get-tuple-element.4), kind=kOutput, calls=%fused_computation.28 | convolution fusion | flops 33816576 | bytes 4981376 | tf_op jit(solution)/shard_map/sut,csu->cst/dot_general | solution.py:80
  134.1 0.9 copy.156
  135.0 5.0 %all-to-all-start.8 = ((f32[16,8,512]{2,1,0:T(8,128)}), f32[16,8,512]{2,1,0:T(8,128)S(1)}, u32[]{:S(2)}, u32[]{:S(2)}) async-start(f32[16,8,512]{2,1,0:T(8,128)} %bitcast.220), calls=%async_computation.8 | async-start | bytes 524288 | tf_op jit(solution)/shard_map/all_to_all | solution.py:44
  140.0 4.5 %fusion.27 = f32[8,128,128,1]{2,0,1,3:T(8,128)S(1)} fusion(bf16[1,1,128,128,128]{4,3,2,1,0:T(8,128)(2,1)} %param.11, bf16[128,8,128]{2,1,0:T(8,128)(2,1)S(1)} %gather_fusion.5, f32[128]{0:T(128)S(1)} %compare_convert_fusion, pred[128]{0:T(512)(128)(4,1)S(1)} %get-tuple-element.13), kind=kOutput, calls=%fused_computation.26 | convolution fusion | flops 33816576 | bytes 4981376 | tf_op jit(solution)/shard_map/sut,cst->csu/dot_general | solution.py:76
  144.9 0.8 copy.157
  145.7 1.5 all-to-all-done.8
  147.3 3.5 %all-to-all-start.6 = ((f32[16,8,512]{2,1,0:T(8,128)}), f32[16,8,512]{2,1,0:T(8,128)S(1)}, u32[]{:S(2)}, u32[]{:S(2)}) async-start(f32[16,8,512]{2,1,0:T(8,128)} %bitcast.221), calls=%async_computation.6 | async-start | bytes 524288 | tf_op jit(solution)/shard_map/all_to_all | solution.py:44
  151.4 9.7 %all-to-all-done.6 = f32[16,8,512]{2,1,0:T(8,128)S(1)} async-done(((f32[16,8,512]{2,1,0:T(8,128)}), f32[16,8,512]{2,1,0:T(8,128)S(1)}, u32[]{:S(2)}, u32[]{:S(2)}) %all-to-all-start.6) | async-done | bytes 262176 | tf_op jit(solution)/shard_map/all_to_all | solution.py:44
  162.2 9.2 %all-to-all-start.9 = ((f32[256,1,128]{2,1,0:T(1,128)}), f32[256,1,128]{2,1,0:T(1,128)S(1)}, u32[]{:S(2)}, u32[]{:S(2)}) async-start(f32[256,1,128]{2,1,0:T(1,128)} %broadcast_in_dim.42), calls=%async_computation.9 | async-start | bytes 262144 | tf_op jit(solution)/shard_map/all_to_all | solution.py:55
  171.5 12.6 %all-to-all-done.9 = f32[256,1,128]{2,1,0:T(1,128)S(1)} async-done(((f32[256,1,128]{2,1,0:T(1,128)}), f32[256,1,128]{2,1,0:T(1,128)S(1)}, u32[]{:S(2)}, u32[]{:S(2)}) %all-to-all-start.9) | async-done | bytes 131104 | tf_op jit(solution)/shard_map/all_to_all | solution.py:55
  189.2 4.4 %all-to-all-start.10 = ((bf16[16,8,512]{2,1,0:T(8,128)(2,1)}), bf16[16,8,512]{2,1,0:T(8,128)(2,1)S(1)}, u32[]{:S(2)}, u32[]{:S(2)}) async-start(bf16[16,8,512]{2,1,0:T(8,128)(2,1)} %broadcast_in_dim.43), calls=%async_computation.10 | async-start | bytes 262144 | tf_op jit(solution)/shard_map/all_to_all | solution.py:39
  193.8 6.0 %all-to-all-done.10 = bf16[16,8,512]{2,1,0:T(8,128)(2,1)S(1)} async-done(((bf16[16,8,512]{2,1,0:T(8,128)(2,1)}), bf16[16,8,512]{2,1,0:T(8,128)(2,1)S(1)}, u32[]{:S(2)}, u32[]{:S(2)}) %all-to-all-start.10) | async-done | bytes 131104 | tf_op jit(solution)/shard_map/all_to_all | solution.py:39
  199.8 3.5 %all-to-all-start.12 = ((bf16[16,8,512]{2,1,0:T(8,128)(2,1)}), bf16[16,8,512]{2,1,0:T(8,128)(2,1)S(1)}, u32[]{:S(2)}, u32[]{:S(2)}) async-start(bf16[16,8,512]{2,1,0:T(8,128)(2,1)} %broadcast_in_dim.43), calls=%async_computation.12 | async-start | bytes 262144 | tf_op jit(solution)/shard_map/all_to_all | solution.py:39
  204.3 7.9 %all-to-all-done.12 = bf16[16,8,512]{2,1,0:T(8,128)(2,1)S(1)} async-done(((bf16[16,8,512]{2,1,0:T(8,128)(2,1)}), bf16[16,8,512]{2,1,0:T(8,128)(2,1)S(1)}, u32[]{:S(2)}, u32[]{:S(2)}) %all-to-all-start.12) | async-done | bytes 131104 | tf_op jit(solution)/shard_map/all_to_all | solution.py:39
  213.0 3.4 %fusion.45 = f32[8,128,128,1]{2,0,1,3:T(8,128)S(1)} fusion(bf16[1,1,128,128,128]{4,3,2,1,0:T(8,128)(2,1)} %param.11, bf16[128,8,128]{2,1,0:T(8,128)(2,1)S(1)} %gather_fusion.8, f32[128]{0:T(128)S(1)} %compare_select_fusion.1, pred[128]{0:T(512)(128)(4,1)S(1)} %get-tuple-element.4), kind=kOutput, calls=%fused_computation.32 | convolution fusion | flops 33816576 | bytes 4981376 | tf_op jit(solution)/shard_map/sut,csu->cst/dot_general | solution.py:80
  216.8 0.9 copy.154
  217.6 5.0 %all-to-all-start.13 = ((f32[16,8,512]{2,1,0:T(8,128)}), f32[16,8,512]{2,1,0:T(8,128)S(1)}, u32[]{:S(2)}, u32[]{:S(2)}) async-start(f32[16,8,512]{2,1,0:T(8,128)} %bitcast.218), calls=%async_computation.13 | async-start | bytes 524288 | tf_op jit(solution)/shard_map/all_to_all | solution.py:44
  222.7 4.5 %fusion.39 = f32[8,128,128,1]{2,0,1,3:T(8,128)S(1)} fusion(bf16[1,1,128,128,128]{4,3,2,1,0:T(8,128)(2,1)} %param.11, bf16[128,8,128]{2,1,0:T(8,128)(2,1)S(1)} %gather_fusion.7, f32[128]{0:T(128)S(1)} %compare_convert_fusion, pred[128]{0:T(512)(128)(4,1)S(1)} %get-tuple-element.13), kind=kOutput, calls=%fused_computation.30 | convolution fusion | flops 33816576 | bytes 4981376 | tf_op jit(solution)/shard_map/sut,cst->csu/dot_general | solution.py:76
  227.5 0.8 copy.155
  228.4 1.5 all-to-all-done.13
  229.9 3.5 %all-to-all-start.11 = ((f32[16,8,512]{2,1,0:T(8,128)}), f32[16,8,512]{2,1,0:T(8,128)S(1)}, u32[]{:S(2)}, u32[]{:S(2)}) async-start(f32[16,8,512]{2,1,0:T(8,128)} %bitcast.219), calls=%async_computation.11 | async-start | bytes 524288 | tf_op jit(solution)/shard_map/all_to_all | solution.py:44
  234.0 9.7 %all-to-all-done.11 = f32[16,8,512]{2,1,0:T(8,128)S(1)} async-done(((f32[16,8,512]{2,1,0:T(8,128)}), f32[16,8,512]{2,1,0:T(8,128)S(1)}, u32[]{:S(2)}, u32[]{:S(2)}) %all-to-all-start.11) | async-done | bytes 262176 | tf_op jit(solution)/shard_map/all_to_all | solution.py:44
  244.2 21.7 %all_to_all.79 = f32[256,1,128]{2,1,0:T(1,128)S(1)} all-to-all(f32[256,1,128]{2,1,0:T(1,128)S(1)} %broadcast_in_dim.44), channel_id=1, replica_groups=mesh['row'=16,'col'=16] {'row','col'}, dimensions={0} | all-to-all | bytes 262144 | tf_op jit(solution)/shard_map/all_to_all | solution.py:55
  269.7 0.8 fusion.190
  270.5 0.7 fusion.192
  (126 shorter events, 26.5 us)
Async XLA Ops:
  2.8 14.0 %all-to-all-start = ((bf16[16,9,512]{2,1,0:T(8,128)(2,1)}), bf16[16,9,512]{2,1,0:T(8,128)(2,1)S(1)}, u32[]{:S(2)}, u32[]{:S(2)}) async-start(bf16[16,9,512]{2,1,0:T(8,128)(2,1)} %broadcast_in_dim.38), calls=%async_computation | async-start | bytes 524288 | tf_op jit(solution)/shard_map/all_to_all | solution.py:39
  16.8 20.0 %all-to-all-start.2 = ((bf16[16,9,512]{2,1,0:T(8,128)(2,1)}), bf16[16,9,512]{2,1,0:T(8,128)(2,1)S(1)}, u32[]{:S(2)}, u32[]{:S(2)}) async-start(bf16[16,9,512]{2,1,0:T(8,128)(2,1)} %broadcast_in_dim.38), calls=%async_computation.2 | async-start | bytes 524288 | tf_op jit(solution)/shard_map/all_to_all | solution.py:39
  42.9 16.4 %all-to-all-start.3 = ((f32[16,9,512]{2,1,0:T(8,128)}), f32[16,9,512]{2,1,0:T(8,128)S(1)}, u32[]{:S(2)}, u32[]{:S(2)}) async-start(f32[16,9,512]{2,1,0:T(8,128)} %reshape.370), calls=%async_computation.3 | async-start | bytes 1048576 | tf_op jit(solution)/shard_map/all_to_all | solution.py:44
  49.3 14.3 %copy-start = (f32[8,512]{1,0:T(8,128)S(1)}, f32[8,512]{1,0:T(8,128)}, u32[]{:S(2)}) copy-start(f32[8,512]{1,0:T(8,128)} %param.15) | copy-start | bytes 49156
  59.3 18.5 %all-to-all-start.1 = ((f32[16,9,512]{2,1,0:T(8,128)}), f32[16,9,512]{2,1,0:T(8,128)S(1)}, u32[]{:S(2)}, u32[]{:S(2)}) async-start(f32[16,9,512]{2,1,0:T(8,128)} %reshape.369), calls=%async_computation.1 | async-start | bytes 1048576 | tf_op jit(solution)/shard_map/all_to_all | solution.py:44
  78.9 22.5 %all-to-all-start.4 = ((f32[256,1,128]{2,1,0:T(1,128)}), f32[256,1,128]{2,1,0:T(1,128)S(1)}, u32[]{:S(2)}, u32[]{:S(2)}) async-start(f32[256,1,128]{2,1,0:T(1,128)} %broadcast_in_dim.39), calls=%async_computation.4 | async-start | bytes 262144 | tf_op jit(solution)/shard_map/all_to_all | solution.py:55
  117.1 12.5 %all-to-all-start.7 = ((bf16[16,8,512]{2,1,0:T(8,128)(2,1)}), bf16[16,8,512]{2,1,0:T(8,128)(2,1)S(1)}, u32[]{:S(2)}, u32[]{:S(2)}) async-start(bf16[16,8,512]{2,1,0:T(8,128)(2,1)} %broadcast_in_dim.41), calls=%async_computation.7 | async-start | bytes 262144 | tf_op jit(solution)/shard_map/all_to_all | solution.py:39
  133.8 17.2 %copy-start.1 = (f32[2,8,24]{2,1,0:T(8,128)S(1)}, f32[2,8,24]{2,1,0:T(8,128)}, u32[]{:S(2)}) copy-start(f32[2,8,24]{2,1,0:T(8,128)} %param.16) | copy-start | bytes 4612
  135.0 12.2 %all-to-all-start.8 = ((f32[16,8,512]{2,1,0:T(8,128)}), f32[16,8,512]{2,1,0:T(8,128)S(1)}, u32[]{:S(2)}, u32[]{:S(2)}) async-start(f32[16,8,512]{2,1,0:T(8,128)} %bitcast.220), calls=%async_computation.8 | async-start | bytes 524288 | tf_op jit(solution)/shard_map/all_to_all | solution.py:44
  147.3 13.8 %all-to-all-start.6 = ((f32[16,8,512]{2,1,0:T(8,128)}), f32[16,8,512]{2,1,0:T(8,128)S(1)}, u32[]{:S(2)}, u32[]{:S(2)}) async-start(f32[16,8,512]{2,1,0:T(8,128)} %bitcast.221), calls=%async_computation.6 | async-start | bytes 524288 | tf_op jit(solution)/shard_map/all_to_all | solution.py:44
  162.2 21.8 %all-to-all-start.9 = ((f32[256,1,128]{2,1,0:T(1,128)}), f32[256,1,128]{2,1,0:T(1,128)S(1)}, u32[]{:S(2)}, u32[]{:S(2)}) async-start(f32[256,1,128]{2,1,0:T(1,128)} %broadcast_in_dim.42), calls=%async_computation.9 | async-start | bytes 262144 | tf_op jit(solution)/shard_map/all_to_all | solution.py:55
  189.2 10.6 %all-to-all-start.10 = ((bf16[16,8,512]{2,1,0:T(8,128)(2,1)}), bf16[16,8,512]{2,1,0:T(8,128)(2,1)S(1)}, u32[]{:S(2)}, u32[]{:S(2)}) async-start(bf16[16,8,512]{2,1,0:T(8,128)(2,1)} %broadcast_in_dim.43), calls=%async_computation.10 | async-start | bytes 262144 | tf_op jit(solution)/shard_map/all_to_all | solution.py:39
  199.8 12.5 %all-to-all-start.12 = ((bf16[16,8,512]{2,1,0:T(8,128)(2,1)}), bf16[16,8,512]{2,1,0:T(8,128)(2,1)S(1)}, u32[]{:S(2)}, u32[]{:S(2)}) async-start(bf16[16,8,512]{2,1,0:T(8,128)(2,1)} %broadcast_in_dim.43), calls=%async_computation.12 | async-start | bytes 262144 | tf_op jit(solution)/shard_map/all_to_all | solution.py:39
  217.6 12.3 %all-to-all-start.13 = ((f32[16,8,512]{2,1,0:T(8,128)}), f32[16,8,512]{2,1,0:T(8,128)S(1)}, u32[]{:S(2)}, u32[]{:S(2)}) async-start(f32[16,8,512]{2,1,0:T(8,128)} %bitcast.218), calls=%async_computation.13 | async-start | bytes 524288 | tf_op jit(solution)/shard_map/all_to_all | solution.py:44
  229.9 13.8 %all-to-all-start.11 = ((f32[16,8,512]{2,1,0:T(8,128)}), f32[16,8,512]{2,1,0:T(8,128)S(1)}, u32[]{:S(2)}, u32[]{:S(2)}) async-start(f32[16,8,512]{2,1,0:T(8,128)} %bitcast.219), calls=%async_computation.11 | async-start | bytes 524288 | tf_op jit(solution)/shard_map/all_to_all | solution.py:44

commit v4 on v2

--- a/solution.py
+++ b/solution.py
@@ -40,47 +40,56 @@
     return jnp.swapaxes(held, 0, 1).reshape(local.shape[0], count * local.shape[1])
 
 
-def scatter_sum_by_exchange(total, axis):
-    count = lax.axis_size(axis)
-    width, length = total.shape
-    chunks = jnp.swapaxes(total.reshape(width, count, length // count), 0, 1)
+def scatter_sum_by_exchange(chunks, axis):
     held = lax.all_to_all(chunks, axis, 0, 0, tiled=True)
     return jnp.sum(held, axis=0)
 
 
 def gram_sums(new_vecs, new_images):
-    local = jnp.stack([matmul_high(new_vecs, new_vecs.T), matmul_high(new_images, new_vecs.T)])
+    order = new_vecs.shape[0]
+    local = jnp.concatenate(
+        [matmul_high(new_vecs, new_vecs.T).reshape(-1), matmul_high(new_images, new_vecs.T).reshape(-1)]
+    )
     count = lax.axis_size("row") * lax.axis_size("col")
     copies = jnp.broadcast_to(local[None], (count,) + local.shape)
     held = lax.all_to_all(copies, ("row", "col"), 0, 0, tiled=True)
     total = jnp.sum(held, axis=0)
-    return total[0], total[1]
+    return total[: order * order].reshape(order, order), total[order * order :].reshape(order, order)
 
 
-def local_terms(
-    part_tiles, part_rows, part_cols, weight_direct, weight_mirror, col_blocks, row_blocks
-):
-    row_span = row_blocks.shape[1]
-    col_span = col_blocks.shape[1]
+def block_sums(pick, part_values, owners):
+    slots, span = pick.shape
+    sums = jnp.einsum(
+        "sjb,csu->jcbu",
+        pick.reshape(slots, owners, span // owners),
+        part_values,
+        precision=lax.Precision.HIGHEST,
+    )
+    return sums.reshape(owners, part_values.shape[0], -1)
+
+
+def direct_terms(part_tiles, part_rows, part_cols, weight_direct, col_blocks, row_span, owners):
     col_values = jnp.take(col_blocks, part_cols, axis=1)
-    row_values = jnp.take(row_blocks, part_rows, axis=1)
     direct = (
         jnp.einsum("sut,cst->csu", part_tiles, col_values, preferred_element_type=jnp.float32)
         * weight_direct[None, :, None]
     )
+    pick_rows = (part_rows[:, None] == jnp.arange(row_span, dtype=jnp.int32)[None, :]).astype(
+        jnp.float32
+    )
+    return block_sums(pick_rows, direct, owners)
+
+
+def mirror_terms(part_tiles, part_rows, part_cols, weight_mirror, row_blocks, col_span, owners):
+    row_values = jnp.take(row_blocks, part_rows, axis=1)
     mirror = (
         jnp.einsum("sut,csu->cst", part_tiles, row_values, preferred_element_type=jnp.float32)
         * weight_mirror[None, :, None]
     )
-    pick_rows = (part_rows[:, None] == jnp.arange(row_span, dtype=jnp.int32)[None, :]).astype(
-        jnp.float32
-    )
     pick_cols = (part_cols[:, None] == jnp.arange(col_span, dtype=jnp.int32)[None, :]).astype(
         jnp.float32
     )
-    rows_sum = jnp.einsum("sp,csu->cpu", pick_rows, direct, precision=lax.Precision.HIGHEST)
-    cols_sum = jnp.einsum("sq,cst->cqt", pick_cols, mirror, precision=lax.Precision.HIGHEST)
-    return (rows_sum, cols_sum)
+    return block_sums(pick_cols, mirror, owners)
 
 
 def body(tiles, coords, counts, valid, start, rotations):
@@ -111,14 +120,19 @@
         width = vectors.shape[0]
         short = vectors.astype(jnp.bfloat16)
         col_side = gather_by_exchange(short, "row")
+        col_blocks = col_side.reshape(width, col_span, tile_side)
+        rows_total = direct_terms(
+            flat_tiles, block_rows, block_cols, live, col_blocks, row_span, col_count
+        )
         row_side = gather_by_exchange(short, "col")
-        col_blocks = col_side.reshape(width, col_span, tile_side)
+        rows_total, row_side = lax.optimization_barrier((rows_total, row_side))
         row_blocks = row_side.reshape(width, row_span, tile_side)
-        rows_total, cols_total = local_terms(
-            flat_tiles, block_rows, block_cols, live, mirror_weight, col_blocks, row_blocks
+        cols_total = mirror_terms(
+            flat_tiles, block_rows, block_cols, mirror_weight, row_blocks, col_span, row_count
         )
-        direct_part = scatter_sum_by_exchange(rows_total.reshape(width, row_span * tile_side), "col")
-        mirror_part = scatter_sum_by_exchange(cols_total.reshape(width, col_span * tile_side), "row")
+        direct_part = scatter_sum_by_exchange(rows_total, "col")
+        direct_part, cols_total = lax.optimization_barrier((direct_part, cols_total))
+        mirror_part = scatter_sum_by_exchange(cols_total, "row")
         return direct_part + mirror_part
 
     node_mask = valid.astype(jnp.float32)

time: 283 us -> 259 us (0.915)
  blocking collectives: 32.3 us -> 18.8 us
  waiting for transfers between devices: 100 us -> 91.1 us
  starting transfers between devices: 76.1 us -> 84.8 us
  local copies, waits for them, and re-layouts: 24.2 us -> 17.9 us
  other arithmetic: 13.1 us -> 9.19 us
    all_to_all x6, starting transfers between devices: 27.8 us -> 38.9 us  [scatter_sum_by_exchange(): held = lax.all_to_all(chunks, axis, 0, 0, tiled=True)]
    all_to_all x1 -> x0, blocking collectives: 10.6 us -> none  [gather_by_exchange(): held = lax.all_to_all(copies, axis, 0, 0, tiled=True)]
    all_to_all x5 -> x6, waiting for transfers between devices: 34.6 us -> 25.3 us  [gather_by_exchange(): held = lax.all_to_all(copies, axis, 0, 0, tiled=True)]
    unnamed x10 -> x9, local copies, waits for them, and re-layouts: 7.87 us -> 0.23 us
    all_to_all x2, starting transfers between devices: 19.2 us -> 12.6 us  [gram_sums(): held = lax.all_to_all(copies, ('row', 'col'), 0, 0, tiled=True)]
    another operation x14 -> x0, local copies, waits for them, and re-layouts: 5.85 us -> none  [the longest x12 5.64 us: scatter_sum_by_exchange(): chunks = jnp.swapaxes(total.reshape(width, count, length // count), 0, 1)]
    all_to_all x5 -> x6, starting transfers between devices: 29.1 us -> 33.3 us  [gather_by_exchange(): held = lax.all_to_all(copies, axis, 0, 0, tiled=True)]
    transpose x0 -> x4, local copies, waits for them, and re-layouts: none -> 3.41 us  [block_sums(): jnp.einsum('sjb,csu->jcbu', pick.reshape(slots, owners, span // owners),...]
  transfers between devices with their start and end apart: 13 -> 14, of which waited for: 13 -> 14; matrix products, arithmetic and copies ran while one was open for 9% -> 15% of each run, Pallas kernels for 0% -> 0%
where the time goes in v4:
time: 259 us; the launch traced here: 257 us
  waiting for transfers between devices  91.1 us (35%)
  starting transfers between devices  84.8 us (33%)
  matrix products  33.7 us (13%)
  blocking collectives  18.8 us (7%)
  local copies, waits for them, and re-layouts  17.9 us (7%)
  other arithmetic  9.19 us (4%)
    all_to_all x6, waiting for transfers between devices, scatter_sum_by_exchange(): held = lax.all_to_all(chunks, axis, 0, 0, tiled=True)  41.1 us
    all_to_all x6, starting transfers between devices, scatter_sum_by_exchange(): held = lax.all_to_all(chunks, axis, 0, 0, tiled=True)  38.9 us
    all_to_all x6, starting transfers between devices, gather_by_exchange(): held = lax.all_to_all(copies, axis, 0, 0, tiled=True)  33.3 us
    all_to_all x6, waiting for transfers between devices, gather_by_exchange(): held = lax.all_to_all(copies, axis, 0, 0, tiled=True)  25.3 us
    all_to_all x2, waiting for transfers between devices, gram_sums(): held = lax.all_to_all(copies, ('row', 'col'), 0, 0, tiled=True)  24.8 us
    all_to_all x1, blocking collectives, gram_sums(): held = lax.all_to_all(copies, ('row', 'col'), 0, 0, tiled=True)  18.8 us
    dot_general x3, matrix products, direct_terms(): jnp.einsum('sut,cst->csu', part_tiles, col_values, preferred_element_type...  13.5 us
    all_to_all x2, starting transfers between devices, gram_sums(): held = lax.all_to_all(copies, ('row', 'col'), 0, 0, tiled=True)  12.6 us
  transfers between devices with their start and end apart: 14, of which 14 were waited for; matrix products, arithmetic and copies ran while one was open for 15% of the time, Pallas kernels for 0%

profile of v4, /device:TPU:1, one launch (start us, length us, event | category | flops | bytes accessed | tf_op | source)
XLA Modules:
  0.0 257.2 jit_solution(1019975677425343483)
XLA Ops:
  1.3 0.7 multiply_convert_fusion
  2.1 0.7 broadcast_in_dim.38
  2.8 6.8 %all-to-all-start = ((bf16[16,9,512]{2,1,0:T(8,128)(2,1)}), bf16[16,9,512]{2,1,0:T(8,128)(2,1)S(1)}, u32[]{:S(2)}, u32[]{:S(2)}) async-start(bf16[16,9,512]{2,1,0:T(8,128)(2,1)} %broadcast_in_dim.38), calls=%async_computation | async-start | bytes 524288 | tf_op jit(solution)/shard_map/all_to_all | solution.py:39
  9.6 0.8 compare_and_fusion
  10.4 0.8 slice_bitcast_fusion.2
  11.8 5.0 %all-to-all-done = bf16[16,9,512]{2,1,0:T(8,128)(2,1)S(1)} async-done(((bf16[16,9,512]{2,1,0:T(8,128)(2,1)}), bf16[16,9,512]{2,1,0:T(8,128)(2,1)S(1)}, u32[]{:S(2)}, u32[]{:S(2)}) %all-to-all-start) | async-done | bytes 147488 | tf_op jit(solution)/shard_map/all_to_all | solution.py:39
  16.8 10.6 %all-to-all-start.1 = ((bf16[16,9,512]{2,1,0:T(8,128)(2,1)}), bf16[16,9,512]{2,1,0:T(8,128)(2,1)S(1)}, u32[]{:S(2)}, u32[]{:S(2)}) async-start(bf16[16,9,512]{2,1,0:T(8,128)(2,1)} %broadcast_in_dim.38), calls=%async_computation.1 | async-start | bytes 524288 | tf_op jit(solution)/shard_map/all_to_all | solution.py:39
  28.5 4.5 %fusion.15 = f32[9,128,128,1]{2,0,1,3:T(8,128)S(1)} fusion(bf16[1,1,128,128,128]{4,3,2,1,0:T(8,128)(2,1)} %param.11, bf16[128,9,128]{2,1,0:T(8,128)(2,1)S(1)} %gather_fusion.3, f32[128]{0:T(128)S(1)} %compare_convert_fusion, pred[128]{0:T(512)(128)(4,1)S(1)} %get-tuple-element.37), kind=kOutput, calls=%fused_computation.22 | convolution fusion | flops 38043648 | bytes 5079680 | tf_op jit(solution)/shard_map/sut,cst->csu/dot_general | solution.py:74
  33.5 3.3 %all-to-all-done.1 = bf16[16,9,512]{2,1,0:T(8,128)(2,1)S(1)} async-done(((bf16[16,9,512]{2,1,0:T(8,128)(2,1)}), bf16[16,9,512]{2,1,0:T(8,128)(2,1)S(1)}, u32[]{:S(2)}, u32[]{:S(2)}) %all-to-all-start.1) | async-done | bytes 147488 | tf_op jit(solution)/shard_map/all_to_all | solution.py:39
  37.1 1.0 copy.97
  38.1 6.2 %all-to-all-start.2 = ((f32[16,9,512]{2,1,0:T(8,128)}), f32[16,9,512]{2,1,0:T(8,128)S(1)}, u32[]{:S(2)}, u32[]{:S(2)}) async-start(f32[16,9,512]{2,1,0:T(8,128)} %copy.97), calls=%async_computation.2 | async-start | bytes 1048576 | tf_op jit(solution)/shard_map/all_to_all | solution.py:44
  45.3 3.5 %fusion.21 = f32[9,128,128,1]{2,0,1,3:T(8,128)S(1)} fusion(bf16[1,1,128,128,128]{4,3,2,1,0:T(8,128)(2,1)} %param.11, bf16[128,9,128]{2,1,0:T(8,128)(2,1)S(1)} %gather_fusion.4, f32[128]{0:T(128)S(1)} %compare_select_fusion.1, pred[128]{0:T(512)(128)(4,1)S(1)} %get-tuple-element.29), kind=kOutput, calls=%fused_computation.24 | convolution fusion | flops 38043648 | bytes 5079680 | tf_op jit(solution)/shard_map/sut,csu->cst/dot_general | solution.py:86
  49.3 9.2 %all-to-all-done.2 = f32[16,9,512]{2,1,0:T(8,128)S(1)} async-done(((f32[16,9,512]{2,1,0:T(8,128)}), f32[16,9,512]{2,1,0:T(8,128)S(1)}, u32[]{:S(2)}, u32[]{:S(2)}) %all-to-all-start.2) | async-done | bytes 294944 | tf_op jit(solution)/shard_map/all_to_all | solution.py:44
  58.5 1.0 copy.101
  59.5 7.2 %all-to-all-start.3 = ((f32[16,9,512]{2,1,0:T(8,128)}), f32[16,9,512]{2,1,0:T(8,128)S(1)}, u32[]{:S(2)}, u32[]{:S(2)}) async-start(f32[16,9,512]{2,1,0:T(8,128)} %copy.101), calls=%async_computation.3 | async-start | bytes 1048576 | tf_op jit(solution)/shard_map/all_to_all | solution.py:44
  67.0 9.7 %all-to-all-done.3 = f32[16,9,512]{2,1,0:T(8,128)S(1)} async-done(((f32[16,9,512]{2,1,0:T(8,128)}), f32[16,9,512]{2,1,0:T(8,128)S(1)}, u32[]{:S(2)}, u32[]{:S(2)}) %all-to-all-start.3) | async-done | bytes 294944 | tf_op jit(solution)/shard_map/all_to_all | solution.py:44
  77.0 0.7 broadcast_in_dim.39
  77.7 6.3 %all-to-all-start.4 = ((f32[256,1,128]{2,1,0:T(1,128)}), f32[256,1,128]{2,1,0:T(1,128)S(1)}, u32[]{:S(2)}, u32[]{:S(2)}) async-start(f32[256,1,128]{2,1,0:T(1,128)} %broadcast_in_dim.39), calls=%async_computation.4 | async-start | bytes 262144 | tf_op jit(solution)/shard_map/all_to_all | solution.py:55
  84.1 12.6 %all-to-all-done.4 = f32[256,1,128]{2,1,0:T(1,128)S(1)} async-done(((f32[256,1,128]{2,1,0:T(1,128)}), f32[256,1,128]{2,1,0:T(1,128)S(1)}, u32[]{:S(2)}, u32[]{:S(2)}) %all-to-all-start.4) | async-done | bytes 131104 | tf_op jit(solution)/shard_map/all_to_all | solution.py:55
  101.8 4.4 %all-to-all-start.5 = ((bf16[16,8,512]{2,1,0:T(8,128)(2,1)}), bf16[16,8,512]{2,1,0:T(8,128)(2,1)S(1)}, u32[]{:S(2)}, u32[]{:S(2)}) async-start(bf16[16,8,512]{2,1,0:T(8,128)(2,1)} %broadcast_in_dim.41), calls=%async_computation.5 | async-start | bytes 262144 | tf_op jit(solution)/shard_map/all_to_all | solution.py:39
  106.4 6.0 %all-to-all-done.5 = bf16[16,8,512]{2,1,0:T(8,128)(2,1)S(1)} async-done(((bf16[16,8,512]{2,1,0:T(8,128)(2,1)}), bf16[16,8,512]{2,1,0:T(8,128)(2,1)S(1)}, u32[]{:S(2)}, u32[]{:S(2)}) %all-to-all-start.5) | async-done | bytes 131104 | tf_op jit(solution)/shard_map/all_to_all | solution.py:39
  112.4 3.5 %all-to-all-start.6 = ((bf16[16,8,512]{2,1,0:T(8,128)(2,1)}), bf16[16,8,512]{2,1,0:T(8,128)(2,1)S(1)}, u32[]{:S(2)}, u32[]{:S(2)}) async-start(bf16[16,8,512]{2,1,0:T(8,128)(2,1)} %broadcast_in_dim.41), calls=%async_computation.6 | async-start | bytes 262144 | tf_op jit(solution)/shard_map/all_to_all | solution.py:39
  116.6 4.5 %fusion.27 = f32[8,128,128,1]{2,0,1,3:T(8,128)S(1)} fusion(bf16[1,1,128,128,128]{4,3,2,1,0:T(8,128)(2,1)} %param.11, bf16[128,8,128]{2,1,0:T(8,128)(2,1)S(1)} %gather_fusion.5, f32[128]{0:T(128)S(1)} %compare_convert_fusion, pred[128]{0:T(512)(128)(4,1)S(1)} %get-tuple-element.37), kind=kOutput, calls=%fused_computation.26 | convolution fusion | flops 33816576 | bytes 4981376 | tf_op jit(solution)/shard_map/sut,cst->csu/dot_general | solution.py:74
  121.5 0.8 copy.165
  122.3 2.6 all-to-all-done.6
  124.9 6.5 %all-to-all-start.7 = ((f32[16,8,512]{2,1,0:T(8,128)}), f32[16,8,512]{2,1,0:T(8,128)S(1)}, u32[]{:S(2)}, u32[]{:S(2)}) async-start(f32[16,8,512]{2,1,0:T(8,128)} %bitcast.237), calls=%async_computation.7 | async-start | bytes 524288 | tf_op jit(solution)/shard_map/all_to_all | solution.py:44
  132.1 3.4 %fusion.33 = f32[8,128,128,1]{2,0,1,3:T(8,128)S(1)} fusion(bf16[1,1,128,128,128]{4,3,2,1,0:T(8,128)(2,1)} %param.11, bf16[128,8,128]{2,1,0:T(8,128)(2,1)S(1)} %gather_fusion.6, f32[128]{0:T(128)S(1)} %compare_select_fusion.1, pred[128]{0:T(512)(128)(4,1)S(1)} %get-tuple-element.29), kind=kOutput, calls=%fused_computation.28 | convolution fusion | flops 33816576 | bytes 4981376 | tf_op jit(solution)/shard_map/sut,csu->cst/dot_general | solution.py:86
  135.9 0.9 copy.164
  136.7 4.2 %all-to-all-done.7 = f32[16,8,512]{2,1,0:T(8,128)S(1)} async-done(((f32[16,8,512]{2,1,0:T(8,128)}), f32[16,8,512]{2,1,0:T(8,128)S(1)}, u32[]{:S(2)}, u32[]{:S(2)}) %all-to-all-start.7) | async-done | bytes 262176 | tf_op jit(solution)/shard_map/all_to_all | solution.py:44
  141.0 6.3 %all-to-all-start.8 = ((f32[16,8,512]{2,1,0:T(8,128)}), f32[16,8,512]{2,1,0:T(8,128)S(1)}, u32[]{:S(2)}, u32[]{:S(2)}) async-start(f32[16,8,512]{2,1,0:T(8,128)} %bitcast.236), calls=%async_computation.8 | async-start | bytes 524288 | tf_op jit(solution)/shard_map/all_to_all | solution.py:44
  147.6 6.9 %all-to-all-done.8 = f32[16,8,512]{2,1,0:T(8,128)S(1)} async-done(((f32[16,8,512]{2,1,0:T(8,128)}), f32[16,8,512]{2,1,0:T(8,128)S(1)}, u32[]{:S(2)}, u32[]{:S(2)}) %all-to-all-start.8) | async-done | bytes 262176 | tf_op jit(solution)/shard_map/all_to_all | solution.py:44
  155.7 6.3 %all-to-all-start.9 = ((f32[256,1,128]{2,1,0:T(1,128)}), f32[256,1,128]{2,1,0:T(1,128)S(1)}, u32[]{:S(2)}, u32[]{:S(2)}) async-start(f32[256,1,128]{2,1,0:T(1,128)} %broadcast_in_dim.45), calls=%async_computation.9 | async-start | bytes 262144 | tf_op jit(solution)/shard_map/all_to_all | solution.py:55
  162.4 12.2 %all-to-all-done.9 = f32[256,1,128]{2,1,0:T(1,128)S(1)} async-done(((f32[256,1,128]{2,1,0:T(1,128)}), f32[256,1,128]{2,1,0:T(1,128)S(1)}, u32[]{:S(2)}, u32[]{:S(2)}) %all-to-all-start.9) | async-done | bytes 131104 | tf_op jit(solution)/shard_map/all_to_all | solution.py:55
  179.8 4.4 %all-to-all-start.10 = ((bf16[16,8,512]{2,1,0:T(8,128)(2,1)}), bf16[16,8,512]{2,1,0:T(8,128)(2,1)S(1)}, u32[]{:S(2)}, u32[]{:S(2)}) async-start(bf16[16,8,512]{2,1,0:T(8,128)(2,1)} %broadcast_in_dim.46), calls=%async_computation.10 | async-start | bytes 262144 | tf_op jit(solution)/shard_map/all_to_all | solution.py:39
  184.5 5.9 %all-to-all-done.10 = bf16[16,8,512]{2,1,0:T(8,128)(2,1)S(1)} async-done(((bf16[16,8,512]{2,1,0:T(8,128)(2,1)}), bf16[16,8,512]{2,1,0:T(8,128)(2,1)S(1)}, u32[]{:S(2)}, u32[]{:S(2)}) %all-to-all-start.10) | async-done | bytes 131104 | tf_op jit(solution)/shard_map/all_to_all | solution.py:39
  190.4 3.5 %all-to-all-start.11 = ((bf16[16,8,512]{2,1,0:T(8,128)(2,1)}), bf16[16,8,512]{2,1,0:T(8,128)(2,1)S(1)}, u32[]{:S(2)}, u32[]{:S(2)}) async-start(bf16[16,8,512]{2,1,0:T(8,128)(2,1)} %broadcast_in_dim.46), calls=%async_computation.11 | async-start | bytes 262144 | tf_op jit(solution)/shard_map/all_to_all | solution.py:39
  194.6 4.5 %fusion.39 = f32[8,128,128,1]{2,0,1,3:T(8,128)S(1)} fusion(bf16[1,1,128,128,128]{4,3,2,1,0:T(8,128)(2,1)} %param.11, bf16[128,8,128]{2,1,0:T(8,128)(2,1)S(1)} %gather_fusion.7, f32[128]{0:T(128)S(1)} %compare_convert_fusion, pred[128]{0:T(512)(128)(4,1)S(1)} %get-tuple-element.37), kind=kOutput, calls=%fused_computation.30 | convolution fusion | flops 33816576 | bytes 4981376 | tf_op jit(solution)/shard_map/sut,cst->csu/dot_general | solution.py:74
  199.5 0.8 copy.163
  200.3 2.6 all-to-all-done.11
  202.9 6.5 %all-to-all-start.12 = ((f32[16,8,512]{2,1,0:T(8,128)}), f32[16,8,512]{2,1,0:T(8,128)S(1)}, u32[]{:S(2)}, u32[]{:S(2)}) async-start(f32[16,8,512]{2,1,0:T(8,128)} %bitcast.235), calls=%async_computation.12 | async-start | bytes 524288 | tf_op jit(solution)/shard_map/all_to_all | solution.py:44
  210.0 3.4 %fusion.45 = f32[8,128,128,1]{2,0,1,3:T(8,128)S(1)} fusion(bf16[1,1,128,128,128]{4,3,2,1,0:T(8,128)(2,1)} %param.11, bf16[128,8,128]{2,1,0:T(8,128)(2,1)S(1)} %gather_fusion.8, f32[128]{0:T(128)S(1)} %compare_select_fusion.1, pred[128]{0:T(512)(128)(4,1)S(1)} %get-tuple-element.29), kind=kOutput, calls=%fused_computation.32 | convolution fusion | flops 33816576 | bytes 4981376 | tf_op jit(solution)/shard_map/sut,csu->cst/dot_general | solution.py:86
  213.8 0.9 copy.162
  214.7 4.2 %all-to-all-done.12 = f32[16,8,512]{2,1,0:T(8,128)S(1)} async-done(((f32[16,8,512]{2,1,0:T(8,128)}), f32[16,8,512]{2,1,0:T(8,128)S(1)}, u32[]{:S(2)}, u32[]{:S(2)}) %all-to-all-start.12) | async-done | bytes 262176 | tf_op jit(solution)/shard_map/all_to_all | solution.py:44
  219.0 6.2 %all-to-all-start.13 = ((f32[16,8,512]{2,1,0:T(8,128)}), f32[16,8,512]{2,1,0:T(8,128)S(1)}, u32[]{:S(2)}, u32[]{:S(2)}) async-start(f32[16,8,512]{2,1,0:T(8,128)} %bitcast.234), calls=%async_computation.13 | async-start | bytes 524288 | tf_op jit(solution)/shard_map/all_to_all | solution.py:44
  225.6 6.9 %all-to-all-done.13 = f32[16,8,512]{2,1,0:T(8,128)S(1)} async-done(((f32[16,8,512]{2,1,0:T(8,128)}), f32[16,8,512]{2,1,0:T(8,128)S(1)}, u32[]{:S(2)}, u32[]{:S(2)}) %all-to-all-start.13) | async-done | bytes 262176 | tf_op jit(solution)/shard_map/all_to_all | solution.py:44
  233.0 18.8 %all_to_all.78 = f32[256,1,128]{2,1,0:T(1,128)S(1)} all-to-all(f32[256,1,128]{2,1,0:T(1,128)S(1)} %broadcast_in_dim.47), channel_id=1, replica_groups=mesh['row'=16,'col'=16] {'row','col'}, dimensions={0} | all-to-all | bytes 262144 | tf_op jit(solution)/shard_map/all_to_all | solution.py:55
  255.5 0.8 fusion.190
  256.4 0.7 fusion.192
  (132 shorter events, 26.4 us)
Async XLA Ops:
  2.8 14.0 %all-to-all-start = ((bf16[16,9,512]{2,1,0:T(8,128)(2,1)}), bf16[16,9,512]{2,1,0:T(8,128)(2,1)S(1)}, u32[]{:S(2)}, u32[]{:S(2)}) async-start(bf16[16,9,512]{2,1,0:T(8,128)(2,1)} %broadcast_in_dim.38), calls=%async_computation | async-start | bytes 524288 | tf_op jit(solution)/shard_map/all_to_all | solution.py:39
  16.8 20.0 %all-to-all-start.1 = ((bf16[16,9,512]{2,1,0:T(8,128)(2,1)}), bf16[16,9,512]{2,1,0:T(8,128)(2,1)S(1)}, u32[]{:S(2)}, u32[]{:S(2)}) async-start(bf16[16,9,512]{2,1,0:T(8,128)(2,1)} %broadcast_in_dim.38), calls=%async_computation.1 | async-start | bytes 524288 | tf_op jit(solution)/shard_map/all_to_all | solution.py:39
  28.5 15.9 %copy-start.2 = (s32[1,1,2,128]{3,2,1,0:T(2,128)S(1)}, s32[1,1,2,128]{3,2,1,0:T(2,128)}, u32[]{:S(2)}) copy-start(s32[1,1,2,128]{3,2,1,0:T(2,128)} %param.12) | copy-start | bytes 3076
  38.1 20.4 %all-to-all-start.2 = ((f32[16,9,512]{2,1,0:T(8,128)}), f32[16,9,512]{2,1,0:T(8,128)S(1)}, u32[]{:S(2)}, u32[]{:S(2)}) async-start(f32[16,9,512]{2,1,0:T(8,128)} %copy.97), calls=%async_computation.2 | async-start | bytes 1048576 | tf_op jit(solution)/shard_map/all_to_all | solution.py:44
  45.3 21.5 %copy-start = (f32[8,512]{1,0:T(8,128)S(1)}, f32[8,512]{1,0:T(8,128)}, u32[]{:S(2)}) copy-start(f32[8,512]{1,0:T(8,128)} %param.15) | copy-start | bytes 49156
  45.3 38.8 %copy-start.1 = (f32[2,8,24]{2,1,0:T(8,128)S(1)}, f32[2,8,24]{2,1,0:T(8,128)}, u32[]{:S(2)}) copy-start(f32[2,8,24]{2,1,0:T(8,128)} %param.16) | copy-start | bytes 4612
  59.5 17.1 %all-to-all-start.3 = ((f32[16,9,512]{2,1,0:T(8,128)}), f32[16,9,512]{2,1,0:T(8,128)S(1)}, u32[]{:S(2)}, u32[]{:S(2)}) async-start(f32[16,9,512]{2,1,0:T(8,128)} %copy.101), calls=%async_computation.3 | async-start | bytes 1048576 | tf_op jit(solution)/shard_map/all_to_all | solution.py:44
  77.7 18.9 %all-to-all-start.4 = ((f32[256,1,128]{2,1,0:T(1,128)}), f32[256,1,128]{2,1,0:T(1,128)S(1)}, u32[]{:S(2)}, u32[]{:S(2)}) async-start(f32[256,1,128]{2,1,0:T(1,128)} %broadcast_in_dim.39), calls=%async_computation.4 | async-start | bytes 262144 | tf_op jit(solution)/shard_map/all_to_all | solution.py:55
  101.8 10.6 %all-to-all-start.5 = ((bf16[16,8,512]{2,1,0:T(8,128)(2,1)}), bf16[16,8,512]{2,1,0:T(8,128)(2,1)S(1)}, u32[]{:S(2)}, u32[]{:S(2)}) async-start(bf16[16,8,512]{2,1,0:T(8,128)(2,1)} %broadcast_in_dim.41), calls=%async_computation.5 | async-start | bytes 262144 | tf_op jit(solution)/shard_map/all_to_all | solution.py:39
  112.4 12.5 %all-to-all-start.6 = ((bf16[16,8,512]{2,1,0:T(8,128)(2,1)}), bf16[16,8,512]{2,1,0:T(8,128)(2,1)S(1)}, u32[]{:S(2)}, u32[]{:S(2)}) async-start(bf16[16,8,512]{2,1,0:T(8,128)(2,1)} %broadcast_in_dim.41), calls=%async_computation.6 | async-start | bytes 262144 | tf_op jit(solution)/shard_map/all_to_all | solution.py:39
  124.9 16.1 %all-to-all-start.7 = ((f32[16,8,512]{2,1,0:T(8,128)}), f32[16,8,512]{2,1,0:T(8,128)S(1)}, u32[]{:S(2)}, u32[]{:S(2)}) async-start(f32[16,8,512]{2,1,0:T(8,128)} %bitcast.237), calls=%async_computation.7 | async-start | bytes 524288 | tf_op jit(solution)/shard_map/all_to_all | solution.py:44
  141.0 13.5 %all-to-all-start.8 = ((f32[16,8,512]{2,1,0:T(8,128)}), f32[16,8,512]{2,1,0:T(8,128)S(1)}, u32[]{:S(2)}, u32[]{:S(2)}) async-start(f32[16,8,512]{2,1,0:T(8,128)} %bitcast.236), calls=%async_computation.8 | async-start | bytes 524288 | tf_op jit(solution)/shard_map/all_to_all | solution.py:44
  155.7 18.9 %all-to-all-start.9 = ((f32[256,1,128]{2,1,0:T(1,128)}), f32[256,1,128]{2,1,0:T(1,128)S(1)}, u32[]{:S(2)}, u32[]{:S(2)}) async-start(f32[256,1,128]{2,1,0:T(1,128)} %broadcast_in_dim.45), calls=%async_computation.9 | async-start | bytes 262144 | tf_op jit(solution)/shard_map/all_to_all | solution.py:55
  179.8 10.6 %all-to-all-start.10 = ((bf16[16,8,512]{2,1,0:T(8,128)(2,1)}), bf16[16,8,512]{2,1,0:T(8,128)(2,1)S(1)}, u32[]{:S(2)}, u32[]{:S(2)}) async-start(bf16[16,8,512]{2,1,0:T(8,128)(2,1)} %broadcast_in_dim.46), calls=%async_computation.10 | async-start | bytes 262144 | tf_op jit(solution)/shard_map/all_to_all | solution.py:39
  190.4 12.5 %all-to-all-start.11 = ((bf16[16,8,512]{2,1,0:T(8,128)(2,1)}), bf16[16,8,512]{2,1,0:T(8,128)(2,1)S(1)}, u32[]{:S(2)}, u32[]{:S(2)}) async-start(bf16[16,8,512]{2,1,0:T(8,128)(2,1)} %broadcast_in_dim.46), calls=%async_computation.11 | async-start | bytes 262144 | tf_op jit(solution)/shard_map/all_to_all | solution.py:39
  202.9 16.1 %all-to-all-start.12 = ((f32[16,8,512]{2,1,0:T(8,128)}), f32[16,8,512]{2,1,0:T(8,128)S(1)}, u32[]{:S(2)}, u32[]{:S(2)}) async-start(f32[16,8,512]{2,1,0:T(8,128)} %bitcast.235), calls=%async_computation.12 | async-start | bytes 524288 | tf_op jit(solution)/shard_map/all_to_all | solution.py:44
  219.0 13.5 %all-to-all-start.13 = ((f32[16,8,512]{2,1,0:T(8,128)}), f32[16,8,512]{2,1,0:T(8,128)S(1)}, u32[]{:S(2)}, u32[]{:S(2)}) async-start(f32[16,8,512]{2,1,0:T(8,128)} %bitcast.234), calls=%async_computation.13 | async-start | bytes 524288 | tf_op jit(solution)/shard_map/all_to_all | solution.py:44

commit v5 on v4

--- a/solution.py
+++ b/solution.py
@@ -124,14 +124,16 @@
         rows_total = direct_terms(
             flat_tiles, block_rows, block_cols, live, col_blocks, row_span, col_count
         )
-        row_side = gather_by_exchange(short, "col")
-        rows_total, row_side = lax.optimization_barrier((rows_total, row_side))
+        copies = jnp.broadcast_to(short.astype(jnp.float32)[None], (col_count,) + short.shape)
+        held = lax.all_to_all(
+            jnp.concatenate([rows_total, copies], axis=1), "col", 0, 0, tiled=True
+        )
+        direct_part = jnp.sum(held[:, :width], axis=0)
+        row_side = jnp.swapaxes(held[:, width:].astype(jnp.bfloat16), 0, 1)
         row_blocks = row_side.reshape(width, row_span, tile_side)
         cols_total = mirror_terms(
             flat_tiles, block_rows, block_cols, mirror_weight, row_blocks, col_span, row_count
         )
-        direct_part = scatter_sum_by_exchange(rows_total, "col")
-        direct_part, cols_total = lax.optimization_barrier((direct_part, cols_total))
         mirror_part = scatter_sum_by_exchange(cols_total, "row")
         return direct_part + mirror_part
 

time: 259 us -> 261 us (level)
  starting transfers between devices: 84.8 us -> 53.6 us
  blocking collectives: 18.8 us -> 47.5 us
  waiting for transfers between devices: 91.1 us -> 97.2 us
    all_to_all x0 -> x3, waiting for transfers between devices: none -> 49.8 us  [graph_product(): lax.all_to_all(jnp.concatenate([rows_total, copies], axis=1), 'col', 0, 0...]
    all_to_all x6 -> x2, starting transfers between devices: 33.3 us -> 11.2 us  [gather_by_exchange(): held = lax.all_to_all(copies, axis, 0, 0, tiled=True)]
    all_to_all x6 -> x3, starting transfers between devices: 38.9 us -> 18.1 us  [scatter_sum_by_exchange(): held = lax.all_to_all(chunks, axis, 0, 0, tiled=True)]
    all_to_all x1 -> x2, blocking collectives: 18.8 us -> 37.8 us  [gram_sums(): held = lax.all_to_all(copies, ('row', 'col'), 0, 0, tiled=True)]
    all_to_all x0 -> x3, starting transfers between devices: none -> 17.9 us  [graph_product(): lax.all_to_all(jnp.concatenate([rows_total, copies], axis=1), 'col', 0, 0...]
    all_to_all x6 -> x3, waiting for transfers between devices: 41.1 us -> 23.7 us  [scatter_sum_by_exchange(): held = lax.all_to_all(chunks, axis, 0, 0, tiled=True)]
    all_to_all x6 -> x2, waiting for transfers between devices: 25.3 us -> 11.1 us  [gather_by_exchange(): held = lax.all_to_all(copies, axis, 0, 0, tiled=True)]
    all_to_all x2 -> x1, waiting for transfers between devices: 24.8 us -> 12.6 us  [gram_sums(): held = lax.all_to_all(copies, ('row', 'col'), 0, 0, tiled=True)]
  transfers between devices with their start and end apart: 14 -> 9, of which waited for: 14 -> 9; matrix products, arithmetic and copies ran while one was open for 15% -> 1% of each run, Pallas kernels for 0% -> 0%
where the time goes in v5:
time: 261 us; the launch traced here: 260 us
  waiting for transfers between devices  97.2 us (37%)
  starting transfers between devices  53.6 us (21%)
  blocking collectives  47.5 us (18%)
  matrix products  33.7 us (13%)
  local copies, waits for them, and re-layouts  15.4 us (6%)
  other arithmetic  10.9 us (4%)
    all_to_all x3, waiting for transfers between devices, graph_product(): lax.all_to_all(jnp.concatenate([rows_total, copies], axis=1), 'col', 0, 0...  49.8 us
    all_to_all x2, blocking collectives, gram_sums(): held = lax.all_to_all(copies, ('row', 'col'), 0, 0, tiled=True)  37.8 us
    all_to_all x3, waiting for transfers between devices, scatter_sum_by_exchange(): held = lax.all_to_all(chunks, axis, 0, 0, tiled=True)  23.7 us
    all_to_all x3, starting transfers between devices, scatter_sum_by_exchange(): held = lax.all_to_all(chunks, axis, 0, 0, tiled=True)  18.1 us
    all_to_all x3, starting transfers between devices, graph_product(): lax.all_to_all(jnp.concatenate([rows_total, copies], axis=1), 'col', 0, 0...  17.9 us
    dot_general x3, matrix products, direct_terms(): jnp.einsum('sut,cst->csu', part_tiles, col_values, preferred_element_type...  13.5 us
    all_to_all x1, waiting for transfers between devices, gram_sums(): held = lax.all_to_all(copies, ('row', 'col'), 0, 0, tiled=True)  12.6 us
    all_to_all x2, starting transfers between devices, gather_by_exchange(): held = lax.all_to_all(copies, axis, 0, 0, tiled=True)  11.2 us
  transfers between devices with their start and end apart: 9, of which 9 were waited for; matrix products, arithmetic and copies ran while one was open for 1% of the time, Pallas kernels for 0%

profile of v5, /device:TPU:1, one launch (start us, length us, event | category | flops | bytes accessed | tf_op | source)
XLA Modules:
  0.0 260.0 jit_solution(5019746063417171804)
XLA Ops:
  1.3 0.7 multiply_convert_fusion
  2.1 0.7 broadcast_in_dim.47
  2.8 6.8 %all-to-all-start = ((bf16[16,9,512]{2,1,0:T(8,128)(2,1)}), bf16[16,9,512]{2,1,0:T(8,128)(2,1)S(1)}, u32[]{:S(2)}, u32[]{:S(2)}) async-start(bf16[16,9,512]{2,1,0:T(8,128)(2,1)} %broadcast_in_dim.47), calls=%async_computation | async-start | bytes 524288 | tf_op jit(solution)/shard_map/all_to_all | solution.py:39
  9.6 0.8 compare_and_fusion
  10.4 0.8 slice_bitcast_fusion.2
  11.8 5.0 %all-to-all-done = bf16[16,9,512]{2,1,0:T(8,128)(2,1)S(1)} async-done(((bf16[16,9,512]{2,1,0:T(8,128)(2,1)}), bf16[16,9,512]{2,1,0:T(8,128)(2,1)S(1)}, u32[]{:S(2)}, u32[]{:S(2)}) %all-to-all-start) | async-done | bytes 147488 | tf_op jit(solution)/shard_map/all_to_all | solution.py:39
  17.1 0.7 gather_fusion.3
  17.8 4.5 %fusion.15 = f32[9,128,128,1]{2,0,1,3:T(8,128)S(1)} fusion(bf16[1,1,128,128,128]{4,3,2,1,0:T(8,128)(2,1)} %param.11, bf16[128,9,128]{2,1,0:T(8,128)(2,1)S(1)} %gather_fusion.3, f32[128]{0:T(128)S(1)} %compare_convert_fusion, pred[128]{0:T(512)(128)(4,1)S(1)} %get-tuple-element.15), kind=kOutput, calls=%fused_computation.22 | convolution fusion | flops 38043648 | bytes 5079680 | tf_op jit(solution)/shard_map/sut,cst->csu/dot_general | solution.py:74
  23.0 1.2 copy.90
  24.2 10.6 %all-to-all-start.1 = ((f32[16,18,512]{2,1,0:T(8,128)}), f32[16,18,512]{2,1,0:T(8,128)S(1)}, u32[]{:S(2)}, u32[]{:S(2)}) async-start(f32[16,18,512]{2,1,0:T(8,128)} %copy.90), calls=%async_computation.1 | async-start | bytes 1572864 | tf_op jit(solution)/shard_map/all_to_all | solution.py:128
  34.9 21.0 %all-to-all-done.1 = f32[16,18,512]{2,1,0:T(8,128)S(1)} async-done(((f32[16,18,512]{2,1,0:T(8,128)}), f32[16,18,512]{2,1,0:T(8,128)S(1)}, u32[]{:S(2)}, u32[]{:S(2)}) %all-to-all-start.1) | async-done | bytes 589856 | tf_op jit(solution)/shard_map/all_to_all | solution.py:128
  56.2 0.7 gather_fusion.4
  57.0 3.4 %fusion.21 = f32[9,128,128,1]{2,0,1,3:T(8,128)S(1)} fusion(bf16[1,1,128,128,128]{4,3,2,1,0:T(8,128)(2,1)} %param.11, bf16[128,9,128]{2,1,0:T(8,128)(2,1)S(1)} %gather_fusion.4, f32[128]{0:T(128)S(1)} %compare_select_fusion.1, pred[128]{0:T(512)(128)(4,1)S(1)} %get-tuple-element.4), kind=kOutput, calls=%fused_computation.24 | convolution fusion | flops 38043648 | bytes 5079680 | tf_op jit(solution)/shard_map/sut,csu->cst/dot_general | solution.py:86
  61.0 0.9 reshape.394
  62.0 6.0 %all-to-all-start.2 = ((f32[16,9,512]{2,1,0:T(8,128)}), f32[16,9,512]{2,1,0:T(8,128)S(1)}, u32[]{:S(2)}, u32[]{:S(2)}) async-start(f32[16,9,512]{2,1,0:T(8,128)} %reshape.394), calls=%async_computation.2 | async-start | bytes 1048576 | tf_op jit(solution)/shard_map/all_to_all | solution.py:44
  68.2 9.6 %all-to-all-done.2 = f32[16,9,512]{2,1,0:T(8,128)S(1)} async-done(((f32[16,9,512]{2,1,0:T(8,128)}), f32[16,9,512]{2,1,0:T(8,128)S(1)}, u32[]{:S(2)}, u32[]{:S(2)}) %all-to-all-start.2) | async-done | bytes 294944 | tf_op jit(solution)/shard_map/all_to_all | solution.py:44
  78.2 0.7 broadcast_in_dim.49
  78.9 6.3 %all-to-all-start.3 = ((f32[256,1,128]{2,1,0:T(1,128)}), f32[256,1,128]{2,1,0:T(1,128)S(1)}, u32[]{:S(2)}, u32[]{:S(2)}) async-start(f32[256,1,128]{2,1,0:T(1,128)} %broadcast_in_dim.49), calls=%async_computation.3 | async-start | bytes 262144 | tf_op jit(solution)/shard_map/all_to_all | solution.py:55
  85.3 12.6 %all-to-all-done.3 = f32[256,1,128]{2,1,0:T(1,128)S(1)} async-done(((f32[256,1,128]{2,1,0:T(1,128)}), f32[256,1,128]{2,1,0:T(1,128)S(1)}, u32[]{:S(2)}, u32[]{:S(2)}) %all-to-all-start.3) | async-done | bytes 131104 | tf_op jit(solution)/shard_map/all_to_all | solution.py:55
  98.2 0.7 cholesky.59
  102.4 9.7 %all_to_all.63 = bf16[16,8,512]{2,1,0:T(8,128)(2,1)S(1)} all-to-all(bf16[16,8,512]{2,1,0:T(8,128)(2,1)S(1)} %broadcast_in_dim.51), channel_id=1, replica_groups=mesh['row'=16,'col'=16] {'row'}, dimensions={0} | all-to-all | bytes 262144 | tf_op jit(solution)/shard_map/all_to_all | solution.py:39
  112.0 0.7 gather_fusion.5
  112.8 4.5 %fusion.27 = f32[8,128,128,1]{2,0,1,3:T(8,128)S(1)} fusion(bf16[1,1,128,128,128]{4,3,2,1,0:T(8,128)(2,1)} %param.11, bf16[128,8,128]{2,1,0:T(8,128)(2,1)S(1)} %gather_fusion.5, f32[128]{0:T(128)S(1)} %compare_convert_fusion, pred[128]{0:T(512)(128)(4,1)S(1)} %get-tuple-element.15), kind=kOutput, calls=%fused_computation.26 | convolution fusion | flops 33816576 | bytes 4981376 | tf_op jit(solution)/shard_map/sut,cst->csu/dot_general | solution.py:74
  117.8 0.8 pad_maximum_fusion.1
  118.7 3.8 %all-to-all-start.5 = ((f32[16,16,512]{2,1,0:T(8,128)}), f32[16,16,512]{2,1,0:T(8,128)S(1)}, u32[]{:S(2)}, u32[]{:S(2)}) async-start(f32[16,16,512]{2,1,0:T(8,128)} %pad_maximum_fusion.1), calls=%async_computation.5 | async-start | bytes 1048576 | tf_op jit(solution)/shard_map/all_to_all | solution.py:128
  122.7 14.6 %all-to-all-done.5 = f32[16,16,512]{2,1,0:T(8,128)S(1)} async-done(((f32[16,16,512]{2,1,0:T(8,128)}), f32[16,16,512]{2,1,0:T(8,128)S(1)}, u32[]{:S(2)}, u32[]{:S(2)}) %all-to-all-start.5) | async-done | bytes 524320 | tf_op jit(solution)/shard_map/all_to_all | solution.py:128
  137.4 0.7 gather_fusion.6
  138.1 3.4 %fusion.33 = f32[8,128,128,1]{2,0,1,3:T(8,128)S(1)} fusion(bf16[1,1,128,128,128]{4,3,2,1,0:T(8,128)(2,1)} %param.11, bf16[128,8,128]{2,1,0:T(8,128)(2,1)S(1)} %gather_fusion.6, f32[128]{0:T(128)S(1)} %compare_select_fusion.1, pred[128]{0:T(512)(128)(4,1)S(1)} %get-tuple-element.4), kind=kOutput, calls=%fused_computation.28 | convolution fusion | flops 33816576 | bytes 4981376 | tf_op jit(solution)/shard_map/sut,csu->cst/dot_general | solution.py:86
  141.9 0.8 copy.159
  142.7 6.1 %all-to-all-start.6 = ((f32[16,8,512]{2,1,0:T(8,128)}), f32[16,8,512]{2,1,0:T(8,128)S(1)}, u32[]{:S(2)}, u32[]{:S(2)}) async-start(f32[16,8,512]{2,1,0:T(8,128)} %bitcast.225), calls=%async_computation.6 | async-start | bytes 524288 | tf_op jit(solution)/shard_map/all_to_all | solution.py:44
  149.1 7.0 %all-to-all-done.6 = f32[16,8,512]{2,1,0:T(8,128)S(1)} async-done(((f32[16,8,512]{2,1,0:T(8,128)}), f32[16,8,512]{2,1,0:T(8,128)S(1)}, u32[]{:S(2)}, u32[]{:S(2)}) %all-to-all-start.6) | async-done | bytes 262176 | tf_op jit(solution)/shard_map/all_to_all | solution.py:44
  156.6 18.9 %all_to_all.64 = f32[256,1,128]{2,1,0:T(1,128)S(1)} all-to-all(f32[256,1,128]{2,1,0:T(1,128)S(1)} %broadcast_in_dim.53), channel_id=1, replica_groups=mesh['row'=16,'col'=16] {'row','col'}, dimensions={0} | all-to-all | bytes 262144 | tf_op jit(solution)/shard_map/all_to_all | solution.py:55
  175.8 0.7 cholesky.70
  180.6 4.4 %all-to-all-start.8 = ((bf16[16,8,512]{2,1,0:T(8,128)(2,1)}), bf16[16,8,512]{2,1,0:T(8,128)(2,1)S(1)}, u32[]{:S(2)}, u32[]{:S(2)}) async-start(bf16[16,8,512]{2,1,0:T(8,128)(2,1)} %broadcast_in_dim.54), calls=%async_computation.8 | async-start | bytes 262144 | tf_op jit(solution)/shard_map/all_to_all | solution.py:39
  185.0 6.2 %all-to-all-done.8 = bf16[16,8,512]{2,1,0:T(8,128)(2,1)S(1)} async-done(((bf16[16,8,512]{2,1,0:T(8,128)(2,1)}), bf16[16,8,512]{2,1,0:T(8,128)(2,1)S(1)}, u32[]{:S(2)}, u32[]{:S(2)}) %all-to-all-start.8) | async-done | bytes 131104 | tf_op jit(solution)/shard_map/all_to_all | solution.py:39
  191.9 4.5 %fusion.39 = f32[8,128,128,1]{2,0,1,3:T(8,128)S(1)} fusion(bf16[1,1,128,128,128]{4,3,2,1,0:T(8,128)(2,1)} %param.11, bf16[128,8,128]{2,1,0:T(8,128)(2,1)S(1)} %gather_fusion.7, f32[128]{0:T(128)S(1)} %compare_convert_fusion, pred[128]{0:T(512)(128)(4,1)S(1)} %get-tuple-element.15), kind=kOutput, calls=%fused_computation.30 | convolution fusion | flops 33816576 | bytes 4981376 | tf_op jit(solution)/shard_map/sut,cst->csu/dot_general | solution.py:74
  197.0 0.8 pad_maximum_fusion.2
  197.8 3.6 %all-to-all-start.9 = ((f32[16,16,512]{2,1,0:T(8,128)}), f32[16,16,512]{2,1,0:T(8,128)S(1)}, u32[]{:S(2)}, u32[]{:S(2)}) async-start(f32[16,16,512]{2,1,0:T(8,128)} %pad_maximum_fusion.2), calls=%async_computation.9 | async-start | bytes 1048576 | tf_op jit(solution)/shard_map/all_to_all | solution.py:128
  202.3 14.2 %all-to-all-done.9 = f32[16,16,512]{2,1,0:T(8,128)S(1)} async-done(((f32[16,16,512]{2,1,0:T(8,128)}), f32[16,16,512]{2,1,0:T(8,128)S(1)}, u32[]{:S(2)}, u32[]{:S(2)}) %all-to-all-start.9) | async-done | bytes 524320 | tf_op jit(solution)/shard_map/all_to_all | solution.py:128
  216.6 0.7 gather_fusion.8
  217.2 3.4 %fusion.45 = f32[8,128,128,1]{2,0,1,3:T(8,128)S(1)} fusion(bf16[1,1,128,128,128]{4,3,2,1,0:T(8,128)(2,1)} %param.11, bf16[128,8,128]{2,1,0:T(8,128)(2,1)S(1)} %gather_fusion.8, f32[128]{0:T(128)S(1)} %compare_select_fusion.1, pred[128]{0:T(512)(128)(4,1)S(1)} %get-tuple-element.4), kind=kOutput, calls=%fused_computation.32 | convolution fusion | flops 33816576 | bytes 4981376 | tf_op jit(solution)/shard_map/sut,csu->cst/dot_general | solution.py:86
  221.1 0.8 copy.157
  221.9 6.0 %all-to-all-start.10 = ((f32[16,8,512]{2,1,0:T(8,128)}), f32[16,8,512]{2,1,0:T(8,128)S(1)}, u32[]{:S(2)}, u32[]{:S(2)}) async-start(f32[16,8,512]{2,1,0:T(8,128)} %bitcast.223), calls=%async_computation.10 | async-start | bytes 524288 | tf_op jit(solution)/shard_map/all_to_all | solution.py:44
  228.1 7.1 %all-to-all-done.10 = f32[16,8,512]{2,1,0:T(8,128)S(1)} async-done(((f32[16,8,512]{2,1,0:T(8,128)}), f32[16,8,512]{2,1,0:T(8,128)S(1)}, u32[]{:S(2)}, u32[]{:S(2)}) %all-to-all-start.10) | async-done | bytes 262176 | tf_op jit(solution)/shard_map/all_to_all | solution.py:44
  235.7 18.9 %all_to_all.65 = f32[256,1,128]{2,1,0:T(1,128)S(1)} all-to-all(f32[256,1,128]{2,1,0:T(1,128)S(1)} %broadcast_in_dim.56), channel_id=1, replica_groups=mesh['row'=16,'col'=16] {'row','col'}, dimensions={0} | all-to-all | bytes 262144 | tf_op jit(solution)/shard_map/all_to_all | solution.py:55
  254.9 0.7 cholesky.81
  258.3 0.8 fusion.192
  259.3 0.7 fusion.194
  (130 shorter events, 20.0 us)
Async XLA Ops:
  2.8 14.0 %all-to-all-start = ((bf16[16,9,512]{2,1,0:T(8,128)(2,1)}), bf16[16,9,512]{2,1,0:T(8,128)(2,1)S(1)}, u32[]{:S(2)}, u32[]{:S(2)}) async-start(bf16[16,9,512]{2,1,0:T(8,128)(2,1)} %broadcast_in_dim.47), calls=%async_computation | async-start | bytes 524288 | tf_op jit(solution)/shard_map/all_to_all | solution.py:39
  22.3 12.5 %copy-start.2 = (s32[1,1,2,128]{3,2,1,0:T(2,128)S(1)}, s32[1,1,2,128]{3,2,1,0:T(2,128)}, u32[]{:S(2)}) copy-start(s32[1,1,2,128]{3,2,1,0:T(2,128)} %param.12) | copy-start | bytes 3076
  24.2 31.6 %all-to-all-start.1 = ((f32[16,18,512]{2,1,0:T(8,128)}), f32[16,18,512]{2,1,0:T(8,128)S(1)}, u32[]{:S(2)}, u32[]{:S(2)}) async-start(f32[16,18,512]{2,1,0:T(8,128)} %copy.90), calls=%async_computation.1 | async-start | bytes 1572864 | tf_op jit(solution)/shard_map/all_to_all | solution.py:128
  56.9 11.0 %copy-start = (f32[8,512]{1,0:T(8,128)S(1)}, f32[8,512]{1,0:T(8,128)}, u32[]{:S(2)}) copy-start(f32[8,512]{1,0:T(8,128)} %param.15) | copy-start | bytes 49156
  62.0 15.9 %all-to-all-start.2 = ((f32[16,9,512]{2,1,0:T(8,128)}), f32[16,9,512]{2,1,0:T(8,128)S(1)}, u32[]{:S(2)}, u32[]{:S(2)}) async-start(f32[16,9,512]{2,1,0:T(8,128)} %reshape.394), calls=%async_computation.2 | async-start | bytes 1048576 | tf_op jit(solution)/shard_map/all_to_all | solution.py:44
  78.9 18.9 %all-to-all-start.3 = ((f32[256,1,128]{2,1,0:T(1,128)}), f32[256,1,128]{2,1,0:T(1,128)S(1)}, u32[]{:S(2)}, u32[]{:S(2)}) async-start(f32[256,1,128]{2,1,0:T(1,128)} %broadcast_in_dim.49), calls=%async_computation.3 | async-start | bytes 262144 | tf_op jit(solution)/shard_map/all_to_all | solution.py:55
  112.7 9.8 %copy-start.1 = (f32[2,8,24]{2,1,0:T(8,128)S(1)}, f32[2,8,24]{2,1,0:T(8,128)}, u32[]{:S(2)}) copy-start(f32[2,8,24]{2,1,0:T(8,128)} %param.16) | copy-start | bytes 4612
  118.7 18.7 %all-to-all-start.5 = ((f32[16,16,512]{2,1,0:T(8,128)}), f32[16,16,512]{2,1,0:T(8,128)S(1)}, u32[]{:S(2)}, u32[]{:S(2)}) async-start(f32[16,16,512]{2,1,0:T(8,128)} %pad_maximum_fusion.1), calls=%async_computation.5 | async-start | bytes 1048576 | tf_op jit(solution)/shard_map/all_to_all | solution.py:128
  142.7 13.3 %all-to-all-start.6 = ((f32[16,8,512]{2,1,0:T(8,128)}), f32[16,8,512]{2,1,0:T(8,128)S(1)}, u32[]{:S(2)}, u32[]{:S(2)}) async-start(f32[16,8,512]{2,1,0:T(8,128)} %bitcast.225), calls=%async_computation.6 | async-start | bytes 524288 | tf_op jit(solution)/shard_map/all_to_all | solution.py:44
  180.6 10.6 %all-to-all-start.8 = ((bf16[16,8,512]{2,1,0:T(8,128)(2,1)}), bf16[16,8,512]{2,1,0:T(8,128)(2,1)S(1)}, u32[]{:S(2)}, u32[]{:S(2)}) async-start(bf16[16,8,512]{2,1,0:T(8,128)(2,1)} %broadcast_in_dim.54), calls=%async_computation.8 | async-start | bytes 262144 | tf_op jit(solution)/shard_map/all_to_all | solution.py:39
  197.8 18.7 %all-to-all-start.9 = ((f32[16,16,512]{2,1,0:T(8,128)}), f32[16,16,512]{2,1,0:T(8,128)S(1)}, u32[]{:S(2)}, u32[]{:S(2)}) async-start(f32[16,16,512]{2,1,0:T(8,128)} %pad_maximum_fusion.2), calls=%async_computation.9 | async-start | bytes 1048576 | tf_op jit(solution)/shard_map/all_to_all | solution.py:128
  221.9 13.2 %all-to-all-start.10 = ((f32[16,8,512]{2,1,0:T(8,128)}), f32[16,8,512]{2,1,0:T(8,128)S(1)}, u32[]{:S(2)}, u32[]{:S(2)}) async-start(f32[16,8,512]{2,1,0:T(8,128)} %bitcast.223), calls=%async_computation.10 | async-start | bytes 524288 | tf_op jit(solution)/shard_map/all_to_all | solution.py:44

commit v6 on v4

--- a/solution.py
+++ b/solution.py
@@ -45,15 +45,18 @@
     return jnp.sum(held, axis=0)
 
 
+def sum_by_exchange(local, axis):
+    count = lax.axis_size(axis)
+    copies = jnp.broadcast_to(local[None], (count,) + local.shape)
+    return jnp.sum(lax.all_to_all(copies, axis, 0, 0, tiled=True), axis=0)
+
+
 def gram_sums(new_vecs, new_images):
     order = new_vecs.shape[0]
     local = jnp.concatenate(
         [matmul_high(new_vecs, new_vecs.T).reshape(-1), matmul_high(new_images, new_vecs.T).reshape(-1)]
     )
-    count = lax.axis_size("row") * lax.axis_size("col")
-    copies = jnp.broadcast_to(local[None], (count,) + local.shape)
-    held = lax.all_to_all(copies, ("row", "col"), 0, 0, tiled=True)
-    total = jnp.sum(held, axis=0)
+    total = sum_by_exchange(sum_by_exchange(local, "row"), "col")
     return total[: order * order].reshape(order, order), total[order * order :].reshape(order, order)
 
 

time: 259 us -> 273 us (1.054)
  starting transfers between devices: 84.8 us -> 91.5 us
  waiting for transfers between devices: 91.1 us -> 94.3 us
  blocking collectives: 18.8 us -> 21.7 us
    all_to_all x2 -> x4, starting transfers between devices: 12.6 us -> 17.3 us  [sum_by_exchange(): return jnp.sum(lax.all_to_all(copies, axis, 0, 0, tiled=True), axis=0)]
    all_to_all x2 -> x4, waiting for transfers between devices: 24.8 us -> 28 us  [sum_by_exchange(): return jnp.sum(lax.all_to_all(copies, axis, 0, 0, tiled=True), axis=0)]
    all_to_all x1 -> x2, blocking collectives: 18.8 us -> 21.7 us  [sum_by_exchange(): return jnp.sum(lax.all_to_all(copies, axis, 0, 0, tiled=True), axis=0)]
  transfers between devices with their start and end apart: 14 -> 16, of which waited for: 14 -> 16; matrix products, arithmetic and copies ran while one was open for 15% -> 14% of each run, Pallas kernels for 0% -> 0%
where the time goes in v6:
time: 273 us; the launch traced here: 271 us
  waiting for transfers between devices  94.3 us (35%)
  starting transfers between devices  91.5 us (34%)
  matrix products  33.7 us (12%)
  blocking collectives  21.7 us (8%)
  local copies, waits for them, and re-layouts  18.8 us (7%)
  other arithmetic  9.15 us (3%)
    all_to_all x6, waiting for transfers between devices, scatter_sum_by_exchange(): held = lax.all_to_all(chunks, axis, 0, 0, tiled=True)  41.1 us
    all_to_all x6, starting transfers between devices, scatter_sum_by_exchange(): held = lax.all_to_all(chunks, axis, 0, 0, tiled=True)  38.9 us
    all_to_all x6, starting transfers between devices, gather_by_exchange(): held = lax.all_to_all(copies, axis, 0, 0, tiled=True)  35.3 us
    all_to_all x4, waiting for transfers between devices, sum_by_exchange(): return jnp.sum(lax.all_to_all(copies, axis, 0, 0, tiled=True), axis=0)  28 us
    all_to_all x6, waiting for transfers between devices, gather_by_exchange(): held = lax.all_to_all(copies, axis, 0, 0, tiled=True)  25.3 us
    all_to_all x2, blocking collectives, sum_by_exchange(): return jnp.sum(lax.all_to_all(copies, axis, 0, 0, tiled=True), axis=0)  21.7 us
    all_to_all x4, starting transfers between devices, sum_by_exchange(): return jnp.sum(lax.all_to_all(copies, axis, 0, 0, tiled=True), axis=0)  17.3 us
    dot_general x3, matrix products, direct_terms(): jnp.einsum('sut,cst->csu', part_tiles, col_values, preferred_element_type...  13.5 us
  transfers between devices with their start and end apart: 16, of which 16 were waited for; matrix products, arithmetic and copies ran while one was open for 14% of the time, Pallas kernels for 0%

profile of v6, /device:TPU:1, one launch (start us, length us, event | category | flops | bytes accessed | tf_op | source)
XLA Modules:
  0.0 270.8 jit_solution(4213548051264844712)
XLA Ops:
  2.8 6.8 %all-to-all-start = ((bf16[16,9,512]{2,1,0:T(8,128)(2,1)}), bf16[16,9,512]{2,1,0:T(8,128)(2,1)S(1)}, u32[]{:S(2)}, u32[]{:S(2)}) async-start(bf16[16,9,512]{2,1,0:T(8,128)(2,1)} %broadcast_in_dim.44), calls=%async_computation | async-start | bytes 524288 | tf_op jit(solution)/shard_map/all_to_all | solution.py:39
  9.6 0.8 compare_and_fusion
  11.8 5.0 %all-to-all-done = bf16[16,9,512]{2,1,0:T(8,128)(2,1)S(1)} async-done(((bf16[16,9,512]{2,1,0:T(8,128)(2,1)}), bf16[16,9,512]{2,1,0:T(8,128)(2,1)S(1)}, u32[]{:S(2)}, u32[]{:S(2)}) %all-to-all-start) | async-done | bytes 147488 | tf_op jit(solution)/shard_map/all_to_all | solution.py:39
  16.8 10.6 %all-to-all-start.1 = ((bf16[16,9,512]{2,1,0:T(8,128)(2,1)}), bf16[16,9,512]{2,1,0:T(8,128)(2,1)S(1)}, u32[]{:S(2)}, u32[]{:S(2)}) async-start(bf16[16,9,512]{2,1,0:T(8,128)(2,1)} %broadcast_in_dim.44), calls=%async_computation.1 | async-start | bytes 524288 | tf_op jit(solution)/shard_map/all_to_all | solution.py:39
  28.5 4.5 %fusion.15 = f32[9,128,128,1]{2,0,1,3:T(8,128)S(1)} fusion(bf16[1,1,128,128,128]{4,3,2,1,0:T(8,128)(2,1)} %param.11, bf16[128,9,128]{2,1,0:T(8,128)(2,1)S(1)} %gather_fusion.3, f32[128]{0:T(128)S(1)} %compare_convert_fusion, pred[128]{0:T(512)(128)(4,1)S(1)} %get-tuple-element.37), kind=kOutput, calls=%fused_computation.22 | convolution fusion | flops 38043648 | bytes 5079680 | tf_op jit(solution)/shard_map/sut,cst->csu/dot_general | solution.py:77
  33.5 3.3 %all-to-all-done.1 = bf16[16,9,512]{2,1,0:T(8,128)(2,1)S(1)} async-done(((bf16[16,9,512]{2,1,0:T(8,128)(2,1)}), bf16[16,9,512]{2,1,0:T(8,128)(2,1)S(1)}, u32[]{:S(2)}, u32[]{:S(2)}) %all-to-all-start.1) | async-done | bytes 147488 | tf_op jit(solution)/shard_map/all_to_all | solution.py:39
  37.1 1.0 copy.97
  38.1 6.2 %all-to-all-start.2 = ((f32[16,9,512]{2,1,0:T(8,128)}), f32[16,9,512]{2,1,0:T(8,128)S(1)}, u32[]{:S(2)}, u32[]{:S(2)}) async-start(f32[16,9,512]{2,1,0:T(8,128)} %copy.97), calls=%async_computation.2 | async-start | bytes 1048576 | tf_op jit(solution)/shard_map/all_to_all | solution.py:44
  45.3 3.5 %fusion.21 = f32[9,128,128,1]{2,0,1,3:T(8,128)S(1)} fusion(bf16[1,1,128,128,128]{4,3,2,1,0:T(8,128)(2,1)} %param.11, bf16[128,9,128]{2,1,0:T(8,128)(2,1)S(1)} %gather_fusion.4, f32[128]{0:T(128)S(1)} %compare_select_fusion.1, pred[128]{0:T(512)(128)(4,1)S(1)} %get-tuple-element.29), kind=kOutput, calls=%fused_computation.24 | convolution fusion | flops 38043648 | bytes 5079680 | tf_op jit(solution)/shard_map/sut,csu->cst/dot_general | solution.py:89
  49.3 9.2 %all-to-all-done.2 = f32[16,9,512]{2,1,0:T(8,128)S(1)} async-done(((f32[16,9,512]{2,1,0:T(8,128)}), f32[16,9,512]{2,1,0:T(8,128)S(1)}, u32[]{:S(2)}, u32[]{:S(2)}) %all-to-all-start.2) | async-done | bytes 294944 | tf_op jit(solution)/shard_map/all_to_all | solution.py:44
  58.5 1.0 copy.101
  59.5 7.2 %all-to-all-start.3 = ((f32[16,9,512]{2,1,0:T(8,128)}), f32[16,9,512]{2,1,0:T(8,128)S(1)}, u32[]{:S(2)}, u32[]{:S(2)}) async-start(f32[16,9,512]{2,1,0:T(8,128)} %copy.101), calls=%async_computation.3 | async-start | bytes 1048576 | tf_op jit(solution)/shard_map/all_to_all | solution.py:44
  67.0 9.7 %all-to-all-done.3 = f32[16,9,512]{2,1,0:T(8,128)S(1)} async-done(((f32[16,9,512]{2,1,0:T(8,128)}), f32[16,9,512]{2,1,0:T(8,128)S(1)}, u32[]{:S(2)}, u32[]{:S(2)}) %all-to-all-start.3) | async-done | bytes 294944 | tf_op jit(solution)/shard_map/all_to_all | solution.py:44
  77.6 4.3 %all-to-all-start.4 = ((f32[16,1,128]{2,1,0:T(1,128)}), f32[16,1,128]{2,1,0:T(1,128)S(1)}, u32[]{:S(2)}, u32[]{:S(2)}) async-start(f32[16,1,128]{2,1,0:T(1,128)} %broadcast_in_dim.45), calls=%async_computation.4 | async-start | bytes 16384 | tf_op jit(solution)/shard_map/all_to_all | solution.py:51
  82.0 5.5 %all-to-all-done.4 = f32[16,1,128]{2,1,0:T(1,128)S(1)} async-done(((f32[16,1,128]{2,1,0:T(1,128)}), f32[16,1,128]{2,1,0:T(1,128)S(1)}, u32[]{:S(2)}, u32[]{:S(2)}) %all-to-all-start.4) | async-done | bytes 8224 | tf_op jit(solution)/shard_map/all_to_all | solution.py:51
  88.1 4.5 %all-to-all-start.5 = ((f32[16,1,128]{2,1,0:T(1,128)}), f32[16,1,128]{2,1,0:T(1,128)S(1)}, u32[]{:S(2)}, u32[]{:S(2)}) async-start(f32[16,1,128]{2,1,0:T(1,128)} %broadcast_in_dim.49), calls=%async_computation.5 | async-start | bytes 16384 | tf_op jit(solution)/shard_map/all_to_all | solution.py:51
  92.6 8.7 %all-to-all-done.5 = f32[16,1,128]{2,1,0:T(1,128)S(1)} async-done(((f32[16,1,128]{2,1,0:T(1,128)}), f32[16,1,128]{2,1,0:T(1,128)S(1)}, u32[]{:S(2)}, u32[]{:S(2)}) %all-to-all-start.5) | async-done | bytes 8224 | tf_op jit(solution)/shard_map/all_to_all | solution.py:51
  106.4 5.4 %all-to-all-start.6 = ((bf16[16,8,512]{2,1,0:T(8,128)(2,1)}), bf16[16,8,512]{2,1,0:T(8,128)(2,1)S(1)}, u32[]{:S(2)}, u32[]{:S(2)}) async-start(bf16[16,8,512]{2,1,0:T(8,128)(2,1)} %broadcast_in_dim.51), calls=%async_computation.6 | async-start | bytes 262144 | tf_op jit(solution)/shard_map/all_to_all | solution.py:39
  111.9 6.0 %all-to-all-done.6 = bf16[16,8,512]{2,1,0:T(8,128)(2,1)S(1)} async-done(((bf16[16,8,512]{2,1,0:T(8,128)(2,1)}), bf16[16,8,512]{2,1,0:T(8,128)(2,1)S(1)}, u32[]{:S(2)}, u32[]{:S(2)}) %all-to-all-start.6) | async-done | bytes 131104 | tf_op jit(solution)/shard_map/all_to_all | solution.py:39
  117.9 3.5 %all-to-all-start.7 = ((bf16[16,8,512]{2,1,0:T(8,128)(2,1)}), bf16[16,8,512]{2,1,0:T(8,128)(2,1)S(1)}, u32[]{:S(2)}, u32[]{:S(2)}) async-start(bf16[16,8,512]{2,1,0:T(8,128)(2,1)} %broadcast_in_dim.51), calls=%async_computation.7 | async-start | bytes 262144 | tf_op jit(solution)/shard_map/all_to_all | solution.py:39
  122.1 4.5 %fusion.27 = f32[8,128,128,1]{2,0,1,3:T(8,128)S(1)} fusion(bf16[1,1,128,128,128]{4,3,2,1,0:T(8,128)(2,1)} %param.11, bf16[128,8,128]{2,1,0:T(8,128)(2,1)S(1)} %gather_fusion.5, f32[128]{0:T(128)S(1)} %compare_convert_fusion, pred[128]{0:T(512)(128)(4,1)S(1)} %get-tuple-element.37), kind=kOutput, calls=%fused_computation.26 | convolution fusion | flops 33816576 | bytes 4981376 | tf_op jit(solution)/shard_map/sut,cst->csu/dot_general | solution.py:77
  127.0 0.8 copy.168
  127.9 2.6 all-to-all-done.7
  130.4 6.5 %all-to-all-start.8 = ((f32[16,8,512]{2,1,0:T(8,128)}), f32[16,8,512]{2,1,0:T(8,128)S(1)}, u32[]{:S(2)}, u32[]{:S(2)}) async-start(f32[16,8,512]{2,1,0:T(8,128)} %bitcast.240), calls=%async_computation.8 | async-start | bytes 524288 | tf_op jit(solution)/shard_map/all_to_all | solution.py:44
  137.6 3.4 %fusion.33 = f32[8,128,128,1]{2,0,1,3:T(8,128)S(1)} fusion(bf16[1,1,128,128,128]{4,3,2,1,0:T(8,128)(2,1)} %param.11, bf16[128,8,128]{2,1,0:T(8,128)(2,1)S(1)} %gather_fusion.6, f32[128]{0:T(128)S(1)} %compare_select_fusion.1, pred[128]{0:T(512)(128)(4,1)S(1)} %get-tuple-element.29), kind=kOutput, calls=%fused_computation.28 | convolution fusion | flops 33816576 | bytes 4981376 | tf_op jit(solution)/shard_map/sut,csu->cst/dot_general | solution.py:89
  141.4 0.9 copy.167
  142.3 4.2 %all-to-all-done.8 = f32[16,8,512]{2,1,0:T(8,128)S(1)} async-done(((f32[16,8,512]{2,1,0:T(8,128)}), f32[16,8,512]{2,1,0:T(8,128)S(1)}, u32[]{:S(2)}, u32[]{:S(2)}) %all-to-all-start.8) | async-done | bytes 262176 | tf_op jit(solution)/shard_map/all_to_all | solution.py:44
  146.5 6.3 %all-to-all-start.9 = ((f32[16,8,512]{2,1,0:T(8,128)}), f32[16,8,512]{2,1,0:T(8,128)S(1)}, u32[]{:S(2)}, u32[]{:S(2)}) async-start(f32[16,8,512]{2,1,0:T(8,128)} %bitcast.239), calls=%async_computation.9 | async-start | bytes 524288 | tf_op jit(solution)/shard_map/all_to_all | solution.py:44
  153.2 6.9 %all-to-all-done.9 = f32[16,8,512]{2,1,0:T(8,128)S(1)} async-done(((f32[16,8,512]{2,1,0:T(8,128)}), f32[16,8,512]{2,1,0:T(8,128)S(1)}, u32[]{:S(2)}, u32[]{:S(2)}) %all-to-all-start.9) | async-done | bytes 262176 | tf_op jit(solution)/shard_map/all_to_all | solution.py:44
  161.1 4.3 %all-to-all-start.10 = ((f32[16,1,128]{2,1,0:T(1,128)}), f32[16,1,128]{2,1,0:T(1,128)S(1)}, u32[]{:S(2)}, u32[]{:S(2)}) async-start(f32[16,1,128]{2,1,0:T(1,128)} %broadcast_in_dim.52), calls=%async_computation.10 | async-start | bytes 16384 | tf_op jit(solution)/shard_map/all_to_all | solution.py:51
  165.6 5.3 %all-to-all-done.10 = f32[16,1,128]{2,1,0:T(1,128)S(1)} async-done(((f32[16,1,128]{2,1,0:T(1,128)}), f32[16,1,128]{2,1,0:T(1,128)S(1)}, u32[]{:S(2)}, u32[]{:S(2)}) %all-to-all-start.10) | async-done | bytes 8224 | tf_op jit(solution)/shard_map/all_to_all | solution.py:51
  171.5 4.3 %all-to-all-start.11 = ((f32[16,1,128]{2,1,0:T(1,128)}), f32[16,1,128]{2,1,0:T(1,128)S(1)}, u32[]{:S(2)}, u32[]{:S(2)}) async-start(f32[16,1,128]{2,1,0:T(1,128)} %broadcast_in_dim.53), calls=%async_computation.11 | async-start | bytes 16384 | tf_op jit(solution)/shard_map/all_to_all | solution.py:51
  176.0 8.5 %all-to-all-done.11 = f32[16,1,128]{2,1,0:T(1,128)S(1)} async-done(((f32[16,1,128]{2,1,0:T(1,128)}), f32[16,1,128]{2,1,0:T(1,128)S(1)}, u32[]{:S(2)}, u32[]{:S(2)}) %all-to-all-start.11) | async-done | bytes 8224 | tf_op jit(solution)/shard_map/all_to_all | solution.py:51
  189.6 5.4 %all-to-all-start.12 = ((bf16[16,8,512]{2,1,0:T(8,128)(2,1)}), bf16[16,8,512]{2,1,0:T(8,128)(2,1)S(1)}, u32[]{:S(2)}, u32[]{:S(2)}) async-start(bf16[16,8,512]{2,1,0:T(8,128)(2,1)} %broadcast_in_dim.54), calls=%async_computation.12 | async-start | bytes 262144 | tf_op jit(solution)/shard_map/all_to_all | solution.py:39
  195.3 5.9 %all-to-all-done.12 = bf16[16,8,512]{2,1,0:T(8,128)(2,1)S(1)} async-done(((bf16[16,8,512]{2,1,0:T(8,128)(2,1)}), bf16[16,8,512]{2,1,0:T(8,128)(2,1)S(1)}, u32[]{:S(2)}, u32[]{:S(2)}) %all-to-all-start.12) | async-done | bytes 131104 | tf_op jit(solution)/shard_map/all_to_all | solution.py:39
  201.2 3.5 %all-to-all-start.13 = ((bf16[16,8,512]{2,1,0:T(8,128)(2,1)}), bf16[16,8,512]{2,1,0:T(8,128)(2,1)S(1)}, u32[]{:S(2)}, u32[]{:S(2)}) async-start(bf16[16,8,512]{2,1,0:T(8,128)(2,1)} %broadcast_in_dim.54), calls=%async_computation.13 | async-start | bytes 262144 | tf_op jit(solution)/shard_map/all_to_all | solution.py:39
  205.4 4.5 %fusion.39 = f32[8,128,128,1]{2,0,1,3:T(8,128)S(1)} fusion(bf16[1,1,128,128,128]{4,3,2,1,0:T(8,128)(2,1)} %param.11, bf16[128,8,128]{2,1,0:T(8,128)(2,1)S(1)} %gather_fusion.7, f32[128]{0:T(128)S(1)} %compare_convert_fusion, pred[128]{0:T(512)(128)(4,1)S(1)} %get-tuple-element.37), kind=kOutput, calls=%fused_computation.30 | convolution fusion | flops 33816576 | bytes 4981376 | tf_op jit(solution)/shard_map/sut,cst->csu/dot_general | solution.py:77
  210.3 0.8 copy.166
  211.1 2.6 all-to-all-done.13
  213.7 6.5 %all-to-all-start.14 = ((f32[16,8,512]{2,1,0:T(8,128)}), f32[16,8,512]{2,1,0:T(8,128)S(1)}, u32[]{:S(2)}, u32[]{:S(2)}) async-start(f32[16,8,512]{2,1,0:T(8,128)} %bitcast.238), calls=%async_computation.14 | async-start | bytes 524288 | tf_op jit(solution)/shard_map/all_to_all | solution.py:44
  220.9 3.4 %fusion.45 = f32[8,128,128,1]{2,0,1,3:T(8,128)S(1)} fusion(bf16[1,1,128,128,128]{4,3,2,1,0:T(8,128)(2,1)} %param.11, bf16[128,8,128]{2,1,0:T(8,128)(2,1)S(1)} %gather_fusion.8, f32[128]{0:T(128)S(1)} %compare_select_fusion.1, pred[128]{0:T(512)(128)(4,1)S(1)} %get-tuple-element.29), kind=kOutput, calls=%fused_computation.32 | convolution fusion | flops 33816576 | bytes 4981376 | tf_op jit(solution)/shard_map/sut,csu->cst/dot_general | solution.py:89
  224.7 0.9 copy.165
  225.5 4.2 %all-to-all-done.14 = f32[16,8,512]{2,1,0:T(8,128)S(1)} async-done(((f32[16,8,512]{2,1,0:T(8,128)}), f32[16,8,512]{2,1,0:T(8,128)S(1)}, u32[]{:S(2)}, u32[]{:S(2)}) %all-to-all-start.14) | async-done | bytes 262176 | tf_op jit(solution)/shard_map/all_to_all | solution.py:44
  229.8 6.3 %all-to-all-start.15 = ((f32[16,8,512]{2,1,0:T(8,128)}), f32[16,8,512]{2,1,0:T(8,128)S(1)}, u32[]{:S(2)}, u32[]{:S(2)}) async-start(f32[16,8,512]{2,1,0:T(8,128)} %bitcast.237), calls=%async_computation.15 | async-start | bytes 524288 | tf_op jit(solution)/shard_map/all_to_all | solution.py:44
  236.4 6.9 %all-to-all-done.15 = f32[16,8,512]{2,1,0:T(8,128)S(1)} async-done(((f32[16,8,512]{2,1,0:T(8,128)}), f32[16,8,512]{2,1,0:T(8,128)S(1)}, u32[]{:S(2)}, u32[]{:S(2)}) %all-to-all-start.15) | async-done | bytes 262176 | tf_op jit(solution)/shard_map/all_to_all | solution.py:44
  243.8 8.8 %all_to_all.96 = f32[16,1,128]{2,1,0:T(1,128)S(1)} all-to-all(f32[16,1,128]{2,1,0:T(1,128)S(1)} %broadcast_in_dim.55), channel_id=1, replica_groups=mesh['row'=16,'col'=16] {'row'}, dimensions={0} | all-to-all | bytes 16384 | tf_op jit(solution)/shard_map/all_to_all | solution.py:51
  252.6 12.9 %all_to_all.97 = f32[16,1,128]{2,1,0:T(1,128)S(1)} all-to-all(f32[16,1,128]{2,1,0:T(1,128)S(1)} %broadcast_in_dim.56), channel_id=1, replica_groups=mesh['row'=16,'col'=16] {'col'}, dimensions={0} | all-to-all | bytes 16384 | tf_op jit(solution)/shard_map/all_to_all | solution.py:51
  269.1 0.8 fusion.190
  (143 shorter events, 31.0 us)
Async XLA Ops:
  2.8 14.0 %all-to-all-start = ((bf16[16,9,512]{2,1,0:T(8,128)(2,1)}), bf16[16,9,512]{2,1,0:T(8,128)(2,1)S(1)}, u32[]{:S(2)}, u32[]{:S(2)}) async-start(bf16[16,9,512]{2,1,0:T(8,128)(2,1)} %broadcast_in_dim.44), calls=%async_computation | async-start | bytes 524288 | tf_op jit(solution)/shard_map/all_to_all | solution.py:39
  16.8 20.0 %all-to-all-start.1 = ((bf16[16,9,512]{2,1,0:T(8,128)(2,1)}), bf16[16,9,512]{2,1,0:T(8,128)(2,1)S(1)}, u32[]{:S(2)}, u32[]{:S(2)}) async-start(bf16[16,9,512]{2,1,0:T(8,128)(2,1)} %broadcast_in_dim.44), calls=%async_computation.1 | async-start | bytes 524288 | tf_op jit(solution)/shard_map/all_to_all | solution.py:39
  28.5 15.9 %copy-start.2 = (s32[1,1,2,128]{3,2,1,0:T(2,128)S(1)}, s32[1,1,2,128]{3,2,1,0:T(2,128)}, u32[]{:S(2)}) copy-start(s32[1,1,2,128]{3,2,1,0:T(2,128)} %param.12) | copy-start | bytes 3076
  38.1 20.4 %all-to-all-start.2 = ((f32[16,9,512]{2,1,0:T(8,128)}), f32[16,9,512]{2,1,0:T(8,128)S(1)}, u32[]{:S(2)}, u32[]{:S(2)}) async-start(f32[16,9,512]{2,1,0:T(8,128)} %copy.97), calls=%async_computation.2 | async-start | bytes 1048576 | tf_op jit(solution)/shard_map/all_to_all | solution.py:44
  45.3 21.5 %copy-start = (f32[8,512]{1,0:T(8,128)S(1)}, f32[8,512]{1,0:T(8,128)}, u32[]{:S(2)}) copy-start(f32[8,512]{1,0:T(8,128)} %param.15) | copy-start | bytes 49156
  45.3 36.7 %copy-start.1 = (f32[2,8,24]{2,1,0:T(8,128)S(1)}, f32[2,8,24]{2,1,0:T(8,128)}, u32[]{:S(2)}) copy-start(f32[2,8,24]{2,1,0:T(8,128)} %param.16) | copy-start | bytes 4612
  59.5 17.1 %all-to-all-start.3 = ((f32[16,9,512]{2,1,0:T(8,128)}), f32[16,9,512]{2,1,0:T(8,128)S(1)}, u32[]{:S(2)}, u32[]{:S(2)}) async-start(f32[16,9,512]{2,1,0:T(8,128)} %copy.101), calls=%async_computation.3 | async-start | bytes 1048576 | tf_op jit(solution)/shard_map/all_to_all | solution.py:44
  77.6 9.8 %all-to-all-start.4 = ((f32[16,1,128]{2,1,0:T(1,128)}), f32[16,1,128]{2,1,0:T(1,128)S(1)}, u32[]{:S(2)}, u32[]{:S(2)}) async-start(f32[16,1,128]{2,1,0:T(1,128)} %broadcast_in_dim.45), calls=%async_computation.4 | async-start | bytes 16384 | tf_op jit(solution)/shard_map/all_to_all | solution.py:51
  88.1 13.2 %all-to-all-start.5 = ((f32[16,1,128]{2,1,0:T(1,128)}), f32[16,1,128]{2,1,0:T(1,128)S(1)}, u32[]{:S(2)}, u32[]{:S(2)}) async-start(f32[16,1,128]{2,1,0:T(1,128)} %broadcast_in_dim.49), calls=%async_computation.5 | async-start | bytes 16384 | tf_op jit(solution)/shard_map/all_to_all | solution.py:51
  106.4 11.6 %all-to-all-start.6 = ((bf16[16,8,512]{2,1,0:T(8,128)(2,1)}), bf16[16,8,512]{2,1,0:T(8,128)(2,1)S(1)}, u32[]{:S(2)}, u32[]{:S(2)}) async-start(bf16[16,8,512]{2,1,0:T(8,128)(2,1)} %broadcast_in_dim.51), calls=%async_computation.6 | async-start | bytes 262144 | tf_op jit(solution)/shard_map/all_to_all | solution.py:39
  117.9 12.5 %all-to-all-start.7 = ((bf16[16,8,512]{2,1,0:T(8,128)(2,1)}), bf16[16,8,512]{2,1,0:T(8,128)(2,1)S(1)}, u32[]{:S(2)}, u32[]{:S(2)}) async-start(bf16[16,8,512]{2,1,0:T(8,128)(2,1)} %broadcast_in_dim.51), calls=%async_computation.7 | async-start | bytes 262144 | tf_op jit(solution)/shard_map/all_to_all | solution.py:39
  130.4 16.1 %all-to-all-start.8 = ((f32[16,8,512]{2,1,0:T(8,128)}), f32[16,8,512]{2,1,0:T(8,128)S(1)}, u32[]{:S(2)}, u32[]{:S(2)}) async-start(f32[16,8,512]{2,1,0:T(8,128)} %bitcast.240), calls=%async_computation.8 | async-start | bytes 524288 | tf_op jit(solution)/shard_map/all_to_all | solution.py:44
  146.5 13.5 %all-to-all-start.9 = ((f32[16,8,512]{2,1,0:T(8,128)}), f32[16,8,512]{2,1,0:T(8,128)S(1)}, u32[]{:S(2)}, u32[]{:S(2)}) async-start(f32[16,8,512]{2,1,0:T(8,128)} %bitcast.239), calls=%async_computation.9 | async-start | bytes 524288 | tf_op jit(solution)/shard_map/all_to_all | solution.py:44
  161.1 9.7 %all-to-all-start.10 = ((f32[16,1,128]{2,1,0:T(1,128)}), f32[16,1,128]{2,1,0:T(1,128)S(1)}, u32[]{:S(2)}, u32[]{:S(2)}) async-start(f32[16,1,128]{2,1,0:T(1,128)} %broadcast_in_dim.52), calls=%async_computation.10 | async-start | bytes 16384 | tf_op jit(solution)/shard_map/all_to_all | solution.py:51
  171.5 13.0 %all-to-all-start.11 = ((f32[16,1,128]{2,1,0:T(1,128)}), f32[16,1,128]{2,1,0:T(1,128)S(1)}, u32[]{:S(2)}, u32[]{:S(2)}) async-start(f32[16,1,128]{2,1,0:T(1,128)} %broadcast_in_dim.53), calls=%async_computation.11 | async-start | bytes 16384 | tf_op jit(solution)/shard_map/all_to_all | solution.py:51
  189.6 11.6 %all-to-all-start.12 = ((bf16[16,8,512]{2,1,0:T(8,128)(2,1)}), bf16[16,8,512]{2,1,0:T(8,128)(2,1)S(1)}, u32[]{:S(2)}, u32[]{:S(2)}) async-start(bf16[16,8,512]{2,1,0:T(8,128)(2,1)} %broadcast_in_dim.54), calls=%async_computation.12 | async-start | bytes 262144 | tf_op jit(solution)/shard_map/all_to_all | solution.py:39
  201.2 12.5 %all-to-all-start.13 = ((bf16[16,8,512]{2,1,0:T(8,128)(2,1)}), bf16[16,8,512]{2,1,0:T(8,128)(2,1)S(1)}, u32[]{:S(2)}, u32[]{:S(2)}) async-start(bf16[16,8,512]{2,1,0:T(8,128)(2,1)} %broadcast_in_dim.54), calls=%async_computation.13 | async-start | bytes 262144 | tf_op jit(solution)/shard_map/all_to_all | solution.py:39
  213.7 16.1 %all-to-all-start.14 = ((f32[16,8,512]{2,1,0:T(8,128)}), f32[16,8,512]{2,1,0:T(8,128)S(1)}, u32[]{:S(2)}, u32[]{:S(2)}) async-start(f32[16,8,512]{2,1,0:T(8,128)} %bitcast.238), calls=%async_computation.14 | async-start | bytes 524288 | tf_op jit(solution)/shard_map/all_to_all | solution.py:44
  229.8 13.5 %all-to-all-start.15 = ((f32[16,8,512]{2,1,0:T(8,128)}), f32[16,8,512]{2,1,0:T(8,128)S(1)}, u32[]{:S(2)}, u32[]{:S(2)}) async-start(f32[16,8,512]{2,1,0:T(8,128)} %bitcast.237), calls=%async_computation.15 | async-start | bytes 524288 | tf_op jit(solution)/shard_map/all_to_all | solution.py:44

commit v7 on v4

--- a/solution.py
+++ b/solution.py
@@ -33,16 +33,23 @@
     )
 
 
+def dense_rows(chunks):
+    peers, rows, nodes = chunks.shape
+    if rows % 8 == 0:
+        return chunks
+    return chunks.reshape(peers, rows * nodes // 128, 128)
+
+
 def gather_by_exchange(local, axis):
     count = lax.axis_size(axis)
     copies = jnp.broadcast_to(local[None], (count,) + local.shape)
-    held = lax.all_to_all(copies, axis, 0, 0, tiled=True)
+    held = lax.all_to_all(dense_rows(copies), axis, 0, 0, tiled=True).reshape(copies.shape)
     return jnp.swapaxes(held, 0, 1).reshape(local.shape[0], count * local.shape[1])
 
 
 def scatter_sum_by_exchange(chunks, axis):
-    held = lax.all_to_all(chunks, axis, 0, 0, tiled=True)
-    return jnp.sum(held, axis=0)
+    held = lax.all_to_all(dense_rows(chunks), axis, 0, 0, tiled=True)
+    return jnp.sum(held, axis=0).reshape(chunks.shape[1:])
 
 
 def gram_sums(new_vecs, new_images):

time: 259 us -> 251 us (0.969)
  waiting for transfers between devices: 91.1 us -> 84.2 us
    all_to_all x12, waiting for transfers between devices: 66.4 us -> 59.4 us  [the longest x6 35.5 us: scatter_sum_by_exchange(): held = lax.all_to_all(dense_rows(chunks), axis, 0, 0, tiled=True)]
where the time goes in v7:
time: 251 us; the launch traced here: 250 us
  starting transfers between devices  84.3 us (34%)
  waiting for transfers between devices  84.2 us (34%)
  matrix products  33.7 us (13%)
  blocking collectives  18.8 us (7%)
  local copies, waits for them, and re-layouts  18 us (7%)
  other arithmetic  9.17 us (4%)
    all_to_all x6, starting transfers between devices, scatter_sum_by_exchange(): held = lax.all_to_all(dense_rows(chunks), axis, 0, 0, tiled=True)  38.1 us
    all_to_all x6, waiting for transfers between devices, scatter_sum_by_exchange(): held = lax.all_to_all(dense_rows(chunks), axis, 0, 0, tiled=True)  35.5 us
    all_to_all x6, starting transfers between devices, gather_by_exchange(): lax.all_to_all(dense_rows(copies), axis, 0, 0, tiled=True)  33.3 us
    all_to_all x2, waiting for transfers between devices, gram_sums(): held = lax.all_to_all(copies, ('row', 'col'), 0, 0, tiled=True)  24.8 us
    all_to_all x6, waiting for transfers between devices, gather_by_exchange(): lax.all_to_all(dense_rows(copies), axis, 0, 0, tiled=True)  23.9 us
    all_to_all x1, blocking collectives, gram_sums(): held = lax.all_to_all(copies, ('row', 'col'), 0, 0, tiled=True)  18.8 us
    dot_general x3, matrix products, direct_terms(): jnp.einsum('sut,cst->csu', part_tiles, col_values, preferred_element_type...  13.5 us
    all_to_all x2, starting transfers between devices, gram_sums(): held = lax.all_to_all(copies, ('row', 'col'), 0, 0, tiled=True)  12.9 us
  transfers between devices with their start and end apart: 14, of which 14 were waited for; matrix products, arithmetic and copies ran while one was open for 15% of the time, Pallas kernels for 0%

profile of v7, /device:TPU:1, one launch (start us, length us, event | category | flops | bytes accessed | tf_op | source)
XLA Modules:
  0.0 249.9 jit_solution(16663346351212248579)
XLA Ops:
  1.3 0.7 fusion.137
  2.8 6.8 %all-to-all-start = ((bf16[16,36,128]{2,1,0:T(8,128)(2,1)}), bf16[16,36,128]{2,1,0:T(8,128)(2,1)S(1)}, u32[]{:S(2)}, u32[]{:S(2)}) async-start(bf16[16,36,128]{2,1,0:T(8,128)(2,1)} %broadcast_in_dim.38), calls=%async_computation | async-start | bytes 327680 | tf_op jit(solution)/shard_map/all_to_all | solution.py:46
  9.6 0.8 compare_and_fusion
  10.4 0.8 slice_bitcast_fusion.2
  11.8 4.2 %all-to-all-done = bf16[16,36,128]{2,1,0:T(8,128)(2,1)S(1)} async-done(((bf16[16,36,128]{2,1,0:T(8,128)(2,1)}), bf16[16,36,128]{2,1,0:T(8,128)(2,1)S(1)}, u32[]{:S(2)}, u32[]{:S(2)}) %all-to-all-start) | async-done | bytes 147488 | tf_op jit(solution)/shard_map/all_to_all | solution.py:46
  16.0 10.6 %all-to-all-start.1 = ((bf16[16,36,128]{2,1,0:T(8,128)(2,1)}), bf16[16,36,128]{2,1,0:T(8,128)(2,1)S(1)}, u32[]{:S(2)}, u32[]{:S(2)}) async-start(bf16[16,36,128]{2,1,0:T(8,128)(2,1)} %broadcast_in_dim.38), calls=%async_computation.1 | async-start | bytes 327680 | tf_op jit(solution)/shard_map/all_to_all | solution.py:46
  27.7 4.5 %fusion.15 = f32[9,128,128,1]{2,0,1,3:T(8,128)S(1)} fusion(bf16[1,1,128,128,128]{4,3,2,1,0:T(8,128)(2,1)} %param.11, bf16[128,9,128]{2,1,0:T(8,128)(2,1)S(1)} %gather_fusion.3, f32[128]{0:T(128)S(1)} %compare_convert_fusion, pred[128]{0:T(512)(128)(4,1)S(1)} %get-tuple-element.37), kind=kOutput, calls=%fused_computation.22 | convolution fusion | flops 38043648 | bytes 5079680 | tf_op jit(solution)/shard_map/sut,cst->csu/dot_general | solution.py:81
  32.8 2.7 %all-to-all-done.1 = bf16[16,36,128]{2,1,0:T(8,128)(2,1)S(1)} async-done(((bf16[16,36,128]{2,1,0:T(8,128)(2,1)}), bf16[16,36,128]{2,1,0:T(8,128)(2,1)S(1)}, u32[]{:S(2)}, u32[]{:S(2)}) %all-to-all-start.1) | async-done | bytes 147488 | tf_op jit(solution)/shard_map/all_to_all | solution.py:46
  36.1 0.8 reshape.309
  36.9 6.3 %all-to-all-start.2 = ((f32[16,36,128]{2,1,0:T(8,128)}), f32[16,36,128]{2,1,0:T(8,128)S(1)}, u32[]{:S(2)}, u32[]{:S(2)}) async-start(f32[16,36,128]{2,1,0:T(8,128)} %reshape.309), calls=%async_computation.2 | async-start | bytes 655360 | tf_op jit(solution)/shard_map/all_to_all | solution.py:51
  44.2 3.5 %fusion.21 = f32[9,128,128,1]{2,0,1,3:T(8,128)S(1)} fusion(bf16[1,1,128,128,128]{4,3,2,1,0:T(8,128)(2,1)} %param.11, bf16[128,9,128]{2,1,0:T(8,128)(2,1)S(1)} %gather_fusion.4, f32[128]{0:T(128)S(1)} %compare_select_fusion.1, pred[128]{0:T(512)(128)(4,1)S(1)} %get-tuple-element.29), kind=kOutput, calls=%fused_computation.24 | convolution fusion | flops 38043648 | bytes 5079680 | tf_op jit(solution)/shard_map/sut,csu->cst/dot_general | solution.py:93
  48.2 5.8 %all-to-all-done.2 = f32[16,36,128]{2,1,0:T(8,128)S(1)} async-done(((f32[16,36,128]{2,1,0:T(8,128)}), f32[16,36,128]{2,1,0:T(8,128)S(1)}, u32[]{:S(2)}, u32[]{:S(2)}) %all-to-all-start.2) | async-done | bytes 294944 | tf_op jit(solution)/shard_map/all_to_all | solution.py:51
  54.2 0.8 reshape.313
  55.0 6.4 %all-to-all-start.3 = ((f32[16,36,128]{2,1,0:T(8,128)}), f32[16,36,128]{2,1,0:T(8,128)S(1)}, u32[]{:S(2)}, u32[]{:S(2)}) async-start(f32[16,36,128]{2,1,0:T(8,128)} %reshape.313), calls=%async_computation.3 | async-start | bytes 655360 | tf_op jit(solution)/shard_map/all_to_all | solution.py:51
  61.6 7.5 %all-to-all-done.3 = f32[16,36,128]{2,1,0:T(8,128)S(1)} async-done(((f32[16,36,128]{2,1,0:T(8,128)}), f32[16,36,128]{2,1,0:T(8,128)S(1)}, u32[]{:S(2)}, u32[]{:S(2)}) %all-to-all-start.3) | async-done | bytes 294944 | tf_op jit(solution)/shard_map/all_to_all | solution.py:51
  69.5 0.7 broadcast_in_dim.39
  70.2 6.6 %all-to-all-start.4 = ((f32[256,1,128]{2,1,0:T(1,128)}), f32[256,1,128]{2,1,0:T(1,128)S(1)}, u32[]{:S(2)}, u32[]{:S(2)}) async-start(f32[256,1,128]{2,1,0:T(1,128)} %broadcast_in_dim.39), calls=%async_computation.4 | async-start | bytes 262144 | tf_op jit(solution)/shard_map/all_to_all | solution.py:62
  76.8 12.6 %all-to-all-done.4 = f32[256,1,128]{2,1,0:T(1,128)S(1)} async-done(((f32[256,1,128]{2,1,0:T(1,128)}), f32[256,1,128]{2,1,0:T(1,128)S(1)}, u32[]{:S(2)}, u32[]{:S(2)}) %all-to-all-start.4) | async-done | bytes 131104 | tf_op jit(solution)/shard_map/all_to_all | solution.py:62
  94.5 4.4 %all-to-all-start.5 = ((bf16[16,8,512]{2,1,0:T(8,128)(2,1)}), bf16[16,8,512]{2,1,0:T(8,128)(2,1)S(1)}, u32[]{:S(2)}, u32[]{:S(2)}) async-start(bf16[16,8,512]{2,1,0:T(8,128)(2,1)} %broadcast_in_dim.41), calls=%async_computation.5 | async-start | bytes 262144 | tf_op jit(solution)/shard_map/all_to_all | solution.py:46
  99.1 6.0 %all-to-all-done.5 = bf16[16,8,512]{2,1,0:T(8,128)(2,1)S(1)} async-done(((bf16[16,8,512]{2,1,0:T(8,128)(2,1)}), bf16[16,8,512]{2,1,0:T(8,128)(2,1)S(1)}, u32[]{:S(2)}, u32[]{:S(2)}) %all-to-all-start.5) | async-done | bytes 131104 | tf_op jit(solution)/shard_map/all_to_all | solution.py:46
  105.1 3.5 %all-to-all-start.6 = ((bf16[16,8,512]{2,1,0:T(8,128)(2,1)}), bf16[16,8,512]{2,1,0:T(8,128)(2,1)S(1)}, u32[]{:S(2)}, u32[]{:S(2)}) async-start(bf16[16,8,512]{2,1,0:T(8,128)(2,1)} %broadcast_in_dim.41), calls=%async_computation.6 | async-start | bytes 262144 | tf_op jit(solution)/shard_map/all_to_all | solution.py:46
  109.3 4.5 %fusion.27 = f32[8,128,128,1]{2,0,1,3:T(8,128)S(1)} fusion(bf16[1,1,128,128,128]{4,3,2,1,0:T(8,128)(2,1)} %param.11, bf16[128,8,128]{2,1,0:T(8,128)(2,1)S(1)} %gather_fusion.5, f32[128]{0:T(128)S(1)} %compare_convert_fusion, pred[128]{0:T(512)(128)(4,1)S(1)} %get-tuple-element.37), kind=kOutput, calls=%fused_computation.26 | convolution fusion | flops 33816576 | bytes 4981376 | tf_op jit(solution)/shard_map/sut,cst->csu/dot_general | solution.py:81
  114.2 0.8 copy.173
  115.1 2.6 %all-to-all-done.6 = bf16[16,8,512]{2,1,0:T(8,128)(2,1)S(1)} async-done(((bf16[16,8,512]{2,1,0:T(8,128)(2,1)}), bf16[16,8,512]{2,1,0:T(8,128)(2,1)S(1)}, u32[]{:S(2)}, u32[]{:S(2)}) %all-to-all-start.6) | async-done | bytes 131104 | tf_op jit(solution)/shard_map/all_to_all | solution.py:46
  117.6 6.5 %all-to-all-start.7 = ((f32[16,8,512]{2,1,0:T(8,128)}), f32[16,8,512]{2,1,0:T(8,128)S(1)}, u32[]{:S(2)}, u32[]{:S(2)}) async-start(f32[16,8,512]{2,1,0:T(8,128)} %bitcast.239), calls=%async_computation.7 | async-start | bytes 524288 | tf_op jit(solution)/shard_map/all_to_all | solution.py:51
  124.8 3.4 %fusion.33 = f32[8,128,128,1]{2,0,1,3:T(8,128)S(1)} fusion(bf16[1,1,128,128,128]{4,3,2,1,0:T(8,128)(2,1)} %param.11, bf16[128,8,128]{2,1,0:T(8,128)(2,1)S(1)} %gather_fusion.6, f32[128]{0:T(128)S(1)} %compare_select_fusion.1, pred[128]{0:T(512)(128)(4,1)S(1)} %get-tuple-element.29), kind=kOutput, calls=%fused_computation.28 | convolution fusion | flops 33816576 | bytes 4981376 | tf_op jit(solution)/shard_map/sut,csu->cst/dot_general | solution.py:93
  128.6 0.9 copy.172
  129.5 4.2 %all-to-all-done.7 = f32[16,8,512]{2,1,0:T(8,128)S(1)} async-done(((f32[16,8,512]{2,1,0:T(8,128)}), f32[16,8,512]{2,1,0:T(8,128)S(1)}, u32[]{:S(2)}, u32[]{:S(2)}) %all-to-all-start.7) | async-done | bytes 262176 | tf_op jit(solution)/shard_map/all_to_all | solution.py:51
  133.7 6.3 %all-to-all-start.8 = ((f32[16,8,512]{2,1,0:T(8,128)}), f32[16,8,512]{2,1,0:T(8,128)S(1)}, u32[]{:S(2)}, u32[]{:S(2)}) async-start(f32[16,8,512]{2,1,0:T(8,128)} %bitcast.238), calls=%async_computation.8 | async-start | bytes 524288 | tf_op jit(solution)/shard_map/all_to_all | solution.py:51
  140.3 6.9 %all-to-all-done.8 = f32[16,8,512]{2,1,0:T(8,128)S(1)} async-done(((f32[16,8,512]{2,1,0:T(8,128)}), f32[16,8,512]{2,1,0:T(8,128)S(1)}, u32[]{:S(2)}, u32[]{:S(2)}) %all-to-all-start.8) | async-done | bytes 262176 | tf_op jit(solution)/shard_map/all_to_all | solution.py:51
  147.7 0.7 broadcast_in_dim.45
  148.4 6.3 %all-to-all-start.9 = ((f32[256,1,128]{2,1,0:T(1,128)}), f32[256,1,128]{2,1,0:T(1,128)S(1)}, u32[]{:S(2)}, u32[]{:S(2)}) async-start(f32[256,1,128]{2,1,0:T(1,128)} %broadcast_in_dim.45), calls=%async_computation.9 | async-start | bytes 262144 | tf_op jit(solution)/shard_map/all_to_all | solution.py:62
  155.1 12.2 %all-to-all-done.9 = f32[256,1,128]{2,1,0:T(1,128)S(1)} async-done(((f32[256,1,128]{2,1,0:T(1,128)}), f32[256,1,128]{2,1,0:T(1,128)S(1)}, u32[]{:S(2)}, u32[]{:S(2)}) %all-to-all-start.9) | async-done | bytes 131104 | tf_op jit(solution)/shard_map/all_to_all | solution.py:62
  172.5 4.4 %all-to-all-start.10 = ((bf16[16,8,512]{2,1,0:T(8,128)(2,1)}), bf16[16,8,512]{2,1,0:T(8,128)(2,1)S(1)}, u32[]{:S(2)}, u32[]{:S(2)}) async-start(bf16[16,8,512]{2,1,0:T(8,128)(2,1)} %broadcast_in_dim.46), calls=%async_computation.10 | async-start | bytes 262144 | tf_op jit(solution)/shard_map/all_to_all | solution.py:46
  177.2 5.9 %all-to-all-done.10 = bf16[16,8,512]{2,1,0:T(8,128)(2,1)S(1)} async-done(((bf16[16,8,512]{2,1,0:T(8,128)(2,1)}), bf16[16,8,512]{2,1,0:T(8,128)(2,1)S(1)}, u32[]{:S(2)}, u32[]{:S(2)}) %all-to-all-start.10) | async-done | bytes 131104 | tf_op jit(solution)/shard_map/all_to_all | solution.py:46
  183.1 3.5 %all-to-all-start.11 = ((bf16[16,8,512]{2,1,0:T(8,128)(2,1)}), bf16[16,8,512]{2,1,0:T(8,128)(2,1)S(1)}, u32[]{:S(2)}, u32[]{:S(2)}) async-start(bf16[16,8,512]{2,1,0:T(8,128)(2,1)} %broadcast_in_dim.46), calls=%async_computation.11 | async-start | bytes 262144 | tf_op jit(solution)/shard_map/all_to_all | solution.py:46
  187.3 4.5 %fusion.39 = f32[8,128,128,1]{2,0,1,3:T(8,128)S(1)} fusion(bf16[1,1,128,128,128]{4,3,2,1,0:T(8,128)(2,1)} %param.11, bf16[128,8,128]{2,1,0:T(8,128)(2,1)S(1)} %gather_fusion.7, f32[128]{0:T(128)S(1)} %compare_convert_fusion, pred[128]{0:T(512)(128)(4,1)S(1)} %get-tuple-element.37), kind=kOutput, calls=%fused_computation.30 | convolution fusion | flops 33816576 | bytes 4981376 | tf_op jit(solution)/shard_map/sut,cst->csu/dot_general | solution.py:81
  192.2 0.8 copy.171
  193.0 2.6 %all-to-all-done.11 = bf16[16,8,512]{2,1,0:T(8,128)(2,1)S(1)} async-done(((bf16[16,8,512]{2,1,0:T(8,128)(2,1)}), bf16[16,8,512]{2,1,0:T(8,128)(2,1)S(1)}, u32[]{:S(2)}, u32[]{:S(2)}) %all-to-all-start.11) | async-done | bytes 131104 | tf_op jit(solution)/shard_map/all_to_all | solution.py:46
  195.6 6.5 %all-to-all-start.12 = ((f32[16,8,512]{2,1,0:T(8,128)}), f32[16,8,512]{2,1,0:T(8,128)S(1)}, u32[]{:S(2)}, u32[]{:S(2)}) async-start(f32[16,8,512]{2,1,0:T(8,128)} %bitcast.237), calls=%async_computation.12 | async-start | bytes 524288 | tf_op jit(solution)/shard_map/all_to_all | solution.py:51
  202.7 3.4 %fusion.45 = f32[8,128,128,1]{2,0,1,3:T(8,128)S(1)} fusion(bf16[1,1,128,128,128]{4,3,2,1,0:T(8,128)(2,1)} %param.11, bf16[128,8,128]{2,1,0:T(8,128)(2,1)S(1)} %gather_fusion.8, f32[128]{0:T(128)S(1)} %compare_select_fusion.1, pred[128]{0:T(512)(128)(4,1)S(1)} %get-tuple-element.29), kind=kOutput, calls=%fused_computation.32 | convolution fusion | flops 33816576 | bytes 4981376 | tf_op jit(solution)/shard_map/sut,csu->cst/dot_general | solution.py:93
  206.6 0.9 copy.170
  207.4 4.2 %all-to-all-done.12 = f32[16,8,512]{2,1,0:T(8,128)S(1)} async-done(((f32[16,8,512]{2,1,0:T(8,128)}), f32[16,8,512]{2,1,0:T(8,128)S(1)}, u32[]{:S(2)}, u32[]{:S(2)}) %all-to-all-start.12) | async-done | bytes 262176 | tf_op jit(solution)/shard_map/all_to_all | solution.py:51
  211.7 6.3 %all-to-all-start.13 = ((f32[16,8,512]{2,1,0:T(8,128)}), f32[16,8,512]{2,1,0:T(8,128)S(1)}, u32[]{:S(2)}, u32[]{:S(2)}) async-start(f32[16,8,512]{2,1,0:T(8,128)} %bitcast.236), calls=%async_computation.13 | async-start | bytes 524288 | tf_op jit(solution)/shard_map/all_to_all | solution.py:51
  218.3 6.9 %all-to-all-done.13 = f32[16,8,512]{2,1,0:T(8,128)S(1)} async-done(((f32[16,8,512]{2,1,0:T(8,128)}), f32[16,8,512]{2,1,0:T(8,128)S(1)}, u32[]{:S(2)}, u32[]{:S(2)}) %all-to-all-start.13) | async-done | bytes 262176 | tf_op jit(solution)/shard_map/all_to_all | solution.py:51
  225.8 18.8 %all_to_all.78 = f32[256,1,128]{2,1,0:T(1,128)S(1)} all-to-all(f32[256,1,128]{2,1,0:T(1,128)S(1)} %broadcast_in_dim.47), channel_id=1, replica_groups=mesh['row'=16,'col'=16] {'row','col'}, dimensions={0} | all-to-all | bytes 262144 | tf_op jit(solution)/shard_map/all_to_all | solution.py:62
  248.2 0.8 fusion.191
  249.1 0.7 fusion.193
  (139 shorter events, 26.9 us)
Async XLA Ops:
  2.8 13.2 %all-to-all-start = ((bf16[16,36,128]{2,1,0:T(8,128)(2,1)}), bf16[16,36,128]{2,1,0:T(8,128)(2,1)S(1)}, u32[]{:S(2)}, u32[]{:S(2)}) async-start(bf16[16,36,128]{2,1,0:T(8,128)(2,1)} %broadcast_in_dim.38), calls=%async_computation | async-start | bytes 327680 | tf_op jit(solution)/shard_map/all_to_all | solution.py:46
  16.0 19.6 %all-to-all-start.1 = ((bf16[16,36,128]{2,1,0:T(8,128)(2,1)}), bf16[16,36,128]{2,1,0:T(8,128)(2,1)S(1)}, u32[]{:S(2)}, u32[]{:S(2)}) async-start(bf16[16,36,128]{2,1,0:T(8,128)(2,1)} %broadcast_in_dim.38), calls=%async_computation.1 | async-start | bytes 327680 | tf_op jit(solution)/shard_map/all_to_all | solution.py:46
  32.3 11.0 %copy-start.2 = (s32[1,1,2,128]{3,2,1,0:T(2,128)S(1)}, s32[1,1,2,128]{3,2,1,0:T(2,128)}, u32[]{:S(2)}) copy-start(s32[1,1,2,128]{3,2,1,0:T(2,128)} %param.12) | copy-start | bytes 3076
  36.9 17.1 %all-to-all-start.2 = ((f32[16,36,128]{2,1,0:T(8,128)}), f32[16,36,128]{2,1,0:T(8,128)S(1)}, u32[]{:S(2)}, u32[]{:S(2)}) async-start(f32[16,36,128]{2,1,0:T(8,128)} %reshape.309), calls=%async_computation.2 | async-start | bytes 655360 | tf_op jit(solution)/shard_map/all_to_all | solution.py:51
  44.2 17.2 %copy-start = (f32[8,512]{1,0:T(8,128)S(1)}, f32[8,512]{1,0:T(8,128)}, u32[]{:S(2)}) copy-start(f32[8,512]{1,0:T(8,128)} %param.15) | copy-start | bytes 49156
  44.2 32.6 %copy-start.1 = (f32[2,8,24]{2,1,0:T(8,128)S(1)}, f32[2,8,24]{2,1,0:T(8,128)}, u32[]{:S(2)}) copy-start(f32[2,8,24]{2,1,0:T(8,128)} %param.16) | copy-start | bytes 4612
  55.0 14.1 %all-to-all-start.3 = ((f32[16,36,128]{2,1,0:T(8,128)}), f32[16,36,128]{2,1,0:T(8,128)S(1)}, u32[]{:S(2)}, u32[]{:S(2)}) async-start(f32[16,36,128]{2,1,0:T(8,128)} %reshape.313), calls=%async_computation.3 | async-start | bytes 655360 | tf_op jit(solution)/shard_map/all_to_all | solution.py:51
  70.2 19.2 %all-to-all-start.4 = ((f32[256,1,128]{2,1,0:T(1,128)}), f32[256,1,128]{2,1,0:T(1,128)S(1)}, u32[]{:S(2)}, u32[]{:S(2)}) async-start(f32[256,1,128]{2,1,0:T(1,128)} %broadcast_in_dim.39), calls=%async_computation.4 | async-start | bytes 262144 | tf_op jit(solution)/shard_map/all_to_all | solution.py:62
  94.5 10.6 %all-to-all-start.5 = ((bf16[16,8,512]{2,1,0:T(8,128)(2,1)}), bf16[16,8,512]{2,1,0:T(8,128)(2,1)S(1)}, u32[]{:S(2)}, u32[]{:S(2)}) async-start(bf16[16,8,512]{2,1,0:T(8,128)(2,1)} %broadcast_in_dim.41), calls=%async_computation.5 | async-start | bytes 262144 | tf_op jit(solution)/shard_map/all_to_all | solution.py:46
  105.1 12.5 %all-to-all-start.6 = ((bf16[16,8,512]{2,1,0:T(8,128)(2,1)}), bf16[16,8,512]{2,1,0:T(8,128)(2,1)S(1)}, u32[]{:S(2)}, u32[]{:S(2)}) async-start(bf16[16,8,512]{2,1,0:T(8,128)(2,1)} %broadcast_in_dim.41), calls=%async_computation.6 | async-start | bytes 262144 | tf_op jit(solution)/shard_map/all_to_all | solution.py:46
  117.6 16.1 %all-to-all-start.7 = ((f32[16,8,512]{2,1,0:T(8,128)}), f32[16,8,512]{2,1,0:T(8,128)S(1)}, u32[]{:S(2)}, u32[]{:S(2)}) async-start(f32[16,8,512]{2,1,0:T(8,128)} %bitcast.239), calls=%async_computation.7 | async-start | bytes 524288 | tf_op jit(solution)/shard_map/all_to_all | solution.py:51
  133.7 13.5 %all-to-all-start.8 = ((f32[16,8,512]{2,1,0:T(8,128)}), f32[16,8,512]{2,1,0:T(8,128)S(1)}, u32[]{:S(2)}, u32[]{:S(2)}) async-start(f32[16,8,512]{2,1,0:T(8,128)} %bitcast.238), calls=%async_computation.8 | async-start | bytes 524288 | tf_op jit(solution)/shard_map/all_to_all | solution.py:51
  148.4 18.9 %all-to-all-start.9 = ((f32[256,1,128]{2,1,0:T(1,128)}), f32[256,1,128]{2,1,0:T(1,128)S(1)}, u32[]{:S(2)}, u32[]{:S(2)}) async-start(f32[256,1,128]{2,1,0:T(1,128)} %broadcast_in_dim.45), calls=%async_computation.9 | async-start | bytes 262144 | tf_op jit(solution)/shard_map/all_to_all | solution.py:62
  172.5 10.6 %all-to-all-start.10 = ((bf16[16,8,512]{2,1,0:T(8,128)(2,1)}), bf16[16,8,512]{2,1,0:T(8,128)(2,1)S(1)}, u32[]{:S(2)}, u32[]{:S(2)}) async-start(bf16[16,8,512]{2,1,0:T(8,128)(2,1)} %broadcast_in_dim.46), calls=%async_computation.10 | async-start | bytes 262144 | tf_op jit(solution)/shard_map/all_to_all | solution.py:46
  183.1 12.5 %all-to-all-start.11 = ((bf16[16,8,512]{2,1,0:T(8,128)(2,1)}), bf16[16,8,512]{2,1,0:T(8,128)(2,1)S(1)}, u32[]{:S(2)}, u32[]{:S(2)}) async-start(bf16[16,8,512]{2,1,0:T(8,128)(2,1)} %broadcast_in_dim.46), calls=%async_computation.11 | async-start | bytes 262144 | tf_op jit(solution)/shard_map/all_to_all | solution.py:46
  195.6 16.1 %all-to-all-start.12 = ((f32[16,8,512]{2,1,0:T(8,128)}), f32[16,8,512]{2,1,0:T(8,128)S(1)}, u32[]{:S(2)}, u32[]{:S(2)}) async-start(f32[16,8,512]{2,1,0:T(8,128)} %bitcast.237), calls=%async_computation.12 | async-start | bytes 524288 | tf_op jit(solution)/shard_map/all_to_all | solution.py:51
  211.7 13.5 %all-to-all-start.13 = ((f32[16,8,512]{2,1,0:T(8,128)}), f32[16,8,512]{2,1,0:T(8,128)S(1)}, u32[]{:S(2)}, u32[]{:S(2)}) async-start(f32[16,8,512]{2,1,0:T(8,128)} %bitcast.236), calls=%async_computation.13 | async-start | bytes 524288 | tf_op jit(solution)/shard_map/all_to_all | solution.py:51

commit v8 on v7

--- a/solution.py
+++ b/solution.py
@@ -35,7 +35,7 @@
 
 def dense_rows(chunks):
     peers, rows, nodes = chunks.shape
-    if rows % 8 == 0:
+    if rows % (32 // chunks.dtype.itemsize) == 0:
         return chunks
     return chunks.reshape(peers, rows * nodes // 128, 128)
 

time: 251 us -> 252 us (level)
  no operation moved by 1% of the time
where the time goes in v8:
time: 252 us; the launch traced here: 250 us
  starting transfers between devices  84.6 us (34%)
  waiting for transfers between devices  84 us (33%)
  matrix products  33.7 us (13%)
  blocking collectives  18.8 us (7%)
  local copies, waits for them, and re-layouts  18.4 us (7%)
  other arithmetic  9.17 us (4%)
    all_to_all x6, starting transfers between devices, scatter_sum_by_exchange(): held = lax.all_to_all(dense_rows(chunks), axis, 0, 0, tiled=True)  38.3 us
    all_to_all x6, waiting for transfers between devices, scatter_sum_by_exchange(): held = lax.all_to_all(dense_rows(chunks), axis, 0, 0, tiled=True)  35.5 us
    all_to_all x6, starting transfers between devices, gather_by_exchange(): lax.all_to_all(dense_rows(copies), axis, 0, 0, tiled=True)  33.3 us
    all_to_all x2, waiting for transfers between devices, gram_sums(): held = lax.all_to_all(copies, ('row', 'col'), 0, 0, tiled=True)  24.8 us
    all_to_all x6, waiting for transfers between devices, gather_by_exchange(): lax.all_to_all(dense_rows(copies), axis, 0, 0, tiled=True)  23.7 us
    all_to_all x1, blocking collectives, gram_sums(): held = lax.all_to_all(copies, ('row', 'col'), 0, 0, tiled=True)  18.8 us
    dot_general x3, matrix products, direct_terms(): jnp.einsum('sut,cst->csu', part_tiles, col_values, preferred_element_type...  13.5 us
    all_to_all x2, starting transfers between devices, gram_sums(): held = lax.all_to_all(copies, ('row', 'col'), 0, 0, tiled=True)  12.9 us
  transfers between devices with their start and end apart: 14, of which 14 were waited for; matrix products, arithmetic and copies ran while one was open for 15% of the time, Pallas kernels for 0%

profile of v8, /device:TPU:1, one launch (start us, length us, event | category | flops | bytes accessed | tf_op | source)
XLA Modules:
  0.0 250.3 jit_solution(1559794916295094833)
XLA Ops:
  1.3 0.7 fusion.137
  2.8 6.8 %all-to-all-start = ((bf16[16,36,128]{2,1,0:T(8,128)(2,1)}), bf16[16,36,128]{2,1,0:T(8,128)(2,1)S(1)}, u32[]{:S(2)}, u32[]{:S(2)}) async-start(bf16[16,36,128]{2,1,0:T(8,128)(2,1)} %broadcast_in_dim.45), calls=%async_computation | async-start | bytes 327680 | tf_op jit(solution)/shard_map/all_to_all | solution.py:46
  9.6 0.8 compare_and_fusion
  10.4 0.8 slice_bitcast_fusion.2
  11.8 4.2 %all-to-all-done = bf16[16,36,128]{2,1,0:T(8,128)(2,1)S(1)} async-done(((bf16[16,36,128]{2,1,0:T(8,128)(2,1)}), bf16[16,36,128]{2,1,0:T(8,128)(2,1)S(1)}, u32[]{:S(2)}, u32[]{:S(2)}) %all-to-all-start) | async-done | bytes 147488 | tf_op jit(solution)/shard_map/all_to_all | solution.py:46
  16.0 10.6 %all-to-all-start.1 = ((bf16[16,36,128]{2,1,0:T(8,128)(2,1)}), bf16[16,36,128]{2,1,0:T(8,128)(2,1)S(1)}, u32[]{:S(2)}, u32[]{:S(2)}) async-start(bf16[16,36,128]{2,1,0:T(8,128)(2,1)} %broadcast_in_dim.45), calls=%async_computation.1 | async-start | bytes 327680 | tf_op jit(solution)/shard_map/all_to_all | solution.py:46
  27.7 4.5 %fusion.15 = f32[9,128,128,1]{2,0,1,3:T(8,128)S(1)} fusion(bf16[1,1,128,128,128]{4,3,2,1,0:T(8,128)(2,1)} %param.11, bf16[128,9,128]{2,1,0:T(8,128)(2,1)S(1)} %gather_fusion.3, f32[128]{0:T(128)S(1)} %compare_convert_fusion, pred[128]{0:T(512)(128)(4,1)S(1)} %get-tuple-element.37), kind=kOutput, calls=%fused_computation.22 | convolution fusion | flops 38043648 | bytes 5079680 | tf_op jit(solution)/shard_map/sut,cst->csu/dot_general | solution.py:81
  32.8 2.7 %all-to-all-done.1 = bf16[16,36,128]{2,1,0:T(8,128)(2,1)S(1)} async-done(((bf16[16,36,128]{2,1,0:T(8,128)(2,1)}), bf16[16,36,128]{2,1,0:T(8,128)(2,1)S(1)}, u32[]{:S(2)}, u32[]{:S(2)}) %all-to-all-start.1) | async-done | bytes 147488 | tf_op jit(solution)/shard_map/all_to_all | solution.py:46
  36.1 0.8 reshape.329
  36.9 6.3 %all-to-all-start.2 = ((f32[16,36,128]{2,1,0:T(8,128)}), f32[16,36,128]{2,1,0:T(8,128)S(1)}, u32[]{:S(2)}, u32[]{:S(2)}) async-start(f32[16,36,128]{2,1,0:T(8,128)} %reshape.329), calls=%async_computation.2 | async-start | bytes 655360 | tf_op jit(solution)/shard_map/all_to_all | solution.py:51
  44.2 3.5 %fusion.21 = f32[9,128,128,1]{2,0,1,3:T(8,128)S(1)} fusion(bf16[1,1,128,128,128]{4,3,2,1,0:T(8,128)(2,1)} %param.11, bf16[128,9,128]{2,1,0:T(8,128)(2,1)S(1)} %gather_fusion.4, f32[128]{0:T(128)S(1)} %compare_select_fusion.1, pred[128]{0:T(512)(128)(4,1)S(1)} %get-tuple-element.29), kind=kOutput, calls=%fused_computation.24 | convolution fusion | flops 38043648 | bytes 5079680 | tf_op jit(solution)/shard_map/sut,csu->cst/dot_general | solution.py:93
  48.2 5.8 %all-to-all-done.2 = f32[16,36,128]{2,1,0:T(8,128)S(1)} async-done(((f32[16,36,128]{2,1,0:T(8,128)}), f32[16,36,128]{2,1,0:T(8,128)S(1)}, u32[]{:S(2)}, u32[]{:S(2)}) %all-to-all-start.2) | async-done | bytes 294944 | tf_op jit(solution)/shard_map/all_to_all | solution.py:51
  54.2 0.8 reshape.333
  55.0 6.4 %all-to-all-start.3 = ((f32[16,36,128]{2,1,0:T(8,128)}), f32[16,36,128]{2,1,0:T(8,128)S(1)}, u32[]{:S(2)}, u32[]{:S(2)}) async-start(f32[16,36,128]{2,1,0:T(8,128)} %reshape.333), calls=%async_computation.3 | async-start | bytes 655360 | tf_op jit(solution)/shard_map/all_to_all | solution.py:51
  61.6 7.5 %all-to-all-done.3 = f32[16,36,128]{2,1,0:T(8,128)S(1)} async-done(((f32[16,36,128]{2,1,0:T(8,128)}), f32[16,36,128]{2,1,0:T(8,128)S(1)}, u32[]{:S(2)}, u32[]{:S(2)}) %all-to-all-start.3) | async-done | bytes 294944 | tf_op jit(solution)/shard_map/all_to_all | solution.py:51
  69.5 0.7 broadcast_in_dim.46
  70.2 6.6 %all-to-all-start.4 = ((f32[256,1,128]{2,1,0:T(1,128)}), f32[256,1,128]{2,1,0:T(1,128)S(1)}, u32[]{:S(2)}, u32[]{:S(2)}) async-start(f32[256,1,128]{2,1,0:T(1,128)} %broadcast_in_dim.46), calls=%async_computation.4 | async-start | bytes 262144 | tf_op jit(solution)/shard_map/all_to_all | solution.py:62
  76.8 12.6 %all-to-all-done.4 = f32[256,1,128]{2,1,0:T(1,128)S(1)} async-done(((f32[256,1,128]{2,1,0:T(1,128)}), f32[256,1,128]{2,1,0:T(1,128)S(1)}, u32[]{:S(2)}, u32[]{:S(2)}) %all-to-all-start.4) | async-done | bytes 131104 | tf_op jit(solution)/shard_map/all_to_all | solution.py:62
  94.6 4.4 %all-to-all-start.5 = ((bf16[16,32,128]{2,1,0:T(8,128)(2,1)}), bf16[16,32,128]{2,1,0:T(8,128)(2,1)S(1)}, u32[]{:S(2)}, u32[]{:S(2)}) async-start(bf16[16,32,128]{2,1,0:T(8,128)(2,1)} %broadcast_in_dim.49), calls=%async_computation.5 | async-start | bytes 262144 | tf_op jit(solution)/shard_map/all_to_all | solution.py:46
  99.1 6.0 %all-to-all-done.5 = bf16[16,32,128]{2,1,0:T(8,128)(2,1)S(1)} async-done(((bf16[16,32,128]{2,1,0:T(8,128)(2,1)}), bf16[16,32,128]{2,1,0:T(8,128)(2,1)S(1)}, u32[]{:S(2)}, u32[]{:S(2)}) %all-to-all-start.5) | async-done | bytes 131104 | tf_op jit(solution)/shard_map/all_to_all | solution.py:46
  105.2 3.5 %all-to-all-start.6 = ((bf16[16,32,128]{2,1,0:T(8,128)(2,1)}), bf16[16,32,128]{2,1,0:T(8,128)(2,1)S(1)}, u32[]{:S(2)}, u32[]{:S(2)}) async-start(bf16[16,32,128]{2,1,0:T(8,128)(2,1)} %broadcast_in_dim.49), calls=%async_computation.6 | async-start | bytes 262144 | tf_op jit(solution)/shard_map/all_to_all | solution.py:46
  109.5 4.5 %fusion.27 = f32[8,128,128,1]{2,0,1,3:T(8,128)S(1)} fusion(bf16[1,1,128,128,128]{4,3,2,1,0:T(8,128)(2,1)} %param.11, bf16[128,8,128]{2,1,0:T(8,128)(2,1)S(1)} %gather_fusion.5, f32[128]{0:T(128)S(1)} %compare_convert_fusion, pred[128]{0:T(512)(128)(4,1)S(1)} %get-tuple-element.37), kind=kOutput, calls=%fused_computation.26 | convolution fusion | flops 33816576 | bytes 4981376 | tf_op jit(solution)/shard_map/sut,cst->csu/dot_general | solution.py:81
  114.3 0.8 copy.150
  115.2 2.5 all-to-all-done.6
  117.8 6.6 %all-to-all-start.7 = ((f32[16,8,512]{2,1,0:T(8,128)}), f32[16,8,512]{2,1,0:T(8,128)S(1)}, u32[]{:S(2)}, u32[]{:S(2)}) async-start(f32[16,8,512]{2,1,0:T(8,128)} %bitcast.239), calls=%async_computation.7 | async-start | bytes 524288 | tf_op jit(solution)/shard_map/all_to_all | solution.py:51
  125.0 3.4 %fusion.33 = f32[8,128,128,1]{2,0,1,3:T(8,128)S(1)} fusion(bf16[1,1,128,128,128]{4,3,2,1,0:T(8,128)(2,1)} %param.11, bf16[128,8,128]{2,1,0:T(8,128)(2,1)S(1)} %gather_fusion.6, f32[128]{0:T(128)S(1)} %compare_select_fusion.1, pred[128]{0:T(512)(128)(4,1)S(1)} %get-tuple-element.29), kind=kOutput, calls=%fused_computation.28 | convolution fusion | flops 33816576 | bytes 4981376 | tf_op jit(solution)/shard_map/sut,csu->cst/dot_general | solution.py:93
  128.8 0.9 copy.149
  129.7 4.2 %all-to-all-done.7 = f32[16,8,512]{2,1,0:T(8,128)S(1)} async-done(((f32[16,8,512]{2,1,0:T(8,128)}), f32[16,8,512]{2,1,0:T(8,128)S(1)}, u32[]{:S(2)}, u32[]{:S(2)}) %all-to-all-start.7) | async-done | bytes 262176 | tf_op jit(solution)/shard_map/all_to_all | solution.py:51
  133.9 6.3 %all-to-all-start.8 = ((f32[16,8,512]{2,1,0:T(8,128)}), f32[16,8,512]{2,1,0:T(8,128)S(1)}, u32[]{:S(2)}, u32[]{:S(2)}) async-start(f32[16,8,512]{2,1,0:T(8,128)} %bitcast.238), calls=%async_computation.8 | async-start | bytes 524288 | tf_op jit(solution)/shard_map/all_to_all | solution.py:51
  140.6 6.9 %all-to-all-done.8 = f32[16,8,512]{2,1,0:T(8,128)S(1)} async-done(((f32[16,8,512]{2,1,0:T(8,128)}), f32[16,8,512]{2,1,0:T(8,128)S(1)}, u32[]{:S(2)}, u32[]{:S(2)}) %all-to-all-start.8) | async-done | bytes 262176 | tf_op jit(solution)/shard_map/all_to_all | solution.py:51
  147.9 0.7 broadcast_in_dim.50
  148.6 6.3 %all-to-all-start.9 = ((f32[256,1,128]{2,1,0:T(1,128)}), f32[256,1,128]{2,1,0:T(1,128)S(1)}, u32[]{:S(2)}, u32[]{:S(2)}) async-start(f32[256,1,128]{2,1,0:T(1,128)} %broadcast_in_dim.50), calls=%async_computation.9 | async-start | bytes 262144 | tf_op jit(solution)/shard_map/all_to_all | solution.py:62
  155.4 12.2 %all-to-all-done.9 = f32[256,1,128]{2,1,0:T(1,128)S(1)} async-done(((f32[256,1,128]{2,1,0:T(1,128)}), f32[256,1,128]{2,1,0:T(1,128)S(1)}, u32[]{:S(2)}, u32[]{:S(2)}) %all-to-all-start.9) | async-done | bytes 131104 | tf_op jit(solution)/shard_map/all_to_all | solution.py:62
  172.7 4.4 %all-to-all-start.10 = ((bf16[16,32,128]{2,1,0:T(8,128)(2,1)}), bf16[16,32,128]{2,1,0:T(8,128)(2,1)S(1)}, u32[]{:S(2)}, u32[]{:S(2)}) async-start(bf16[16,32,128]{2,1,0:T(8,128)(2,1)} %broadcast_in_dim.52), calls=%async_computation.10 | async-start | bytes 262144 | tf_op jit(solution)/shard_map/all_to_all | solution.py:46
  177.5 5.9 %all-to-all-done.10 = bf16[16,32,128]{2,1,0:T(8,128)(2,1)S(1)} async-done(((bf16[16,32,128]{2,1,0:T(8,128)(2,1)}), bf16[16,32,128]{2,1,0:T(8,128)(2,1)S(1)}, u32[]{:S(2)}, u32[]{:S(2)}) %all-to-all-start.10) | async-done | bytes 131104 | tf_op jit(solution)/shard_map/all_to_all | solution.py:46
  183.3 3.5 %all-to-all-start.11 = ((bf16[16,32,128]{2,1,0:T(8,128)(2,1)}), bf16[16,32,128]{2,1,0:T(8,128)(2,1)S(1)}, u32[]{:S(2)}, u32[]{:S(2)}) async-start(bf16[16,32,128]{2,1,0:T(8,128)(2,1)} %broadcast_in_dim.52), calls=%async_computation.11 | async-start | bytes 262144 | tf_op jit(solution)/shard_map/all_to_all | solution.py:46
  187.6 4.5 %fusion.39 = f32[8,128,128,1]{2,0,1,3:T(8,128)S(1)} fusion(bf16[1,1,128,128,128]{4,3,2,1,0:T(8,128)(2,1)} %param.11, bf16[128,8,128]{2,1,0:T(8,128)(2,1)S(1)} %gather_fusion.7, f32[128]{0:T(128)S(1)} %compare_convert_fusion, pred[128]{0:T(512)(128)(4,1)S(1)} %get-tuple-element.37), kind=kOutput, calls=%fused_computation.30 | convolution fusion | flops 33816576 | bytes 4981376 | tf_op jit(solution)/shard_map/sut,cst->csu/dot_general | solution.py:81
  192.5 0.8 copy.148
  193.4 2.5 all-to-all-done.11
  195.9 6.6 %all-to-all-start.12 = ((f32[16,8,512]{2,1,0:T(8,128)}), f32[16,8,512]{2,1,0:T(8,128)S(1)}, u32[]{:S(2)}, u32[]{:S(2)}) async-start(f32[16,8,512]{2,1,0:T(8,128)} %bitcast.237), calls=%async_computation.12 | async-start | bytes 524288 | tf_op jit(solution)/shard_map/all_to_all | solution.py:51
  203.2 3.4 %fusion.45 = f32[8,128,128,1]{2,0,1,3:T(8,128)S(1)} fusion(bf16[1,1,128,128,128]{4,3,2,1,0:T(8,128)(2,1)} %param.11, bf16[128,8,128]{2,1,0:T(8,128)(2,1)S(1)} %gather_fusion.8, f32[128]{0:T(128)S(1)} %compare_select_fusion.1, pred[128]{0:T(512)(128)(4,1)S(1)} %get-tuple-element.29), kind=kOutput, calls=%fused_computation.32 | convolution fusion | flops 33816576 | bytes 4981376 | tf_op jit(solution)/shard_map/sut,csu->cst/dot_general | solution.py:93
  207.0 0.9 copy.147
  207.9 4.2 %all-to-all-done.12 = f32[16,8,512]{2,1,0:T(8,128)S(1)} async-done(((f32[16,8,512]{2,1,0:T(8,128)}), f32[16,8,512]{2,1,0:T(8,128)S(1)}, u32[]{:S(2)}, u32[]{:S(2)}) %all-to-all-start.12) | async-done | bytes 262176 | tf_op jit(solution)/shard_map/all_to_all | solution.py:51
  212.1 6.3 %all-to-all-start.13 = ((f32[16,8,512]{2,1,0:T(8,128)}), f32[16,8,512]{2,1,0:T(8,128)S(1)}, u32[]{:S(2)}, u32[]{:S(2)}) async-start(f32[16,8,512]{2,1,0:T(8,128)} %bitcast.236), calls=%async_computation.13 | async-start | bytes 524288 | tf_op jit(solution)/shard_map/all_to_all | solution.py:51
  218.7 6.9 %all-to-all-done.13 = f32[16,8,512]{2,1,0:T(8,128)S(1)} async-done(((f32[16,8,512]{2,1,0:T(8,128)}), f32[16,8,512]{2,1,0:T(8,128)S(1)}, u32[]{:S(2)}, u32[]{:S(2)}) %all-to-all-start.13) | async-done | bytes 262176 | tf_op jit(solution)/shard_map/all_to_all | solution.py:51
  226.2 18.8 %all_to_all.78 = f32[256,1,128]{2,1,0:T(1,128)S(1)} all-to-all(f32[256,1,128]{2,1,0:T(1,128)S(1)} %broadcast_in_dim.53), channel_id=1, replica_groups=mesh['row'=16,'col'=16] {'row','col'}, dimensions={0} | all-to-all | bytes 262144 | tf_op jit(solution)/shard_map/all_to_all | solution.py:62
  248.6 0.8 fusion.191
  249.6 0.7 fusion.193
  (145 shorter events, 27.4 us)
Async XLA Ops:
  2.8 13.2 %all-to-all-start = ((bf16[16,36,128]{2,1,0:T(8,128)(2,1)}), bf16[16,36,128]{2,1,0:T(8,128)(2,1)S(1)}, u32[]{:S(2)}, u32[]{:S(2)}) async-start(bf16[16,36,128]{2,1,0:T(8,128)(2,1)} %broadcast_in_dim.45), calls=%async_computation | async-start | bytes 327680 | tf_op jit(solution)/shard_map/all_to_all | solution.py:46
  16.0 19.6 %all-to-all-start.1 = ((bf16[16,36,128]{2,1,0:T(8,128)(2,1)}), bf16[16,36,128]{2,1,0:T(8,128)(2,1)S(1)}, u32[]{:S(2)}, u32[]{:S(2)}) async-start(bf16[16,36,128]{2,1,0:T(8,128)(2,1)} %broadcast_in_dim.45), calls=%async_computation.1 | async-start | bytes 327680 | tf_op jit(solution)/shard_map/all_to_all | solution.py:46
  32.3 11.0 %copy-start.2 = (s32[1,1,2,128]{3,2,1,0:T(2,128)S(1)}, s32[1,1,2,128]{3,2,1,0:T(2,128)}, u32[]{:S(2)}) copy-start(s32[1,1,2,128]{3,2,1,0:T(2,128)} %param.12) | copy-start | bytes 3076
  36.9 17.1 %all-to-all-start.2 = ((f32[16,36,128]{2,1,0:T(8,128)}), f32[16,36,128]{2,1,0:T(8,128)S(1)}, u32[]{:S(2)}, u32[]{:S(2)}) async-start(f32[16,36,128]{2,1,0:T(8,128)} %reshape.329), calls=%async_computation.2 | async-start | bytes 655360 | tf_op jit(solution)/shard_map/all_to_all | solution.py:51
  44.2 17.2 %copy-start = (f32[8,512]{1,0:T(8,128)S(1)}, f32[8,512]{1,0:T(8,128)}, u32[]{:S(2)}) copy-start(f32[8,512]{1,0:T(8,128)} %param.15) | copy-start | bytes 49156
  44.2 32.6 %copy-start.1 = (f32[2,8,24]{2,1,0:T(8,128)S(1)}, f32[2,8,24]{2,1,0:T(8,128)}, u32[]{:S(2)}) copy-start(f32[2,8,24]{2,1,0:T(8,128)} %param.16) | copy-start | bytes 4612
  55.0 14.1 %all-to-all-start.3 = ((f32[16,36,128]{2,1,0:T(8,128)}), f32[16,36,128]{2,1,0:T(8,128)S(1)}, u32[]{:S(2)}, u32[]{:S(2)}) async-start(f32[16,36,128]{2,1,0:T(8,128)} %reshape.333), calls=%async_computation.3 | async-start | bytes 655360 | tf_op jit(solution)/shard_map/all_to_all | solution.py:51
  70.2 19.2 %all-to-all-start.4 = ((f32[256,1,128]{2,1,0:T(1,128)}), f32[256,1,128]{2,1,0:T(1,128)S(1)}, u32[]{:S(2)}, u32[]{:S(2)}) async-start(f32[256,1,128]{2,1,0:T(1,128)} %broadcast_in_dim.46), calls=%async_computation.4 | async-start | bytes 262144 | tf_op jit(solution)/shard_map/all_to_all | solution.py:62
  94.6 10.6 %all-to-all-start.5 = ((bf16[16,32,128]{2,1,0:T(8,128)(2,1)}), bf16[16,32,128]{2,1,0:T(8,128)(2,1)S(1)}, u32[]{:S(2)}, u32[]{:S(2)}) async-start(bf16[16,32,128]{2,1,0:T(8,128)(2,1)} %broadcast_in_dim.49), calls=%async_computation.5 | async-start | bytes 262144 | tf_op jit(solution)/shard_map/all_to_all | solution.py:46
  105.2 12.5 %all-to-all-start.6 = ((bf16[16,32,128]{2,1,0:T(8,128)(2,1)}), bf16[16,32,128]{2,1,0:T(8,128)(2,1)S(1)}, u32[]{:S(2)}, u32[]{:S(2)}) async-start(bf16[16,32,128]{2,1,0:T(8,128)(2,1)} %broadcast_in_dim.49), calls=%async_computation.6 | async-start | bytes 262144 | tf_op jit(solution)/shard_map/all_to_all | solution.py:46
  117.8 16.2 %all-to-all-start.7 = ((f32[16,8,512]{2,1,0:T(8,128)}), f32[16,8,512]{2,1,0:T(8,128)S(1)}, u32[]{:S(2)}, u32[]{:S(2)}) async-start(f32[16,8,512]{2,1,0:T(8,128)} %bitcast.239), calls=%async_computation.7 | async-start | bytes 524288 | tf_op jit(solution)/shard_map/all_to_all | solution.py:51
  133.9 13.5 %all-to-all-start.8 = ((f32[16,8,512]{2,1,0:T(8,128)}), f32[16,8,512]{2,1,0:T(8,128)S(1)}, u32[]{:S(2)}, u32[]{:S(2)}) async-start(f32[16,8,512]{2,1,0:T(8,128)} %bitcast.238), calls=%async_computation.8 | async-start | bytes 524288 | tf_op jit(solution)/shard_map/all_to_all | solution.py:51
  148.6 18.9 %all-to-all-start.9 = ((f32[256,1,128]{2,1,0:T(1,128)}), f32[256,1,128]{2,1,0:T(1,128)S(1)}, u32[]{:S(2)}, u32[]{:S(2)}) async-start(f32[256,1,128]{2,1,0:T(1,128)} %broadcast_in_dim.50), calls=%async_computation.9 | async-start | bytes 262144 | tf_op jit(solution)/shard_map/all_to_all | solution.py:62
  172.7 10.6 %all-to-all-start.10 = ((bf16[16,32,128]{2,1,0:T(8,128)(2,1)}), bf16[16,32,128]{2,1,0:T(8,128)(2,1)S(1)}, u32[]{:S(2)}, u32[]{:S(2)}) async-start(bf16[16,32,128]{2,1,0:T(8,128)(2,1)} %broadcast_in_dim.52), calls=%async_computation.10 | async-start | bytes 262144 | tf_op jit(solution)/shard_map/all_to_all | solution.py:46
  183.3 12.5 %all-to-all-start.11 = ((bf16[16,32,128]{2,1,0:T(8,128)(2,1)}), bf16[16,32,128]{2,1,0:T(8,128)(2,1)S(1)}, u32[]{:S(2)}, u32[]{:S(2)}) async-start(bf16[16,32,128]{2,1,0:T(8,128)(2,1)} %broadcast_in_dim.52), calls=%async_computation.11 | async-start | bytes 262144 | tf_op jit(solution)/shard_map/all_to_all | solution.py:46
  195.9 16.2 %all-to-all-start.12 = ((f32[16,8,512]{2,1,0:T(8,128)}), f32[16,8,512]{2,1,0:T(8,128)S(1)}, u32[]{:S(2)}, u32[]{:S(2)}) async-start(f32[16,8,512]{2,1,0:T(8,128)} %bitcast.237), calls=%async_computation.12 | async-start | bytes 524288 | tf_op jit(solution)/shard_map/all_to_all | solution.py:51
  212.1 13.5 %all-to-all-start.13 = ((f32[16,8,512]{2,1,0:T(8,128)}), f32[16,8,512]{2,1,0:T(8,128)S(1)}, u32[]{:S(2)}, u32[]{:S(2)}) async-start(f32[16,8,512]{2,1,0:T(8,128)} %bitcast.236), calls=%async_computation.13 | async-start | bytes 524288 | tf_op jit(solution)/shard_map/all_to_all | solution.py:51

commit v9 on v7

--- a/solution.py
+++ b/solution.py
@@ -12,7 +12,7 @@
     order_size = lower_factor.shape[0]
     assert order_size <= 8
     identity = jnp.eye(order_size, dtype=lower_factor.dtype)
-    diagonal = jnp.diagonal(lower_factor)
+    diagonal = jnp.sum(lower_factor * identity, axis=1)
     strict = lower_factor / diagonal[:, None] - identity
     square = matmul_high(strict, strict)
     fourth = matmul_high(square, square)

time: 251 us -> 254 us (1.012)
  matrix products: 33.7 us -> 37.5 us
    dot_general x40, matrix products: 7.33 us -> 11.2 us  [matmul_high(): return jnp.dot(left, right, precision=lax.Precision.HIGHEST)]
where the time goes in v9:
time: 254 us; the launch traced here: 252 us
  starting transfers between devices  84.3 us (33%)
  waiting for transfers between devices  84.2 us (33%)
  matrix products  37.5 us (15%)
  blocking collectives  18.8 us (7%)
  local copies, waits for them, and re-layouts  16.1 us (6%)
  other arithmetic  9.49 us (4%)
    all_to_all x6, starting transfers between devices, scatter_sum_by_exchange(): held = lax.all_to_all(dense_rows(chunks), axis, 0, 0, tiled=True)  38.1 us
    all_to_all x6, waiting for transfers between devices, scatter_sum_by_exchange(): held = lax.all_to_all(dense_rows(chunks), axis, 0, 0, tiled=True)  35.5 us
    all_to_all x6, starting transfers between devices, gather_by_exchange(): lax.all_to_all(dense_rows(copies), axis, 0, 0, tiled=True)  33.3 us
    all_to_all x2, waiting for transfers between devices, gram_sums(): held = lax.all_to_all(copies, ('row', 'col'), 0, 0, tiled=True)  24.8 us
    all_to_all x6, waiting for transfers between devices, gather_by_exchange(): lax.all_to_all(dense_rows(copies), axis, 0, 0, tiled=True)  23.9 us
    all_to_all x1, blocking collectives, gram_sums(): held = lax.all_to_all(copies, ('row', 'col'), 0, 0, tiled=True)  18.8 us
    dot_general x3, matrix products, direct_terms(): jnp.einsum('sut,cst->csu', part_tiles, col_values, preferred_element_type...  13.5 us
    all_to_all x2, starting transfers between devices, gram_sums(): held = lax.all_to_all(copies, ('row', 'col'), 0, 0, tiled=True)  12.9 us
  transfers between devices with their start and end apart: 14, of which 14 were waited for; matrix products, arithmetic and copies ran while one was open for 15% of the time, Pallas kernels for 0%

profile of v9, /device:TPU:1, one launch (start us, length us, event | category | flops | bytes accessed | tf_op | source)
XLA Modules:
  0.0 252.1 jit_solution(15687995188743232205)
XLA Ops:
  2.8 6.8 %all-to-all-start = ((bf16[16,36,128]{2,1,0:T(8,128)(2,1)}), bf16[16,36,128]{2,1,0:T(8,128)(2,1)S(1)}, u32[]{:S(2)}, u32[]{:S(2)}) async-start(bf16[16,36,128]{2,1,0:T(8,128)(2,1)} %broadcast_in_dim.30), calls=%async_computation | async-start | bytes 327680 | tf_op jit(solution)/shard_map/all_to_all | solution.py:46
  9.6 0.8 compare_and_fusion
  11.8 4.2 %all-to-all-done = bf16[16,36,128]{2,1,0:T(8,128)(2,1)S(1)} async-done(((bf16[16,36,128]{2,1,0:T(8,128)(2,1)}), bf16[16,36,128]{2,1,0:T(8,128)(2,1)S(1)}, u32[]{:S(2)}, u32[]{:S(2)}) %all-to-all-start) | async-done | bytes 147488 | tf_op jit(solution)/shard_map/all_to_all | solution.py:46
  16.0 10.6 %all-to-all-start.1 = ((bf16[16,36,128]{2,1,0:T(8,128)(2,1)}), bf16[16,36,128]{2,1,0:T(8,128)(2,1)S(1)}, u32[]{:S(2)}, u32[]{:S(2)}) async-start(bf16[16,36,128]{2,1,0:T(8,128)(2,1)} %broadcast_in_dim.30), calls=%async_computation.1 | async-start | bytes 327680 | tf_op jit(solution)/shard_map/all_to_all | solution.py:46
  27.7 4.5 %fusion.15 = f32[9,128,128,1]{2,0,1,3:T(8,128)S(1)} fusion(bf16[1,1,128,128,128]{4,3,2,1,0:T(8,128)(2,1)} %param.11, bf16[128,9,128]{2,1,0:T(8,128)(2,1)S(1)} %gather_fusion, f32[128]{0:T(128)S(1)} %compare_convert_fusion, pred[128]{0:T(512)(128)(4,1)S(1)} %get-tuple-element.37), kind=kOutput, calls=%fused_computation.19 | convolution fusion | flops 38043648 | bytes 5079680 | tf_op jit(solution)/shard_map/sut,cst->csu/dot_general | solution.py:81
  32.8 2.7 %all-to-all-done.1 = bf16[16,36,128]{2,1,0:T(8,128)(2,1)S(1)} async-done(((bf16[16,36,128]{2,1,0:T(8,128)(2,1)}), bf16[16,36,128]{2,1,0:T(8,128)(2,1)S(1)}, u32[]{:S(2)}, u32[]{:S(2)}) %all-to-all-start.1) | async-done | bytes 147488 | tf_op jit(solution)/shard_map/all_to_all | solution.py:46
  36.9 6.3 %all-to-all-start.2 = ((f32[16,36,128]{2,1,0:T(8,128)}), f32[16,36,128]{2,1,0:T(8,128)S(1)}, u32[]{:S(2)}, u32[]{:S(2)}) async-start(f32[16,36,128]{2,1,0:T(8,128)} %reshape.309), calls=%async_computation.2 | async-start | bytes 655360 | tf_op jit(solution)/shard_map/all_to_all | solution.py:51
  44.2 3.5 %fusion.21 = f32[9,128,128,1]{2,0,1,3:T(8,128)S(1)} fusion(bf16[1,1,128,128,128]{4,3,2,1,0:T(8,128)(2,1)} %param.11, bf16[128,9,128]{2,1,0:T(8,128)(2,1)S(1)} %gather_fusion.1, f32[128]{0:T(128)S(1)} %compare_select_fusion.1, pred[128]{0:T(512)(128)(4,1)S(1)} %get-tuple-element.29), kind=kOutput, calls=%fused_computation.21 | convolution fusion | flops 38043648 | bytes 5079680 | tf_op jit(solution)/shard_map/sut,csu->cst/dot_general | solution.py:93
  48.2 5.8 %all-to-all-done.2 = f32[16,36,128]{2,1,0:T(8,128)S(1)} async-done(((f32[16,36,128]{2,1,0:T(8,128)}), f32[16,36,128]{2,1,0:T(8,128)S(1)}, u32[]{:S(2)}, u32[]{:S(2)}) %all-to-all-start.2) | async-done | bytes 294944 | tf_op jit(solution)/shard_map/all_to_all | solution.py:51
  55.0 6.4 %all-to-all-start.3 = ((f32[16,36,128]{2,1,0:T(8,128)}), f32[16,36,128]{2,1,0:T(8,128)S(1)}, u32[]{:S(2)}, u32[]{:S(2)}) async-start(f32[16,36,128]{2,1,0:T(8,128)} %reshape.313), calls=%async_computation.3 | async-start | bytes 655360 | tf_op jit(solution)/shard_map/all_to_all | solution.py:51
  61.6 7.5 %all-to-all-done.3 = f32[16,36,128]{2,1,0:T(8,128)S(1)} async-done(((f32[16,36,128]{2,1,0:T(8,128)}), f32[16,36,128]{2,1,0:T(8,128)S(1)}, u32[]{:S(2)}, u32[]{:S(2)}) %all-to-all-start.3) | async-done | bytes 294944 | tf_op jit(solution)/shard_map/all_to_all | solution.py:51
  70.2 6.6 %all-to-all-start.4 = ((f32[256,1,128]{2,1,0:T(1,128)}), f32[256,1,128]{2,1,0:T(1,128)S(1)}, u32[]{:S(2)}, u32[]{:S(2)}) async-start(f32[256,1,128]{2,1,0:T(1,128)} %broadcast_in_dim.31), calls=%async_computation.4 | async-start | bytes 262144 | tf_op jit(solution)/shard_map/all_to_all | solution.py:62
  76.8 12.6 %all-to-all-done.4 = f32[256,1,128]{2,1,0:T(1,128)S(1)} async-done(((f32[256,1,128]{2,1,0:T(1,128)}), f32[256,1,128]{2,1,0:T(1,128)S(1)}, u32[]{:S(2)}, u32[]{:S(2)}) %all-to-all-start.4) | async-done | bytes 131104 | tf_op jit(solution)/shard_map/all_to_all | solution.py:62
  91.1 0.8 select_reduce_fusion.5
  91.8 0.8 fusion.174
  92.7 0.9 fusion.146
  95.3 4.4 %all-to-all-start.5 = ((bf16[16,8,512]{2,1,0:T(8,128)(2,1)}), bf16[16,8,512]{2,1,0:T(8,128)(2,1)S(1)}, u32[]{:S(2)}, u32[]{:S(2)}) async-start(bf16[16,8,512]{2,1,0:T(8,128)(2,1)} %broadcast_in_dim.33), calls=%async_computation.5 | async-start | bytes 262144 | tf_op jit(solution)/shard_map/all_to_all | solution.py:46
  99.8 6.0 %all-to-all-done.5 = bf16[16,8,512]{2,1,0:T(8,128)(2,1)S(1)} async-done(((bf16[16,8,512]{2,1,0:T(8,128)(2,1)}), bf16[16,8,512]{2,1,0:T(8,128)(2,1)S(1)}, u32[]{:S(2)}, u32[]{:S(2)}) %all-to-all-start.5) | async-done | bytes 131104 | tf_op jit(solution)/shard_map/all_to_all | solution.py:46
  105.9 3.5 %all-to-all-start.6 = ((bf16[16,8,512]{2,1,0:T(8,128)(2,1)}), bf16[16,8,512]{2,1,0:T(8,128)(2,1)S(1)}, u32[]{:S(2)}, u32[]{:S(2)}) async-start(bf16[16,8,512]{2,1,0:T(8,128)(2,1)} %broadcast_in_dim.33), calls=%async_computation.6 | async-start | bytes 262144 | tf_op jit(solution)/shard_map/all_to_all | solution.py:46
  110.1 4.5 %fusion.27 = f32[8,128,128,1]{2,0,1,3:T(8,128)S(1)} fusion(bf16[1,1,128,128,128]{4,3,2,1,0:T(8,128)(2,1)} %param.11, bf16[128,8,128]{2,1,0:T(8,128)(2,1)S(1)} %gather_fusion.2, f32[128]{0:T(128)S(1)} %compare_convert_fusion, pred[128]{0:T(512)(128)(4,1)S(1)} %get-tuple-element.37), kind=kOutput, calls=%fused_computation.23 | convolution fusion | flops 33816576 | bytes 4981376 | tf_op jit(solution)/shard_map/sut,cst->csu/dot_general | solution.py:81
  115.0 0.8 copy.173
  115.8 2.6 %all-to-all-done.6 = bf16[16,8,512]{2,1,0:T(8,128)(2,1)S(1)} async-done(((bf16[16,8,512]{2,1,0:T(8,128)(2,1)}), bf16[16,8,512]{2,1,0:T(8,128)(2,1)S(1)}, u32[]{:S(2)}, u32[]{:S(2)}) %all-to-all-start.6) | async-done | bytes 131104 | tf_op jit(solution)/shard_map/all_to_all | solution.py:46
  118.4 6.5 %all-to-all-start.7 = ((f32[16,8,512]{2,1,0:T(8,128)}), f32[16,8,512]{2,1,0:T(8,128)S(1)}, u32[]{:S(2)}, u32[]{:S(2)}) async-start(f32[16,8,512]{2,1,0:T(8,128)} %bitcast.237), calls=%async_computation.7 | async-start | bytes 524288 | tf_op jit(solution)/shard_map/all_to_all | solution.py:51
  125.5 3.4 %fusion.33 = f32[8,128,128,1]{2,0,1,3:T(8,128)S(1)} fusion(bf16[1,1,128,128,128]{4,3,2,1,0:T(8,128)(2,1)} %param.11, bf16[128,8,128]{2,1,0:T(8,128)(2,1)S(1)} %gather_fusion.3, f32[128]{0:T(128)S(1)} %compare_select_fusion.1, pred[128]{0:T(512)(128)(4,1)S(1)} %get-tuple-element.29), kind=kOutput, calls=%fused_computation.25 | convolution fusion | flops 33816576 | bytes 4981376 | tf_op jit(solution)/shard_map/sut,csu->cst/dot_general | solution.py:93
  129.4 0.9 copy.172
  130.2 4.2 %all-to-all-done.7 = f32[16,8,512]{2,1,0:T(8,128)S(1)} async-done(((f32[16,8,512]{2,1,0:T(8,128)}), f32[16,8,512]{2,1,0:T(8,128)S(1)}, u32[]{:S(2)}, u32[]{:S(2)}) %all-to-all-start.7) | async-done | bytes 262176 | tf_op jit(solution)/shard_map/all_to_all | solution.py:51
  134.4 6.3 %all-to-all-start.8 = ((f32[16,8,512]{2,1,0:T(8,128)}), f32[16,8,512]{2,1,0:T(8,128)S(1)}, u32[]{:S(2)}, u32[]{:S(2)}) async-start(f32[16,8,512]{2,1,0:T(8,128)} %bitcast.236), calls=%async_computation.8 | async-start | bytes 524288 | tf_op jit(solution)/shard_map/all_to_all | solution.py:51
  141.1 6.9 %all-to-all-done.8 = f32[16,8,512]{2,1,0:T(8,128)S(1)} async-done(((f32[16,8,512]{2,1,0:T(8,128)}), f32[16,8,512]{2,1,0:T(8,128)S(1)}, u32[]{:S(2)}, u32[]{:S(2)}) %all-to-all-start.8) | async-done | bytes 262176 | tf_op jit(solution)/shard_map/all_to_all | solution.py:51
  149.2 6.3 %all-to-all-start.9 = ((f32[256,1,128]{2,1,0:T(1,128)}), f32[256,1,128]{2,1,0:T(1,128)S(1)}, u32[]{:S(2)}, u32[]{:S(2)}) async-start(f32[256,1,128]{2,1,0:T(1,128)} %broadcast_in_dim.34), calls=%async_computation.9 | async-start | bytes 262144 | tf_op jit(solution)/shard_map/all_to_all | solution.py:62
  155.9 12.2 %all-to-all-done.9 = f32[256,1,128]{2,1,0:T(1,128)S(1)} async-done(((f32[256,1,128]{2,1,0:T(1,128)}), f32[256,1,128]{2,1,0:T(1,128)S(1)}, u32[]{:S(2)}, u32[]{:S(2)}) %all-to-all-start.9) | async-done | bytes 131104 | tf_op jit(solution)/shard_map/all_to_all | solution.py:62
  170.5 0.8 fusion.175
  171.4 0.9 fusion.147
  174.0 4.4 %all-to-all-start.10 = ((bf16[16,8,512]{2,1,0:T(8,128)(2,1)}), bf16[16,8,512]{2,1,0:T(8,128)(2,1)S(1)}, u32[]{:S(2)}, u32[]{:S(2)}) async-start(bf16[16,8,512]{2,1,0:T(8,128)(2,1)} %broadcast_in_dim.35), calls=%async_computation.10 | async-start | bytes 262144 | tf_op jit(solution)/shard_map/all_to_all | solution.py:46
  178.7 5.9 %all-to-all-done.10 = bf16[16,8,512]{2,1,0:T(8,128)(2,1)S(1)} async-done(((bf16[16,8,512]{2,1,0:T(8,128)(2,1)}), bf16[16,8,512]{2,1,0:T(8,128)(2,1)S(1)}, u32[]{:S(2)}, u32[]{:S(2)}) %all-to-all-start.10) | async-done | bytes 131104 | tf_op jit(solution)/shard_map/all_to_all | solution.py:46
  184.6 3.5 %all-to-all-start.11 = ((bf16[16,8,512]{2,1,0:T(8,128)(2,1)}), bf16[16,8,512]{2,1,0:T(8,128)(2,1)S(1)}, u32[]{:S(2)}, u32[]{:S(2)}) async-start(bf16[16,8,512]{2,1,0:T(8,128)(2,1)} %broadcast_in_dim.35), calls=%async_computation.11 | async-start | bytes 262144 | tf_op jit(solution)/shard_map/all_to_all | solution.py:46
  188.8 4.5 %fusion.39 = f32[8,128,128,1]{2,0,1,3:T(8,128)S(1)} fusion(bf16[1,1,128,128,128]{4,3,2,1,0:T(8,128)(2,1)} %param.11, bf16[128,8,128]{2,1,0:T(8,128)(2,1)S(1)} %gather_fusion.4, f32[128]{0:T(128)S(1)} %compare_convert_fusion, pred[128]{0:T(512)(128)(4,1)S(1)} %get-tuple-element.37), kind=kOutput, calls=%fused_computation.27 | convolution fusion | flops 33816576 | bytes 4981376 | tf_op jit(solution)/shard_map/sut,cst->csu/dot_general | solution.py:81
  193.7 0.8 copy.171
  194.5 2.6 %all-to-all-done.11 = bf16[16,8,512]{2,1,0:T(8,128)(2,1)S(1)} async-done(((bf16[16,8,512]{2,1,0:T(8,128)(2,1)}), bf16[16,8,512]{2,1,0:T(8,128)(2,1)S(1)}, u32[]{:S(2)}, u32[]{:S(2)}) %all-to-all-start.11) | async-done | bytes 131104 | tf_op jit(solution)/shard_map/all_to_all | solution.py:46
  197.1 6.5 %all-to-all-start.12 = ((f32[16,8,512]{2,1,0:T(8,128)}), f32[16,8,512]{2,1,0:T(8,128)S(1)}, u32[]{:S(2)}, u32[]{:S(2)}) async-start(f32[16,8,512]{2,1,0:T(8,128)} %bitcast.235), calls=%async_computation.12 | async-start | bytes 524288 | tf_op jit(solution)/shard_map/all_to_all | solution.py:51
  204.2 3.4 %fusion.45 = f32[8,128,128,1]{2,0,1,3:T(8,128)S(1)} fusion(bf16[1,1,128,128,128]{4,3,2,1,0:T(8,128)(2,1)} %param.11, bf16[128,8,128]{2,1,0:T(8,128)(2,1)S(1)} %gather_fusion.5, f32[128]{0:T(128)S(1)} %compare_select_fusion.1, pred[128]{0:T(512)(128)(4,1)S(1)} %get-tuple-element.29), kind=kOutput, calls=%fused_computation.29 | convolution fusion | flops 33816576 | bytes 4981376 | tf_op jit(solution)/shard_map/sut,csu->cst/dot_general | solution.py:93
  208.1 0.9 copy.170
  208.9 4.2 %all-to-all-done.12 = f32[16,8,512]{2,1,0:T(8,128)S(1)} async-done(((f32[16,8,512]{2,1,0:T(8,128)}), f32[16,8,512]{2,1,0:T(8,128)S(1)}, u32[]{:S(2)}, u32[]{:S(2)}) %all-to-all-start.12) | async-done | bytes 262176 | tf_op jit(solution)/shard_map/all_to_all | solution.py:51
  213.2 6.3 %all-to-all-start.13 = ((f32[16,8,512]{2,1,0:T(8,128)}), f32[16,8,512]{2,1,0:T(8,128)S(1)}, u32[]{:S(2)}, u32[]{:S(2)}) async-start(f32[16,8,512]{2,1,0:T(8,128)} %bitcast.234), calls=%async_computation.13 | async-start | bytes 524288 | tf_op jit(solution)/shard_map/all_to_all | solution.py:51
  219.8 6.9 %all-to-all-done.13 = f32[16,8,512]{2,1,0:T(8,128)S(1)} async-done(((f32[16,8,512]{2,1,0:T(8,128)}), f32[16,8,512]{2,1,0:T(8,128)S(1)}, u32[]{:S(2)}, u32[]{:S(2)}) %all-to-all-start.13) | async-done | bytes 262176 | tf_op jit(solution)/shard_map/all_to_all | solution.py:51
  227.2 18.8 %all_to_all.78 = f32[256,1,128]{2,1,0:T(1,128)S(1)} all-to-all(f32[256,1,128]{2,1,0:T(1,128)S(1)} %broadcast_in_dim.36), channel_id=1, replica_groups=mesh['row'=16,'col'=16] {'row','col'}, dimensions={0} | all-to-all | bytes 262144 | tf_op jit(solution)/shard_map/all_to_all | solution.py:62
  248.4 0.8 fusion.176
  249.3 0.9 fusion.148
  250.4 0.8 fusion.191
  (135 shorter events, 28.6 us)
Async XLA Ops:
  2.8 13.2 %all-to-all-start = ((bf16[16,36,128]{2,1,0:T(8,128)(2,1)}), bf16[16,36,128]{2,1,0:T(8,128)(2,1)S(1)}, u32[]{:S(2)}, u32[]{:S(2)}) async-start(bf16[16,36,128]{2,1,0:T(8,128)(2,1)} %broadcast_in_dim.30), calls=%async_computation | async-start | bytes 327680 | tf_op jit(solution)/shard_map/all_to_all | solution.py:46
  16.0 19.6 %all-to-all-start.1 = ((bf16[16,36,128]{2,1,0:T(8,128)(2,1)}), bf16[16,36,128]{2,1,0:T(8,128)(2,1)S(1)}, u32[]{:S(2)}, u32[]{:S(2)}) async-start(bf16[16,36,128]{2,1,0:T(8,128)(2,1)} %broadcast_in_dim.30), calls=%async_computation.1 | async-start | bytes 327680 | tf_op jit(solution)/shard_map/all_to_all | solution.py:46
  32.3 11.0 %copy-start.2 = (s32[1,1,2,128]{3,2,1,0:T(2,128)S(1)}, s32[1,1,2,128]{3,2,1,0:T(2,128)}, u32[]{:S(2)}) copy-start(s32[1,1,2,128]{3,2,1,0:T(2,128)} %param.12) | copy-start | bytes 3076
  36.9 17.1 %all-to-all-start.2 = ((f32[16,36,128]{2,1,0:T(8,128)}), f32[16,36,128]{2,1,0:T(8,128)S(1)}, u32[]{:S(2)}, u32[]{:S(2)}) async-start(f32[16,36,128]{2,1,0:T(8,128)} %reshape.309), calls=%async_computation.2 | async-start | bytes 655360 | tf_op jit(solution)/shard_map/all_to_all | solution.py:51
  44.2 17.2 %copy-start = (f32[8,512]{1,0:T(8,128)S(1)}, f32[8,512]{1,0:T(8,128)}, u32[]{:S(2)}) copy-start(f32[8,512]{1,0:T(8,128)} %param.15) | copy-start | bytes 49156
  44.2 32.6 %copy-start.1 = (f32[2,8,24]{2,1,0:T(8,128)S(1)}, f32[2,8,24]{2,1,0:T(8,128)}, u32[]{:S(2)}) copy-start(f32[2,8,24]{2,1,0:T(8,128)} %param.16) | copy-start | bytes 4612
  55.0 14.1 %all-to-all-start.3 = ((f32[16,36,128]{2,1,0:T(8,128)}), f32[16,36,128]{2,1,0:T(8,128)S(1)}, u32[]{:S(2)}, u32[]{:S(2)}) async-start(f32[16,36,128]{2,1,0:T(8,128)} %reshape.313), calls=%async_computation.3 | async-start | bytes 655360 | tf_op jit(solution)/shard_map/all_to_all | solution.py:51
  70.2 19.2 %all-to-all-start.4 = ((f32[256,1,128]{2,1,0:T(1,128)}), f32[256,1,128]{2,1,0:T(1,128)S(1)}, u32[]{:S(2)}, u32[]{:S(2)}) async-start(f32[256,1,128]{2,1,0:T(1,128)} %broadcast_in_dim.31), calls=%async_computation.4 | async-start | bytes 262144 | tf_op jit(solution)/shard_map/all_to_all | solution.py:62
  95.3 10.6 %all-to-all-start.5 = ((bf16[16,8,512]{2,1,0:T(8,128)(2,1)}), bf16[16,8,512]{2,1,0:T(8,128)(2,1)S(1)}, u32[]{:S(2)}, u32[]{:S(2)}) async-start(bf16[16,8,512]{2,1,0:T(8,128)(2,1)} %broadcast_in_dim.33), calls=%async_computation.5 | async-start | bytes 262144 | tf_op jit(solution)/shard_map/all_to_all | solution.py:46
  105.9 12.5 %all-to-all-start.6 = ((bf16[16,8,512]{2,1,0:T(8,128)(2,1)}), bf16[16,8,512]{2,1,0:T(8,128)(2,1)S(1)}, u32[]{:S(2)}, u32[]{:S(2)}) async-start(bf16[16,8,512]{2,1,0:T(8,128)(2,1)} %broadcast_in_dim.33), calls=%async_computation.6 | async-start | bytes 262144 | tf_op jit(solution)/shard_map/all_to_all | solution.py:46
  118.4 16.0 %all-to-all-start.7 = ((f32[16,8,512]{2,1,0:T(8,128)}), f32[16,8,512]{2,1,0:T(8,128)S(1)}, u32[]{:S(2)}, u32[]{:S(2)}) async-start(f32[16,8,512]{2,1,0:T(8,128)} %bitcast.237), calls=%async_computation.7 | async-start | bytes 524288 | tf_op jit(solution)/shard_map/all_to_all | solution.py:51
  134.4 13.5 %all-to-all-start.8 = ((f32[16,8,512]{2,1,0:T(8,128)}), f32[16,8,512]{2,1,0:T(8,128)S(1)}, u32[]{:S(2)}, u32[]{:S(2)}) async-start(f32[16,8,512]{2,1,0:T(8,128)} %bitcast.236), calls=%async_computation.8 | async-start | bytes 524288 | tf_op jit(solution)/shard_map/all_to_all | solution.py:51
  149.2 18.9 %all-to-all-start.9 = ((f32[256,1,128]{2,1,0:T(1,128)}), f32[256,1,128]{2,1,0:T(1,128)S(1)}, u32[]{:S(2)}, u32[]{:S(2)}) async-start(f32[256,1,128]{2,1,0:T(1,128)} %broadcast_in_dim.34), calls=%async_computation.9 | async-start | bytes 262144 | tf_op jit(solution)/shard_map/all_to_all | solution.py:62
  174.0 10.6 %all-to-all-start.10 = ((bf16[16,8,512]{2,1,0:T(8,128)(2,1)}), bf16[16,8,512]{2,1,0:T(8,128)(2,1)S(1)}, u32[]{:S(2)}, u32[]{:S(2)}) async-start(bf16[16,8,512]{2,1,0:T(8,128)(2,1)} %broadcast_in_dim.35), calls=%async_computation.10 | async-start | bytes 262144 | tf_op jit(solution)/shard_map/all_to_all | solution.py:46
  184.6 12.5 %all-to-all-start.11 = ((bf16[16,8,512]{2,1,0:T(8,128)(2,1)}), bf16[16,8,512]{2,1,0:T(8,128)(2,1)S(1)}, u32[]{:S(2)}, u32[]{:S(2)}) async-start(bf16[16,8,512]{2,1,0:T(8,128)(2,1)} %broadcast_in_dim.35), calls=%async_computation.11 | async-start | bytes 262144 | tf_op jit(solution)/shard_map/all_to_all | solution.py:46
  197.1 16.0 %all-to-all-start.12 = ((f32[16,8,512]{2,1,0:T(8,128)}), f32[16,8,512]{2,1,0:T(8,128)S(1)}, u32[]{:S(2)}, u32[]{:S(2)}) async-start(f32[16,8,512]{2,1,0:T(8,128)} %bitcast.235), calls=%async_computation.12 | async-start | bytes 524288 | tf_op jit(solution)/shard_map/all_to_all | solution.py:51
  213.2 13.5 %all-to-all-start.13 = ((f32[16,8,512]{2,1,0:T(8,128)}), f32[16,8,512]{2,1,0:T(8,128)S(1)}, u32[]{:S(2)}, u32[]{:S(2)}) async-start(f32[16,8,512]{2,1,0:T(8,128)} %bitcast.234), calls=%async_computation.13 | async-start | bytes 524288 | tf_op jit(solution)/shard_map/all_to_all | solution.py:51

commit v10 on v7

--- a/solution.py
+++ b/solution.py
@@ -59,7 +59,7 @@
     )
     count = lax.axis_size("row") * lax.axis_size("col")
     copies = jnp.broadcast_to(local[None], (count,) + local.shape)
-    held = lax.all_to_all(copies, ("row", "col"), 0, 0, tiled=True)
+    held = lax.all_to_all(copies, ("col", "row"), 0, 0, tiled=True)
     total = jnp.sum(held, axis=0)
     return total[: order * order].reshape(order, order), total[order * order :].reshape(order, order)
 

time: 251 us -> 251 us (level)
  no operation moved by 1% of the time
where the time goes in v10:
time: 251 us; the launch traced here: 250 us
  starting transfers between devices  84.3 us (34%)
  waiting for transfers between devices  84.2 us (34%)
  matrix products  33.7 us (13%)
  blocking collectives  18.7 us (7%)
  local copies, waits for them, and re-layouts  18 us (7%)
  other arithmetic  9.17 us (4%)
    all_to_all x6, starting transfers between devices, scatter_sum_by_exchange(): held = lax.all_to_all(dense_rows(chunks), axis, 0, 0, tiled=True)  38.1 us
    all_to_all x6, waiting for transfers between devices, scatter_sum_by_exchange(): held = lax.all_to_all(dense_rows(chunks), axis, 0, 0, tiled=True)  35.5 us
    all_to_all x6, starting transfers between devices, gather_by_exchange(): lax.all_to_all(dense_rows(copies), axis, 0, 0, tiled=True)  33.3 us
    all_to_all x2, waiting for transfers between devices, gram_sums(): held = lax.all_to_all(copies, ('col', 'row'), 0, 0, tiled=True)  24.8 us
    all_to_all x6, waiting for transfers between devices, gather_by_exchange(): lax.all_to_all(dense_rows(copies), axis, 0, 0, tiled=True)  23.9 us
    all_to_all x1, blocking collectives, gram_sums(): held = lax.all_to_all(copies, ('col', 'row'), 0, 0, tiled=True)  18.7 us
    dot_general x3, matrix products, direct_terms(): jnp.einsum('sut,cst->csu', part_tiles, col_values, preferred_element_type...  13.5 us
    all_to_all x2, starting transfers between devices, gram_sums(): held = lax.all_to_all(copies, ('col', 'row'), 0, 0, tiled=True)  12.9 us
  transfers between devices with their start and end apart: 14, of which 14 were waited for; matrix products, arithmetic and copies ran while one was open for 15% of the time, Pallas kernels for 0%

profile of v10, /device:TPU:1, one launch (start us, length us, event | category | flops | bytes accessed | tf_op | source)
XLA Modules:
  0.0 249.9 jit_solution(7028566353667819688)
XLA Ops:
  1.3 0.7 fusion.137
  2.8 6.8 %all-to-all-start = ((bf16[16,36,128]{2,1,0:T(8,128)(2,1)}), bf16[16,36,128]{2,1,0:T(8,128)(2,1)S(1)}, u32[]{:S(2)}, u32[]{:S(2)}) async-start(bf16[16,36,128]{2,1,0:T(8,128)(2,1)} %broadcast_in_dim.38), calls=%async_computation | async-start | bytes 327680 | tf_op jit(solution)/shard_map/all_to_all | solution.py:46
  9.6 0.8 compare_and_fusion
  10.4 0.8 slice_bitcast_fusion.2
  11.8 4.2 %all-to-all-done = bf16[16,36,128]{2,1,0:T(8,128)(2,1)S(1)} async-done(((bf16[16,36,128]{2,1,0:T(8,128)(2,1)}), bf16[16,36,128]{2,1,0:T(8,128)(2,1)S(1)}, u32[]{:S(2)}, u32[]{:S(2)}) %all-to-all-start) | async-done | bytes 147488 | tf_op jit(solution)/shard_map/all_to_all | solution.py:46
  16.0 10.6 %all-to-all-start.1 = ((bf16[16,36,128]{2,1,0:T(8,128)(2,1)}), bf16[16,36,128]{2,1,0:T(8,128)(2,1)S(1)}, u32[]{:S(2)}, u32[]{:S(2)}) async-start(bf16[16,36,128]{2,1,0:T(8,128)(2,1)} %broadcast_in_dim.38), calls=%async_computation.1 | async-start | bytes 327680 | tf_op jit(solution)/shard_map/all_to_all | solution.py:46
  27.7 4.5 %fusion.15 = f32[9,128,128,1]{2,0,1,3:T(8,128)S(1)} fusion(bf16[1,1,128,128,128]{4,3,2,1,0:T(8,128)(2,1)} %param.11, bf16[128,9,128]{2,1,0:T(8,128)(2,1)S(1)} %gather_fusion.3, f32[128]{0:T(128)S(1)} %compare_convert_fusion, pred[128]{0:T(512)(128)(4,1)S(1)} %get-tuple-element.37), kind=kOutput, calls=%fused_computation.22 | convolution fusion | flops 38043648 | bytes 5079680 | tf_op jit(solution)/shard_map/sut,cst->csu/dot_general | solution.py:81
  32.8 2.7 %all-to-all-done.1 = bf16[16,36,128]{2,1,0:T(8,128)(2,1)S(1)} async-done(((bf16[16,36,128]{2,1,0:T(8,128)(2,1)}), bf16[16,36,128]{2,1,0:T(8,128)(2,1)S(1)}, u32[]{:S(2)}, u32[]{:S(2)}) %all-to-all-start.1) | async-done | bytes 147488 | tf_op jit(solution)/shard_map/all_to_all | solution.py:46
  36.1 0.8 reshape.309
  36.9 6.3 %all-to-all-start.2 = ((f32[16,36,128]{2,1,0:T(8,128)}), f32[16,36,128]{2,1,0:T(8,128)S(1)}, u32[]{:S(2)}, u32[]{:S(2)}) async-start(f32[16,36,128]{2,1,0:T(8,128)} %reshape.309), calls=%async_computation.2 | async-start | bytes 655360 | tf_op jit(solution)/shard_map/all_to_all | solution.py:51
  44.2 3.5 %fusion.21 = f32[9,128,128,1]{2,0,1,3:T(8,128)S(1)} fusion(bf16[1,1,128,128,128]{4,3,2,1,0:T(8,128)(2,1)} %param.11, bf16[128,9,128]{2,1,0:T(8,128)(2,1)S(1)} %gather_fusion.4, f32[128]{0:T(128)S(1)} %compare_select_fusion.1, pred[128]{0:T(512)(128)(4,1)S(1)} %get-tuple-element.29), kind=kOutput, calls=%fused_computation.24 | convolution fusion | flops 38043648 | bytes 5079680 | tf_op jit(solution)/shard_map/sut,csu->cst/dot_general | solution.py:93
  48.2 5.8 %all-to-all-done.2 = f32[16,36,128]{2,1,0:T(8,128)S(1)} async-done(((f32[16,36,128]{2,1,0:T(8,128)}), f32[16,36,128]{2,1,0:T(8,128)S(1)}, u32[]{:S(2)}, u32[]{:S(2)}) %all-to-all-start.2) | async-done | bytes 294944 | tf_op jit(solution)/shard_map/all_to_all | solution.py:51
  54.2 0.8 reshape.313
  55.0 6.4 %all-to-all-start.3 = ((f32[16,36,128]{2,1,0:T(8,128)}), f32[16,36,128]{2,1,0:T(8,128)S(1)}, u32[]{:S(2)}, u32[]{:S(2)}) async-start(f32[16,36,128]{2,1,0:T(8,128)} %reshape.313), calls=%async_computation.3 | async-start | bytes 655360 | tf_op jit(solution)/shard_map/all_to_all | solution.py:51
  61.6 7.5 %all-to-all-done.3 = f32[16,36,128]{2,1,0:T(8,128)S(1)} async-done(((f32[16,36,128]{2,1,0:T(8,128)}), f32[16,36,128]{2,1,0:T(8,128)S(1)}, u32[]{:S(2)}, u32[]{:S(2)}) %all-to-all-start.3) | async-done | bytes 294944 | tf_op jit(solution)/shard_map/all_to_all | solution.py:51
  69.5 0.7 broadcast_in_dim.39
  70.2 6.6 %all-to-all-start.4 = ((f32[256,1,128]{2,1,0:T(1,128)}), f32[256,1,128]{2,1,0:T(1,128)S(1)}, u32[]{:S(2)}, u32[]{:S(2)}) async-start(f32[256,1,128]{2,1,0:T(1,128)} %broadcast_in_dim.39), calls=%async_computation.4 | async-start | bytes 262144 | tf_op jit(solution)/shard_map/all_to_all | solution.py:62
  76.8 12.6 %all-to-all-done.4 = f32[256,1,128]{2,1,0:T(1,128)S(1)} async-done(((f32[256,1,128]{2,1,0:T(1,128)}), f32[256,1,128]{2,1,0:T(1,128)S(1)}, u32[]{:S(2)}, u32[]{:S(2)}) %all-to-all-start.4) | async-done | bytes 131104 | tf_op jit(solution)/shard_map/all_to_all | solution.py:62
  94.5 4.4 %all-to-all-start.5 = ((bf16[16,8,512]{2,1,0:T(8,128)(2,1)}), bf16[16,8,512]{2,1,0:T(8,128)(2,1)S(1)}, u32[]{:S(2)}, u32[]{:S(2)}) async-start(bf16[16,8,512]{2,1,0:T(8,128)(2,1)} %broadcast_in_dim.41), calls=%async_computation.5 | async-start | bytes 262144 | tf_op jit(solution)/shard_map/all_to_all | solution.py:46
  99.1 6.0 %all-to-all-done.5 = bf16[16,8,512]{2,1,0:T(8,128)(2,1)S(1)} async-done(((bf16[16,8,512]{2,1,0:T(8,128)(2,1)}), bf16[16,8,512]{2,1,0:T(8,128)(2,1)S(1)}, u32[]{:S(2)}, u32[]{:S(2)}) %all-to-all-start.5) | async-done | bytes 131104 | tf_op jit(solution)/shard_map/all_to_all | solution.py:46
  105.1 3.5 %all-to-all-start.6 = ((bf16[16,8,512]{2,1,0:T(8,128)(2,1)}), bf16[16,8,512]{2,1,0:T(8,128)(2,1)S(1)}, u32[]{:S(2)}, u32[]{:S(2)}) async-start(bf16[16,8,512]{2,1,0:T(8,128)(2,1)} %broadcast_in_dim.41), calls=%async_computation.6 | async-start | bytes 262144 | tf_op jit(solution)/shard_map/all_to_all | solution.py:46
  109.3 4.5 %fusion.27 = f32[8,128,128,1]{2,0,1,3:T(8,128)S(1)} fusion(bf16[1,1,128,128,128]{4,3,2,1,0:T(8,128)(2,1)} %param.11, bf16[128,8,128]{2,1,0:T(8,128)(2,1)S(1)} %gather_fusion.5, f32[128]{0:T(128)S(1)} %compare_convert_fusion, pred[128]{0:T(512)(128)(4,1)S(1)} %get-tuple-element.37), kind=kOutput, calls=%fused_computation.26 | convolution fusion | flops 33816576 | bytes 4981376 | tf_op jit(solution)/shard_map/sut,cst->csu/dot_general | solution.py:81
  114.2 0.8 copy.173
  115.1 2.6 %all-to-all-done.6 = bf16[16,8,512]{2,1,0:T(8,128)(2,1)S(1)} async-done(((bf16[16,8,512]{2,1,0:T(8,128)(2,1)}), bf16[16,8,512]{2,1,0:T(8,128)(2,1)S(1)}, u32[]{:S(2)}, u32[]{:S(2)}) %all-to-all-start.6) | async-done | bytes 131104 | tf_op jit(solution)/shard_map/all_to_all | solution.py:46
  117.6 6.5 %all-to-all-start.7 = ((f32[16,8,512]{2,1,0:T(8,128)}), f32[16,8,512]{2,1,0:T(8,128)S(1)}, u32[]{:S(2)}, u32[]{:S(2)}) async-start(f32[16,8,512]{2,1,0:T(8,128)} %bitcast.239), calls=%async_computation.7 | async-start | bytes 524288 | tf_op jit(solution)/shard_map/all_to_all | solution.py:51
  124.8 3.4 %fusion.33 = f32[8,128,128,1]{2,0,1,3:T(8,128)S(1)} fusion(bf16[1,1,128,128,128]{4,3,2,1,0:T(8,128)(2,1)} %param.11, bf16[128,8,128]{2,1,0:T(8,128)(2,1)S(1)} %gather_fusion.6, f32[128]{0:T(128)S(1)} %compare_select_fusion.1, pred[128]{0:T(512)(128)(4,1)S(1)} %get-tuple-element.29), kind=kOutput, calls=%fused_computation.28 | convolution fusion | flops 33816576 | bytes 4981376 | tf_op jit(solution)/shard_map/sut,csu->cst/dot_general | solution.py:93
  128.6 0.9 copy.172
  129.5 4.2 %all-to-all-done.7 = f32[16,8,512]{2,1,0:T(8,128)S(1)} async-done(((f32[16,8,512]{2,1,0:T(8,128)}), f32[16,8,512]{2,1,0:T(8,128)S(1)}, u32[]{:S(2)}, u32[]{:S(2)}) %all-to-all-start.7) | async-done | bytes 262176 | tf_op jit(solution)/shard_map/all_to_all | solution.py:51
  133.7 6.3 %all-to-all-start.8 = ((f32[16,8,512]{2,1,0:T(8,128)}), f32[16,8,512]{2,1,0:T(8,128)S(1)}, u32[]{:S(2)}, u32[]{:S(2)}) async-start(f32[16,8,512]{2,1,0:T(8,128)} %bitcast.238), calls=%async_computation.8 | async-start | bytes 524288 | tf_op jit(solution)/shard_map/all_to_all | solution.py:51
  140.3 6.9 %all-to-all-done.8 = f32[16,8,512]{2,1,0:T(8,128)S(1)} async-done(((f32[16,8,512]{2,1,0:T(8,128)}), f32[16,8,512]{2,1,0:T(8,128)S(1)}, u32[]{:S(2)}, u32[]{:S(2)}) %all-to-all-start.8) | async-done | bytes 262176 | tf_op jit(solution)/shard_map/all_to_all | solution.py:51
  147.7 0.7 broadcast_in_dim.45
  148.4 6.3 %all-to-all-start.9 = ((f32[256,1,128]{2,1,0:T(1,128)}), f32[256,1,128]{2,1,0:T(1,128)S(1)}, u32[]{:S(2)}, u32[]{:S(2)}) async-start(f32[256,1,128]{2,1,0:T(1,128)} %broadcast_in_dim.45), calls=%async_computation.9 | async-start | bytes 262144 | tf_op jit(solution)/shard_map/all_to_all | solution.py:62
  155.1 12.2 %all-to-all-done.9 = f32[256,1,128]{2,1,0:T(1,128)S(1)} async-done(((f32[256,1,128]{2,1,0:T(1,128)}), f32[256,1,128]{2,1,0:T(1,128)S(1)}, u32[]{:S(2)}, u32[]{:S(2)}) %all-to-all-start.9) | async-done | bytes 131104 | tf_op jit(solution)/shard_map/all_to_all | solution.py:62
  172.5 4.4 %all-to-all-start.10 = ((bf16[16,8,512]{2,1,0:T(8,128)(2,1)}), bf16[16,8,512]{2,1,0:T(8,128)(2,1)S(1)}, u32[]{:S(2)}, u32[]{:S(2)}) async-start(bf16[16,8,512]{2,1,0:T(8,128)(2,1)} %broadcast_in_dim.46), calls=%async_computation.10 | async-start | bytes 262144 | tf_op jit(solution)/shard_map/all_to_all | solution.py:46
  177.2 5.9 %all-to-all-done.10 = bf16[16,8,512]{2,1,0:T(8,128)(2,1)S(1)} async-done(((bf16[16,8,512]{2,1,0:T(8,128)(2,1)}), bf16[16,8,512]{2,1,0:T(8,128)(2,1)S(1)}, u32[]{:S(2)}, u32[]{:S(2)}) %all-to-all-start.10) | async-done | bytes 131104 | tf_op jit(solution)/shard_map/all_to_all | solution.py:46
  183.1 3.5 %all-to-all-start.11 = ((bf16[16,8,512]{2,1,0:T(8,128)(2,1)}), bf16[16,8,512]{2,1,0:T(8,128)(2,1)S(1)}, u32[]{:S(2)}, u32[]{:S(2)}) async-start(bf16[16,8,512]{2,1,0:T(8,128)(2,1)} %broadcast_in_dim.46), calls=%async_computation.11 | async-start | bytes 262144 | tf_op jit(solution)/shard_map/all_to_all | solution.py:46
  187.3 4.5 %fusion.39 = f32[8,128,128,1]{2,0,1,3:T(8,128)S(1)} fusion(bf16[1,1,128,128,128]{4,3,2,1,0:T(8,128)(2,1)} %param.11, bf16[128,8,128]{2,1,0:T(8,128)(2,1)S(1)} %gather_fusion.7, f32[128]{0:T(128)S(1)} %compare_convert_fusion, pred[128]{0:T(512)(128)(4,1)S(1)} %get-tuple-element.37), kind=kOutput, calls=%fused_computation.30 | convolution fusion | flops 33816576 | bytes 4981376 | tf_op jit(solution)/shard_map/sut,cst->csu/dot_general | solution.py:81
  192.2 0.8 copy.171
  193.0 2.6 %all-to-all-done.11 = bf16[16,8,512]{2,1,0:T(8,128)(2,1)S(1)} async-done(((bf16[16,8,512]{2,1,0:T(8,128)(2,1)}), bf16[16,8,512]{2,1,0:T(8,128)(2,1)S(1)}, u32[]{:S(2)}, u32[]{:S(2)}) %all-to-all-start.11) | async-done | bytes 131104 | tf_op jit(solution)/shard_map/all_to_all | solution.py:46
  195.6 6.5 %all-to-all-start.12 = ((f32[16,8,512]{2,1,0:T(8,128)}), f32[16,8,512]{2,1,0:T(8,128)S(1)}, u32[]{:S(2)}, u32[]{:S(2)}) async-start(f32[16,8,512]{2,1,0:T(8,128)} %bitcast.237), calls=%async_computation.12 | async-start | bytes 524288 | tf_op jit(solution)/shard_map/all_to_all | solution.py:51
  202.7 3.4 %fusion.45 = f32[8,128,128,1]{2,0,1,3:T(8,128)S(1)} fusion(bf16[1,1,128,128,128]{4,3,2,1,0:T(8,128)(2,1)} %param.11, bf16[128,8,128]{2,1,0:T(8,128)(2,1)S(1)} %gather_fusion.8, f32[128]{0:T(128)S(1)} %compare_select_fusion.1, pred[128]{0:T(512)(128)(4,1)S(1)} %get-tuple-element.29), kind=kOutput, calls=%fused_computation.32 | convolution fusion | flops 33816576 | bytes 4981376 | tf_op jit(solution)/shard_map/sut,csu->cst/dot_general | solution.py:93
  206.6 0.9 copy.170
  207.4 4.2 %all-to-all-done.12 = f32[16,8,512]{2,1,0:T(8,128)S(1)} async-done(((f32[16,8,512]{2,1,0:T(8,128)}), f32[16,8,512]{2,1,0:T(8,128)S(1)}, u32[]{:S(2)}, u32[]{:S(2)}) %all-to-all-start.12) | async-done | bytes 262176 | tf_op jit(solution)/shard_map/all_to_all | solution.py:51
  211.7 6.3 %all-to-all-start.13 = ((f32[16,8,512]{2,1,0:T(8,128)}), f32[16,8,512]{2,1,0:T(8,128)S(1)}, u32[]{:S(2)}, u32[]{:S(2)}) async-start(f32[16,8,512]{2,1,0:T(8,128)} %bitcast.236), calls=%async_computation.13 | async-start | bytes 524288 | tf_op jit(solution)/shard_map/all_to_all | solution.py:51
  218.3 6.9 %all-to-all-done.13 = f32[16,8,512]{2,1,0:T(8,128)S(1)} async-done(((f32[16,8,512]{2,1,0:T(8,128)}), f32[16,8,512]{2,1,0:T(8,128)S(1)}, u32[]{:S(2)}, u32[]{:S(2)}) %all-to-all-start.13) | async-done | bytes 262176 | tf_op jit(solution)/shard_map/all_to_all | solution.py:51
  225.8 18.7 %all_to_all.78 = f32[256,1,128]{2,1,0:T(1,128)S(1)} all-to-all(f32[256,1,128]{2,1,0:T(1,128)S(1)} %broadcast_in_dim.47), channel_id=1, replica_groups=mesh['row'=16,'col'=16] {'col','row'}, dimensions={0} | all-to-all | bytes 262144 | tf_op jit(solution)/shard_map/all_to_all | solution.py:62
  248.2 0.8 fusion.191
  249.1 0.7 fusion.193
  (139 shorter events, 27.0 us)
Async XLA Ops:
  2.8 13.2 %all-to-all-start = ((bf16[16,36,128]{2,1,0:T(8,128)(2,1)}), bf16[16,36,128]{2,1,0:T(8,128)(2,1)S(1)}, u32[]{:S(2)}, u32[]{:S(2)}) async-start(bf16[16,36,128]{2,1,0:T(8,128)(2,1)} %broadcast_in_dim.38), calls=%async_computation | async-start | bytes 327680 | tf_op jit(solution)/shard_map/all_to_all | solution.py:46
  16.0 19.6 %all-to-all-start.1 = ((bf16[16,36,128]{2,1,0:T(8,128)(2,1)}), bf16[16,36,128]{2,1,0:T(8,128)(2,1)S(1)}, u32[]{:S(2)}, u32[]{:S(2)}) async-start(bf16[16,36,128]{2,1,0:T(8,128)(2,1)} %broadcast_in_dim.38), calls=%async_computation.1 | async-start | bytes 327680 | tf_op jit(solution)/shard_map/all_to_all | solution.py:46
  32.3 11.0 %copy-start.2 = (s32[1,1,2,128]{3,2,1,0:T(2,128)S(1)}, s32[1,1,2,128]{3,2,1,0:T(2,128)}, u32[]{:S(2)}) copy-start(s32[1,1,2,128]{3,2,1,0:T(2,128)} %param.12) | copy-start | bytes 3076
  36.9 17.1 %all-to-all-start.2 = ((f32[16,36,128]{2,1,0:T(8,128)}), f32[16,36,128]{2,1,0:T(8,128)S(1)}, u32[]{:S(2)}, u32[]{:S(2)}) async-start(f32[16,36,128]{2,1,0:T(8,128)} %reshape.309), calls=%async_computation.2 | async-start | bytes 655360 | tf_op jit(solution)/shard_map/all_to_all | solution.py:51
  44.2 17.2 %copy-start = (f32[8,512]{1,0:T(8,128)S(1)}, f32[8,512]{1,0:T(8,128)}, u32[]{:S(2)}) copy-start(f32[8,512]{1,0:T(8,128)} %param.15) | copy-start | bytes 49156
  44.2 32.6 %copy-start.1 = (f32[2,8,24]{2,1,0:T(8,128)S(1)}, f32[2,8,24]{2,1,0:T(8,128)}, u32[]{:S(2)}) copy-start(f32[2,8,24]{2,1,0:T(8,128)} %param.16) | copy-start | bytes 4612
  55.0 14.1 %all-to-all-start.3 = ((f32[16,36,128]{2,1,0:T(8,128)}), f32[16,36,128]{2,1,0:T(8,128)S(1)}, u32[]{:S(2)}, u32[]{:S(2)}) async-start(f32[16,36,128]{2,1,0:T(8,128)} %reshape.313), calls=%async_computation.3 | async-start | bytes 655360 | tf_op jit(solution)/shard_map/all_to_all | solution.py:51
  70.2 19.2 %all-to-all-start.4 = ((f32[256,1,128]{2,1,0:T(1,128)}), f32[256,1,128]{2,1,0:T(1,128)S(1)}, u32[]{:S(2)}, u32[]{:S(2)}) async-start(f32[256,1,128]{2,1,0:T(1,128)} %broadcast_in_dim.39), calls=%async_computation.4 | async-start | bytes 262144 | tf_op jit(solution)/shard_map/all_to_all | solution.py:62
  94.5 10.6 %all-to-all-start.5 = ((bf16[16,8,512]{2,1,0:T(8,128)(2,1)}), bf16[16,8,512]{2,1,0:T(8,128)(2,1)S(1)}, u32[]{:S(2)}, u32[]{:S(2)}) async-start(bf16[16,8,512]{2,1,0:T(8,128)(2,1)} %broadcast_in_dim.41), calls=%async_computation.5 | async-start | bytes 262144 | tf_op jit(solution)/shard_map/all_to_all | solution.py:46
  105.1 12.5 %all-to-all-start.6 = ((bf16[16,8,512]{2,1,0:T(8,128)(2,1)}), bf16[16,8,512]{2,1,0:T(8,128)(2,1)S(1)}, u32[]{:S(2)}, u32[]{:S(2)}) async-start(bf16[16,8,512]{2,1,0:T(8,128)(2,1)} %broadcast_in_dim.41), calls=%async_computation.6 | async-start | bytes 262144 | tf_op jit(solution)/shard_map/all_to_all | solution.py:46
  117.6 16.1 %all-to-all-start.7 = ((f32[16,8,512]{2,1,0:T(8,128)}), f32[16,8,512]{2,1,0:T(8,128)S(1)}, u32[]{:S(2)}, u32[]{:S(2)}) async-start(f32[16,8,512]{2,1,0:T(8,128)} %bitcast.239), calls=%async_computation.7 | async-start | bytes 524288 | tf_op jit(solution)/shard_map/all_to_all | solution.py:51
  133.7 13.5 %all-to-all-start.8 = ((f32[16,8,512]{2,1,0:T(8,128)}), f32[16,8,512]{2,1,0:T(8,128)S(1)}, u32[]{:S(2)}, u32[]{:S(2)}) async-start(f32[16,8,512]{2,1,0:T(8,128)} %bitcast.238), calls=%async_computation.8 | async-start | bytes 524288 | tf_op jit(solution)/shard_map/all_to_all | solution.py:51
  148.4 18.9 %all-to-all-start.9 = ((f32[256,1,128]{2,1,0:T(1,128)}), f32[256,1,128]{2,1,0:T(1,128)S(1)}, u32[]{:S(2)}, u32[]{:S(2)}) async-start(f32[256,1,128]{2,1,0:T(1,128)} %broadcast_in_dim.45), calls=%async_computation.9 | async-start | bytes 262144 | tf_op jit(solution)/shard_map/all_to_all | solution.py:62
  172.5 10.6 %all-to-all-start.10 = ((bf16[16,8,512]{2,1,0:T(8,128)(2,1)}), bf16[16,8,512]{2,1,0:T(8,128)(2,1)S(1)}, u32[]{:S(2)}, u32[]{:S(2)}) async-start(bf16[16,8,512]{2,1,0:T(8,128)(2,1)} %broadcast_in_dim.46), calls=%async_computation.10 | async-start | bytes 262144 | tf_op jit(solution)/shard_map/all_to_all | solution.py:46
  183.1 12.5 %all-to-all-start.11 = ((bf16[16,8,512]{2,1,0:T(8,128)(2,1)}), bf16[16,8,512]{2,1,0:T(8,128)(2,1)S(1)}, u32[]{:S(2)}, u32[]{:S(2)}) async-start(bf16[16,8,512]{2,1,0:T(8,128)(2,1)} %broadcast_in_dim.46), calls=%async_computation.11 | async-start | bytes 262144 | tf_op jit(solution)/shard_map/all_to_all | solution.py:46
  195.6 16.1 %all-to-all-start.12 = ((f32[16,8,512]{2,1,0:T(8,128)}), f32[16,8,512]{2,1,0:T(8,128)S(1)}, u32[]{:S(2)}, u32[]{:S(2)}) async-start(f32[16,8,512]{2,1,0:T(8,128)} %bitcast.237), calls=%async_computation.12 | async-start | bytes 524288 | tf_op jit(solution)/shard_map/all_to_all | solution.py:51
  211.7 13.5 %all-to-all-start.13 = ((f32[16,8,512]{2,1,0:T(8,128)}), f32[16,8,512]{2,1,0:T(8,128)S(1)}, u32[]{:S(2)}, u32[]{:S(2)}) async-start(f32[16,8,512]{2,1,0:T(8,128)} %bitcast.236), calls=%async_computation.13 | async-start | bytes 524288 | tf_op jit(solution)/shard_map/all_to_all | solution.py:51

commit v11 on v7

--- a/solution.py
+++ b/solution.py
@@ -54,11 +54,11 @@
 
 def gram_sums(new_vecs, new_images):
     order = new_vecs.shape[0]
-    local = jnp.concatenate(
-        [matmul_high(new_vecs, new_vecs.T).reshape(-1), matmul_high(new_images, new_vecs.T).reshape(-1)]
+    count = lax.axis_size("row") * lax.axis_size("col")
+    parts = [matmul_high(new_vecs, new_vecs.T), matmul_high(new_images, new_vecs.T)]
+    copies = jnp.concatenate(
+        [jnp.broadcast_to(part.reshape(1, -1), (count, order * order)) for part in parts], axis=1
     )
-    count = lax.axis_size("row") * lax.axis_size("col")
-    copies = jnp.broadcast_to(local[None], (count,) + local.shape)
     held = lax.all_to_all(copies, ("row", "col"), 0, 0, tiled=True)
     total = jnp.sum(held, axis=0)
     return total[: order * order].reshape(order, order), total[order * order :].reshape(order, order)

time: 251 us -> 252 us (level)
  no operation moved by 1% of the time
where the time goes in v11:
time: 252 us; the launch traced here: 250 us
  starting transfers between devices  84.3 us (33%)
  waiting for transfers between devices  84.2 us (33%)
  matrix products  33.7 us (13%)
  blocking collectives  18.8 us (7%)
  local copies, waits for them, and re-layouts  17.8 us (7%)
  other arithmetic  9.88 us (4%)
    all_to_all x6, starting transfers between devices, scatter_sum_by_exchange(): held = lax.all_to_all(dense_rows(chunks), axis, 0, 0, tiled=True)  38.1 us
    all_to_all x6, waiting for transfers between devices, scatter_sum_by_exchange(): held = lax.all_to_all(dense_rows(chunks), axis, 0, 0, tiled=True)  35.5 us
    all_to_all x6, starting transfers between devices, gather_by_exchange(): lax.all_to_all(dense_rows(copies), axis, 0, 0, tiled=True)  33.3 us
    all_to_all x2, waiting for transfers between devices, gram_sums(): held = lax.all_to_all(copies, ('row', 'col'), 0, 0, tiled=True)  24.8 us
    all_to_all x6, waiting for transfers between devices, gather_by_exchange(): lax.all_to_all(dense_rows(copies), axis, 0, 0, tiled=True)  23.9 us
    all_to_all x1, blocking collectives, gram_sums(): held = lax.all_to_all(copies, ('row', 'col'), 0, 0, tiled=True)  18.8 us
    dot_general x3, matrix products, direct_terms(): jnp.einsum('sut,cst->csu', part_tiles, col_values, preferred_element_type...  13.5 us
    all_to_all x2, starting transfers between devices, gram_sums(): held = lax.all_to_all(copies, ('row', 'col'), 0, 0, tiled=True)  12.9 us
  transfers between devices with their start and end apart: 14, of which 14 were waited for; matrix products, arithmetic and copies ran while one was open for 15% of the time, Pallas kernels for 0%

profile of v11, /device:TPU:1, one launch (start us, length us, event | category | flops | bytes accessed | tf_op | source)
XLA Modules:
  0.0 250.4 jit_solution(4968758497615814908)
XLA Ops:
  1.3 0.7 fusion.137
  2.8 6.8 %all-to-all-start = ((bf16[16,36,128]{2,1,0:T(8,128)(2,1)}), bf16[16,36,128]{2,1,0:T(8,128)(2,1)S(1)}, u32[]{:S(2)}, u32[]{:S(2)}) async-start(bf16[16,36,128]{2,1,0:T(8,128)(2,1)} %broadcast_in_dim.61), calls=%async_computation | async-start | bytes 327680 | tf_op jit(solution)/shard_map/all_to_all | solution.py:46
  9.6 0.8 compare_and_fusion
  10.4 0.8 slice_bitcast_fusion.2
  11.8 4.2 %all-to-all-done = bf16[16,36,128]{2,1,0:T(8,128)(2,1)S(1)} async-done(((bf16[16,36,128]{2,1,0:T(8,128)(2,1)}), bf16[16,36,128]{2,1,0:T(8,128)(2,1)S(1)}, u32[]{:S(2)}, u32[]{:S(2)}) %all-to-all-start) | async-done | bytes 147488 | tf_op jit(solution)/shard_map/all_to_all | solution.py:46
  16.0 10.6 %all-to-all-start.1 = ((bf16[16,36,128]{2,1,0:T(8,128)(2,1)}), bf16[16,36,128]{2,1,0:T(8,128)(2,1)S(1)}, u32[]{:S(2)}, u32[]{:S(2)}) async-start(bf16[16,36,128]{2,1,0:T(8,128)(2,1)} %broadcast_in_dim.61), calls=%async_computation.1 | async-start | bytes 327680 | tf_op jit(solution)/shard_map/all_to_all | solution.py:46
  27.0 0.7 gather_fusion.3
  27.7 4.5 %fusion.15 = f32[9,128,128,1]{2,0,1,3:T(8,128)S(1)} fusion(bf16[1,1,128,128,128]{4,3,2,1,0:T(8,128)(2,1)} %param.11, bf16[128,9,128]{2,1,0:T(8,128)(2,1)S(1)} %gather_fusion.3, f32[128]{0:T(128)S(1)} %compare_convert_fusion, pred[128]{0:T(512)(128)(4,1)S(1)} %get-tuple-element.37), kind=kOutput, calls=%fused_computation.22 | convolution fusion | flops 38043648 | bytes 5079680 | tf_op jit(solution)/shard_map/sut,cst->csu/dot_general | solution.py:81
  32.8 2.8 %all-to-all-done.1 = bf16[16,36,128]{2,1,0:T(8,128)(2,1)S(1)} async-done(((bf16[16,36,128]{2,1,0:T(8,128)(2,1)}), bf16[16,36,128]{2,1,0:T(8,128)(2,1)S(1)}, u32[]{:S(2)}, u32[]{:S(2)}) %all-to-all-start.1) | async-done | bytes 147488 | tf_op jit(solution)/shard_map/all_to_all | solution.py:46
  36.1 0.8 reshape.290
  36.9 6.3 %all-to-all-start.2 = ((f32[16,36,128]{2,1,0:T(8,128)}), f32[16,36,128]{2,1,0:T(8,128)S(1)}, u32[]{:S(2)}, u32[]{:S(2)}) async-start(f32[16,36,128]{2,1,0:T(8,128)} %reshape.290), calls=%async_computation.2 | async-start | bytes 655360 | tf_op jit(solution)/shard_map/all_to_all | solution.py:51
  43.5 0.7 gather_fusion.4
  44.2 3.5 %fusion.21 = f32[9,128,128,1]{2,0,1,3:T(8,128)S(1)} fusion(bf16[1,1,128,128,128]{4,3,2,1,0:T(8,128)(2,1)} %param.11, bf16[128,9,128]{2,1,0:T(8,128)(2,1)S(1)} %gather_fusion.4, f32[128]{0:T(128)S(1)} %compare_select_fusion.1, pred[128]{0:T(512)(128)(4,1)S(1)} %get-tuple-element.29), kind=kOutput, calls=%fused_computation.24 | convolution fusion | flops 38043648 | bytes 5079680 | tf_op jit(solution)/shard_map/sut,csu->cst/dot_general | solution.py:93
  48.2 5.8 %all-to-all-done.2 = f32[16,36,128]{2,1,0:T(8,128)S(1)} async-done(((f32[16,36,128]{2,1,0:T(8,128)}), f32[16,36,128]{2,1,0:T(8,128)S(1)}, u32[]{:S(2)}, u32[]{:S(2)}) %all-to-all-start.2) | async-done | bytes 294944 | tf_op jit(solution)/shard_map/all_to_all | solution.py:51
  54.2 0.8 reshape.294
  55.0 6.4 %all-to-all-start.3 = ((f32[16,36,128]{2,1,0:T(8,128)}), f32[16,36,128]{2,1,0:T(8,128)S(1)}, u32[]{:S(2)}, u32[]{:S(2)}) async-start(f32[16,36,128]{2,1,0:T(8,128)} %reshape.294), calls=%async_computation.3 | async-start | bytes 655360 | tf_op jit(solution)/shard_map/all_to_all | solution.py:51
  61.6 7.5 %all-to-all-done.3 = f32[16,36,128]{2,1,0:T(8,128)S(1)} async-done(((f32[16,36,128]{2,1,0:T(8,128)}), f32[16,36,128]{2,1,0:T(8,128)S(1)}, u32[]{:S(2)}, u32[]{:S(2)}) %all-to-all-start.3) | async-done | bytes 294944 | tf_op jit(solution)/shard_map/all_to_all | solution.py:51
  70.1 6.6 %all-to-all-start.4 = ((f32[256,1,128]{2,1,0:T(1,128)}), f32[256,1,128]{2,1,0:T(1,128)S(1)}, u32[]{:S(2)}, u32[]{:S(2)}) async-start(f32[256,1,128]{2,1,0:T(1,128)} %bitcast.18), calls=%async_computation.4 | async-start | bytes 262144 | tf_op jit(solution)/shard_map/all_to_all | solution.py:62
  76.8 12.6 %all-to-all-done.4 = f32[256,1,128]{2,1,0:T(1,128)S(1)} async-done(((f32[256,1,128]{2,1,0:T(1,128)}), f32[256,1,128]{2,1,0:T(1,128)S(1)}, u32[]{:S(2)}, u32[]{:S(2)}) %all-to-all-start.4) | async-done | bytes 131104 | tf_op jit(solution)/shard_map/all_to_all | solution.py:62
  94.7 4.4 %all-to-all-start.5 = ((bf16[16,8,512]{2,1,0:T(8,128)(2,1)}), bf16[16,8,512]{2,1,0:T(8,128)(2,1)S(1)}, u32[]{:S(2)}, u32[]{:S(2)}) async-start(bf16[16,8,512]{2,1,0:T(8,128)(2,1)} %broadcast_in_dim.67), calls=%async_computation.5 | async-start | bytes 262144 | tf_op jit(solution)/shard_map/all_to_all | solution.py:46
  99.3 6.0 %all-to-all-done.5 = bf16[16,8,512]{2,1,0:T(8,128)(2,1)S(1)} async-done(((bf16[16,8,512]{2,1,0:T(8,128)(2,1)}), bf16[16,8,512]{2,1,0:T(8,128)(2,1)S(1)}, u32[]{:S(2)}, u32[]{:S(2)}) %all-to-all-start.5) | async-done | bytes 131104 | tf_op jit(solution)/shard_map/all_to_all | solution.py:46
  105.3 3.5 %all-to-all-start.6 = ((bf16[16,8,512]{2,1,0:T(8,128)(2,1)}), bf16[16,8,512]{2,1,0:T(8,128)(2,1)S(1)}, u32[]{:S(2)}, u32[]{:S(2)}) async-start(bf16[16,8,512]{2,1,0:T(8,128)(2,1)} %broadcast_in_dim.67), calls=%async_computation.6 | async-start | bytes 262144 | tf_op jit(solution)/shard_map/all_to_all | solution.py:46
  109.5 4.5 %fusion.27 = f32[8,128,128,1]{2,0,1,3:T(8,128)S(1)} fusion(bf16[1,1,128,128,128]{4,3,2,1,0:T(8,128)(2,1)} %param.11, bf16[128,8,128]{2,1,0:T(8,128)(2,1)S(1)} %gather_fusion.5, f32[128]{0:T(128)S(1)} %compare_convert_fusion, pred[128]{0:T(512)(128)(4,1)S(1)} %get-tuple-element.37), kind=kOutput, calls=%fused_computation.26 | convolution fusion | flops 33816576 | bytes 4981376 | tf_op jit(solution)/shard_map/sut,cst->csu/dot_general | solution.py:81
  114.4 0.8 copy.120
  115.2 2.6 %all-to-all-done.6 = bf16[16,8,512]{2,1,0:T(8,128)(2,1)S(1)} async-done(((bf16[16,8,512]{2,1,0:T(8,128)(2,1)}), bf16[16,8,512]{2,1,0:T(8,128)(2,1)S(1)}, u32[]{:S(2)}, u32[]{:S(2)}) %all-to-all-start.6) | async-done | bytes 131104 | tf_op jit(solution)/shard_map/all_to_all | solution.py:46
  117.8 6.5 %all-to-all-start.7 = ((f32[16,8,512]{2,1,0:T(8,128)}), f32[16,8,512]{2,1,0:T(8,128)S(1)}, u32[]{:S(2)}, u32[]{:S(2)}) async-start(f32[16,8,512]{2,1,0:T(8,128)} %bitcast.239), calls=%async_computation.7 | async-start | bytes 524288 | tf_op jit(solution)/shard_map/all_to_all | solution.py:51
  125.0 3.4 %fusion.33 = f32[8,128,128,1]{2,0,1,3:T(8,128)S(1)} fusion(bf16[1,1,128,128,128]{4,3,2,1,0:T(8,128)(2,1)} %param.11, bf16[128,8,128]{2,1,0:T(8,128)(2,1)S(1)} %gather_fusion.6, f32[128]{0:T(128)S(1)} %compare_select_fusion.1, pred[128]{0:T(512)(128)(4,1)S(1)} %get-tuple-element.29), kind=kOutput, calls=%fused_computation.28 | convolution fusion | flops 33816576 | bytes 4981376 | tf_op jit(solution)/shard_map/sut,csu->cst/dot_general | solution.py:93
  128.8 0.9 copy.119
  129.7 4.2 %all-to-all-done.7 = f32[16,8,512]{2,1,0:T(8,128)S(1)} async-done(((f32[16,8,512]{2,1,0:T(8,128)}), f32[16,8,512]{2,1,0:T(8,128)S(1)}, u32[]{:S(2)}, u32[]{:S(2)}) %all-to-all-start.7) | async-done | bytes 262176 | tf_op jit(solution)/shard_map/all_to_all | solution.py:51
  133.9 6.3 %all-to-all-start.8 = ((f32[16,8,512]{2,1,0:T(8,128)}), f32[16,8,512]{2,1,0:T(8,128)S(1)}, u32[]{:S(2)}, u32[]{:S(2)}) async-start(f32[16,8,512]{2,1,0:T(8,128)} %bitcast.238), calls=%async_computation.8 | async-start | bytes 524288 | tf_op jit(solution)/shard_map/all_to_all | solution.py:51
  140.5 6.9 %all-to-all-done.8 = f32[16,8,512]{2,1,0:T(8,128)S(1)} async-done(((f32[16,8,512]{2,1,0:T(8,128)}), f32[16,8,512]{2,1,0:T(8,128)S(1)}, u32[]{:S(2)}, u32[]{:S(2)}) %all-to-all-start.8) | async-done | bytes 262176 | tf_op jit(solution)/shard_map/all_to_all | solution.py:51
  148.6 6.3 %all-to-all-start.9 = ((f32[256,1,128]{2,1,0:T(1,128)}), f32[256,1,128]{2,1,0:T(1,128)S(1)}, u32[]{:S(2)}, u32[]{:S(2)}) async-start(f32[256,1,128]{2,1,0:T(1,128)} %bitcast.37), calls=%async_computation.9 | async-start | bytes 262144 | tf_op jit(solution)/shard_map/all_to_all | solution.py:62
  155.3 12.2 %all-to-all-done.9 = f32[256,1,128]{2,1,0:T(1,128)S(1)} async-done(((f32[256,1,128]{2,1,0:T(1,128)}), f32[256,1,128]{2,1,0:T(1,128)S(1)}, u32[]{:S(2)}, u32[]{:S(2)}) %all-to-all-start.9) | async-done | bytes 131104 | tf_op jit(solution)/shard_map/all_to_all | solution.py:62
  172.9 4.4 %all-to-all-start.10 = ((bf16[16,8,512]{2,1,0:T(8,128)(2,1)}), bf16[16,8,512]{2,1,0:T(8,128)(2,1)S(1)}, u32[]{:S(2)}, u32[]{:S(2)}) async-start(bf16[16,8,512]{2,1,0:T(8,128)(2,1)} %broadcast_in_dim.72), calls=%async_computation.10 | async-start | bytes 262144 | tf_op jit(solution)/shard_map/all_to_all | solution.py:46
  177.6 5.9 %all-to-all-done.10 = bf16[16,8,512]{2,1,0:T(8,128)(2,1)S(1)} async-done(((bf16[16,8,512]{2,1,0:T(8,128)(2,1)}), bf16[16,8,512]{2,1,0:T(8,128)(2,1)S(1)}, u32[]{:S(2)}, u32[]{:S(2)}) %all-to-all-start.10) | async-done | bytes 131104 | tf_op jit(solution)/shard_map/all_to_all | solution.py:46
  183.4 3.5 %all-to-all-start.11 = ((bf16[16,8,512]{2,1,0:T(8,128)(2,1)}), bf16[16,8,512]{2,1,0:T(8,128)(2,1)S(1)}, u32[]{:S(2)}, u32[]{:S(2)}) async-start(bf16[16,8,512]{2,1,0:T(8,128)(2,1)} %broadcast_in_dim.72), calls=%async_computation.11 | async-start | bytes 262144 | tf_op jit(solution)/shard_map/all_to_all | solution.py:46
  187.7 4.5 %fusion.39 = f32[8,128,128,1]{2,0,1,3:T(8,128)S(1)} fusion(bf16[1,1,128,128,128]{4,3,2,1,0:T(8,128)(2,1)} %param.11, bf16[128,8,128]{2,1,0:T(8,128)(2,1)S(1)} %gather_fusion.7, f32[128]{0:T(128)S(1)} %compare_convert_fusion, pred[128]{0:T(512)(128)(4,1)S(1)} %get-tuple-element.37), kind=kOutput, calls=%fused_computation.30 | convolution fusion | flops 33816576 | bytes 4981376 | tf_op jit(solution)/shard_map/sut,cst->csu/dot_general | solution.py:81
  192.5 0.8 copy.118
  193.4 2.6 %all-to-all-done.11 = bf16[16,8,512]{2,1,0:T(8,128)(2,1)S(1)} async-done(((bf16[16,8,512]{2,1,0:T(8,128)(2,1)}), bf16[16,8,512]{2,1,0:T(8,128)(2,1)S(1)}, u32[]{:S(2)}, u32[]{:S(2)}) %all-to-all-start.11) | async-done | bytes 131104 | tf_op jit(solution)/shard_map/all_to_all | solution.py:46
  195.9 6.5 %all-to-all-start.12 = ((f32[16,8,512]{2,1,0:T(8,128)}), f32[16,8,512]{2,1,0:T(8,128)S(1)}, u32[]{:S(2)}, u32[]{:S(2)}) async-start(f32[16,8,512]{2,1,0:T(8,128)} %bitcast.237), calls=%async_computation.12 | async-start | bytes 524288 | tf_op jit(solution)/shard_map/all_to_all | solution.py:51
  203.1 3.4 %fusion.45 = f32[8,128,128,1]{2,0,1,3:T(8,128)S(1)} fusion(bf16[1,1,128,128,128]{4,3,2,1,0:T(8,128)(2,1)} %param.11, bf16[128,8,128]{2,1,0:T(8,128)(2,1)S(1)} %gather_fusion.8, f32[128]{0:T(128)S(1)} %compare_select_fusion.1, pred[128]{0:T(512)(128)(4,1)S(1)} %get-tuple-element.29), kind=kOutput, calls=%fused_computation.32 | convolution fusion | flops 33816576 | bytes 4981376 | tf_op jit(solution)/shard_map/sut,csu->cst/dot_general | solution.py:93
  206.9 0.9 copy.117
  207.8 4.2 %all-to-all-done.12 = f32[16,8,512]{2,1,0:T(8,128)S(1)} async-done(((f32[16,8,512]{2,1,0:T(8,128)}), f32[16,8,512]{2,1,0:T(8,128)S(1)}, u32[]{:S(2)}, u32[]{:S(2)}) %all-to-all-start.12) | async-done | bytes 262176 | tf_op jit(solution)/shard_map/all_to_all | solution.py:51
  212.0 6.3 %all-to-all-start.13 = ((f32[16,8,512]{2,1,0:T(8,128)}), f32[16,8,512]{2,1,0:T(8,128)S(1)}, u32[]{:S(2)}, u32[]{:S(2)}) async-start(f32[16,8,512]{2,1,0:T(8,128)} %bitcast.236), calls=%async_computation.13 | async-start | bytes 524288 | tf_op jit(solution)/shard_map/all_to_all | solution.py:51
  218.6 6.9 %all-to-all-done.13 = f32[16,8,512]{2,1,0:T(8,128)S(1)} async-done(((f32[16,8,512]{2,1,0:T(8,128)}), f32[16,8,512]{2,1,0:T(8,128)S(1)}, u32[]{:S(2)}, u32[]{:S(2)}) %all-to-all-start.13) | async-done | bytes 262176 | tf_op jit(solution)/shard_map/all_to_all | solution.py:51
  226.0 18.8 %all_to_all.87 = f32[256,1,128]{2,1,0:T(1,128)S(1)} all-to-all(f32[256,1,128]{2,1,0:T(1,128)S(1)} %bitcast.253), channel_id=1, replica_groups=mesh['row'=16,'col'=16] {'row','col'}, dimensions={0} | all-to-all | bytes 262144 | tf_op jit(solution)/shard_map/all_to_all | solution.py:62
  248.7 0.8 fusion.191
  249.7 0.7 fusion.193
  (139 shorter events, 27.5 us)
Async XLA Ops:
  2.8 13.2 %all-to-all-start = ((bf16[16,36,128]{2,1,0:T(8,128)(2,1)}), bf16[16,36,128]{2,1,0:T(8,128)(2,1)S(1)}, u32[]{:S(2)}, u32[]{:S(2)}) async-start(bf16[16,36,128]{2,1,0:T(8,128)(2,1)} %broadcast_in_dim.61), calls=%async_computation | async-start | bytes 327680 | tf_op jit(solution)/shard_map/all_to_all | solution.py:46
  16.0 19.6 %all-to-all-start.1 = ((bf16[16,36,128]{2,1,0:T(8,128)(2,1)}), bf16[16,36,128]{2,1,0:T(8,128)(2,1)S(1)}, u32[]{:S(2)}, u32[]{:S(2)}) async-start(bf16[16,36,128]{2,1,0:T(8,128)(2,1)} %broadcast_in_dim.61), calls=%async_computation.1 | async-start | bytes 327680 | tf_op jit(solution)/shard_map/all_to_all | solution.py:46
  32.3 11.0 %copy-start.2 = (s32[1,1,2,128]{3,2,1,0:T(2,128)S(1)}, s32[1,1,2,128]{3,2,1,0:T(2,128)}, u32[]{:S(2)}) copy-start(s32[1,1,2,128]{3,2,1,0:T(2,128)} %param.12) | copy-start | bytes 3076
  36.9 17.1 %all-to-all-start.2 = ((f32[16,36,128]{2,1,0:T(8,128)}), f32[16,36,128]{2,1,0:T(8,128)S(1)}, u32[]{:S(2)}, u32[]{:S(2)}) async-start(f32[16,36,128]{2,1,0:T(8,128)} %reshape.290), calls=%async_computation.2 | async-start | bytes 655360 | tf_op jit(solution)/shard_map/all_to_all | solution.py:51
  44.2 17.2 %copy-start = (f32[8,512]{1,0:T(8,128)S(1)}, f32[8,512]{1,0:T(8,128)}, u32[]{:S(2)}) copy-start(f32[8,512]{1,0:T(8,128)} %param.15) | copy-start | bytes 49156
  44.2 32.6 %copy-start.1 = (f32[2,8,24]{2,1,0:T(8,128)S(1)}, f32[2,8,24]{2,1,0:T(8,128)}, u32[]{:S(2)}) copy-start(f32[2,8,24]{2,1,0:T(8,128)} %param.16) | copy-start | bytes 4612
  55.0 14.1 %all-to-all-start.3 = ((f32[16,36,128]{2,1,0:T(8,128)}), f32[16,36,128]{2,1,0:T(8,128)S(1)}, u32[]{:S(2)}, u32[]{:S(2)}) async-start(f32[16,36,128]{2,1,0:T(8,128)} %reshape.294), calls=%async_computation.3 | async-start | bytes 655360 | tf_op jit(solution)/shard_map/all_to_all | solution.py:51
  70.1 19.2 %all-to-all-start.4 = ((f32[256,1,128]{2,1,0:T(1,128)}), f32[256,1,128]{2,1,0:T(1,128)S(1)}, u32[]{:S(2)}, u32[]{:S(2)}) async-start(f32[256,1,128]{2,1,0:T(1,128)} %bitcast.18), calls=%async_computation.4 | async-start | bytes 262144 | tf_op jit(solution)/shard_map/all_to_all | solution.py:62
  94.7 10.6 %all-to-all-start.5 = ((bf16[16,8,512]{2,1,0:T(8,128)(2,1)}), bf16[16,8,512]{2,1,0:T(8,128)(2,1)S(1)}, u32[]{:S(2)}, u32[]{:S(2)}) async-start(bf16[16,8,512]{2,1,0:T(8,128)(2,1)} %broadcast_in_dim.67), calls=%async_computation.5 | async-start | bytes 262144 | tf_op jit(solution)/shard_map/all_to_all | solution.py:46
  105.3 12.5 %all-to-all-start.6 = ((bf16[16,8,512]{2,1,0:T(8,128)(2,1)}), bf16[16,8,512]{2,1,0:T(8,128)(2,1)S(1)}, u32[]{:S(2)}, u32[]{:S(2)}) async-start(bf16[16,8,512]{2,1,0:T(8,128)(2,1)} %broadcast_in_dim.67), calls=%async_computation.6 | async-start | bytes 262144 | tf_op jit(solution)/shard_map/all_to_all | solution.py:46
  117.8 16.1 %all-to-all-start.7 = ((f32[16,8,512]{2,1,0:T(8,128)}), f32[16,8,512]{2,1,0:T(8,128)S(1)}, u32[]{:S(2)}, u32[]{:S(2)}) async-start(f32[16,8,512]{2,1,0:T(8,128)} %bitcast.239), calls=%async_computation.7 | async-start | bytes 524288 | tf_op jit(solution)/shard_map/all_to_all | solution.py:51
  133.9 13.5 %all-to-all-start.8 = ((f32[16,8,512]{2,1,0:T(8,128)}), f32[16,8,512]{2,1,0:T(8,128)S(1)}, u32[]{:S(2)}, u32[]{:S(2)}) async-start(f32[16,8,512]{2,1,0:T(8,128)} %bitcast.238), calls=%async_computation.8 | async-start | bytes 524288 | tf_op jit(solution)/shard_map/all_to_all | solution.py:51
  148.6 18.9 %all-to-all-start.9 = ((f32[256,1,128]{2,1,0:T(1,128)}), f32[256,1,128]{2,1,0:T(1,128)S(1)}, u32[]{:S(2)}, u32[]{:S(2)}) async-start(f32[256,1,128]{2,1,0:T(1,128)} %bitcast.37), calls=%async_computation.9 | async-start | bytes 262144 | tf_op jit(solution)/shard_map/all_to_all | solution.py:62
  172.9 10.6 %all-to-all-start.10 = ((bf16[16,8,512]{2,1,0:T(8,128)(2,1)}), bf16[16,8,512]{2,1,0:T(8,128)(2,1)S(1)}, u32[]{:S(2)}, u32[]{:S(2)}) async-start(bf16[16,8,512]{2,1,0:T(8,128)(2,1)} %broadcast_in_dim.72), calls=%async_computation.10 | async-start | bytes 262144 | tf_op jit(solution)/shard_map/all_to_all | solution.py:46
  183.4 12.5 %all-to-all-start.11 = ((bf16[16,8,512]{2,1,0:T(8,128)(2,1)}), bf16[16,8,512]{2,1,0:T(8,128)(2,1)S(1)}, u32[]{:S(2)}, u32[]{:S(2)}) async-start(bf16[16,8,512]{2,1,0:T(8,128)(2,1)} %broadcast_in_dim.72), calls=%async_computation.11 | async-start | bytes 262144 | tf_op jit(solution)/shard_map/all_to_all | solution.py:46
  195.9 16.0 %all-to-all-start.12 = ((f32[16,8,512]{2,1,0:T(8,128)}), f32[16,8,512]{2,1,0:T(8,128)S(1)}, u32[]{:S(2)}, u32[]{:S(2)}) async-start(f32[16,8,512]{2,1,0:T(8,128)} %bitcast.237), calls=%async_computation.12 | async-start | bytes 524288 | tf_op jit(solution)/shard_map/all_to_all | solution.py:51
  212.0 13.5 %all-to-all-start.13 = ((f32[16,8,512]{2,1,0:T(8,128)}), f32[16,8,512]{2,1,0:T(8,128)S(1)}, u32[]{:S(2)}, u32[]{:S(2)}) async-start(f32[16,8,512]{2,1,0:T(8,128)} %bitcast.236), calls=%async_computation.13 | async-start | bytes 524288 | tf_op jit(solution)/shard_map/all_to_all | solution.py:51

commit v12 on v7

--- a/solution.py
+++ b/solution.py
@@ -21,7 +21,7 @@
 
 
 def settle(new_vecs, new_images, new_steps, step_images, gram_x, gram_ax, node_total):
-    lower_factor = jnp.linalg.cholesky(gram_x / node_total)
+    lower_factor = jnp.linalg.cholesky(gram_x / node_total, symmetrize_input=False)
     inverse = lower_inverse(lower_factor)
     theta = matmul_high(matmul_high(inverse, gram_ax / node_total), inverse.T)
     return (

time: 251 us -> 251 us (level)
  no operation moved by 1% of the time
where the time goes in v12:
time: 251 us; the launch traced here: 250 us
  starting transfers between devices  84.3 us (34%)
  waiting for transfers between devices  84.2 us (34%)
  matrix products  33.7 us (13%)
  blocking collectives  18.8 us (7%)
  local copies, waits for them, and re-layouts  17.8 us (7%)
  other arithmetic  9.14 us (4%)
    all_to_all x6, starting transfers between devices, scatter_sum_by_exchange(): held = lax.all_to_all(dense_rows(chunks), axis, 0, 0, tiled=True)  38.1 us
    all_to_all x6, waiting for transfers between devices, scatter_sum_by_exchange(): held = lax.all_to_all(dense_rows(chunks), axis, 0, 0, tiled=True)  35.5 us
    all_to_all x6, starting transfers between devices, gather_by_exchange(): lax.all_to_all(dense_rows(copies), axis, 0, 0, tiled=True)  33.3 us
    all_to_all x2, waiting for transfers between devices, gram_sums(): held = lax.all_to_all(copies, ('row', 'col'), 0, 0, tiled=True)  24.8 us
    all_to_all x6, waiting for transfers between devices, gather_by_exchange(): lax.all_to_all(dense_rows(copies), axis, 0, 0, tiled=True)  23.9 us
    all_to_all x1, blocking collectives, gram_sums(): held = lax.all_to_all(copies, ('row', 'col'), 0, 0, tiled=True)  18.8 us
    dot_general x3, matrix products, direct_terms(): jnp.einsum('sut,cst->csu', part_tiles, col_values, preferred_element_type...  13.5 us
    all_to_all x2, starting transfers between devices, gram_sums(): held = lax.all_to_all(copies, ('row', 'col'), 0, 0, tiled=True)  12.9 us
  transfers between devices with their start and end apart: 14, of which 14 were waited for; matrix products, arithmetic and copies ran while one was open for 15% of the time, Pallas kernels for 0%

profile of v12, /device:TPU:1, one launch (start us, length us, event | category | flops | bytes accessed | tf_op | source)
XLA Modules:
  0.0 249.6 jit_solution(11199938932209764750)
XLA Ops:
  1.3 0.7 fusion.137
  2.8 6.8 %all-to-all-start = ((bf16[16,36,128]{2,1,0:T(8,128)(2,1)}), bf16[16,36,128]{2,1,0:T(8,128)(2,1)S(1)}, u32[]{:S(2)}, u32[]{:S(2)}) async-start(bf16[16,36,128]{2,1,0:T(8,128)(2,1)} %broadcast_in_dim.38), calls=%async_computation | async-start | bytes 327680 | tf_op jit(solution)/shard_map/all_to_all | solution.py:46
  9.6 0.8 compare_and_fusion
  10.4 0.8 slice_bitcast_fusion.2
  11.8 4.2 %all-to-all-done = bf16[16,36,128]{2,1,0:T(8,128)(2,1)S(1)} async-done(((bf16[16,36,128]{2,1,0:T(8,128)(2,1)}), bf16[16,36,128]{2,1,0:T(8,128)(2,1)S(1)}, u32[]{:S(2)}, u32[]{:S(2)}) %all-to-all-start) | async-done | bytes 147488 | tf_op jit(solution)/shard_map/all_to_all | solution.py:46
  16.0 10.6 %all-to-all-start.1 = ((bf16[16,36,128]{2,1,0:T(8,128)(2,1)}), bf16[16,36,128]{2,1,0:T(8,128)(2,1)S(1)}, u32[]{:S(2)}, u32[]{:S(2)}) async-start(bf16[16,36,128]{2,1,0:T(8,128)(2,1)} %broadcast_in_dim.38), calls=%async_computation.1 | async-start | bytes 327680 | tf_op jit(solution)/shard_map/all_to_all | solution.py:46
  27.7 4.5 %fusion.15 = f32[9,128,128,1]{2,0,1,3:T(8,128)S(1)} fusion(bf16[1,1,128,128,128]{4,3,2,1,0:T(8,128)(2,1)} %param.11, bf16[128,9,128]{2,1,0:T(8,128)(2,1)S(1)} %gather_fusion.3, f32[128]{0:T(128)S(1)} %compare_convert_fusion, pred[128]{0:T(512)(128)(4,1)S(1)} %get-tuple-element.37), kind=kOutput, calls=%fused_computation.22 | convolution fusion | flops 38043648 | bytes 5079680 | tf_op jit(solution)/shard_map/sut,cst->csu/dot_general | solution.py:81
  32.8 2.8 %all-to-all-done.1 = bf16[16,36,128]{2,1,0:T(8,128)(2,1)S(1)} async-done(((bf16[16,36,128]{2,1,0:T(8,128)(2,1)}), bf16[16,36,128]{2,1,0:T(8,128)(2,1)S(1)}, u32[]{:S(2)}, u32[]{:S(2)}) %all-to-all-start.1) | async-done | bytes 147488 | tf_op jit(solution)/shard_map/all_to_all | solution.py:46
  36.1 0.8 reshape.309
  36.9 6.3 %all-to-all-start.2 = ((f32[16,36,128]{2,1,0:T(8,128)}), f32[16,36,128]{2,1,0:T(8,128)S(1)}, u32[]{:S(2)}, u32[]{:S(2)}) async-start(f32[16,36,128]{2,1,0:T(8,128)} %reshape.309), calls=%async_computation.2 | async-start | bytes 655360 | tf_op jit(solution)/shard_map/all_to_all | solution.py:51
  44.2 3.5 %fusion.21 = f32[9,128,128,1]{2,0,1,3:T(8,128)S(1)} fusion(bf16[1,1,128,128,128]{4,3,2,1,0:T(8,128)(2,1)} %param.11, bf16[128,9,128]{2,1,0:T(8,128)(2,1)S(1)} %gather_fusion.4, f32[128]{0:T(128)S(1)} %compare_select_fusion.1, pred[128]{0:T(512)(128)(4,1)S(1)} %get-tuple-element.29), kind=kOutput, calls=%fused_computation.24 | convolution fusion | flops 38043648 | bytes 5079680 | tf_op jit(solution)/shard_map/sut,csu->cst/dot_general | solution.py:93
  48.2 5.8 %all-to-all-done.2 = f32[16,36,128]{2,1,0:T(8,128)S(1)} async-done(((f32[16,36,128]{2,1,0:T(8,128)}), f32[16,36,128]{2,1,0:T(8,128)S(1)}, u32[]{:S(2)}, u32[]{:S(2)}) %all-to-all-start.2) | async-done | bytes 294944 | tf_op jit(solution)/shard_map/all_to_all | solution.py:51
  54.2 0.8 reshape.313
  55.0 6.4 %all-to-all-start.3 = ((f32[16,36,128]{2,1,0:T(8,128)}), f32[16,36,128]{2,1,0:T(8,128)S(1)}, u32[]{:S(2)}, u32[]{:S(2)}) async-start(f32[16,36,128]{2,1,0:T(8,128)} %reshape.313), calls=%async_computation.3 | async-start | bytes 655360 | tf_op jit(solution)/shard_map/all_to_all | solution.py:51
  61.6 7.5 %all-to-all-done.3 = f32[16,36,128]{2,1,0:T(8,128)S(1)} async-done(((f32[16,36,128]{2,1,0:T(8,128)}), f32[16,36,128]{2,1,0:T(8,128)S(1)}, u32[]{:S(2)}, u32[]{:S(2)}) %all-to-all-start.3) | async-done | bytes 294944 | tf_op jit(solution)/shard_map/all_to_all | solution.py:51
  69.5 0.7 broadcast_in_dim.39
  70.2 6.6 %all-to-all-start.4 = ((f32[256,1,128]{2,1,0:T(1,128)}), f32[256,1,128]{2,1,0:T(1,128)S(1)}, u32[]{:S(2)}, u32[]{:S(2)}) async-start(f32[256,1,128]{2,1,0:T(1,128)} %broadcast_in_dim.39), calls=%async_computation.4 | async-start | bytes 262144 | tf_op jit(solution)/shard_map/all_to_all | solution.py:62
  76.8 12.6 %all-to-all-done.4 = f32[256,1,128]{2,1,0:T(1,128)S(1)} async-done(((f32[256,1,128]{2,1,0:T(1,128)}), f32[256,1,128]{2,1,0:T(1,128)S(1)}, u32[]{:S(2)}, u32[]{:S(2)}) %all-to-all-start.4) | async-done | bytes 131104 | tf_op jit(solution)/shard_map/all_to_all | solution.py:62
  94.5 4.4 %all-to-all-start.5 = ((bf16[16,8,512]{2,1,0:T(8,128)(2,1)}), bf16[16,8,512]{2,1,0:T(8,128)(2,1)S(1)}, u32[]{:S(2)}, u32[]{:S(2)}) async-start(bf16[16,8,512]{2,1,0:T(8,128)(2,1)} %broadcast_in_dim.41), calls=%async_computation.5 | async-start | bytes 262144 | tf_op jit(solution)/shard_map/all_to_all | solution.py:46
  99.0 6.0 %all-to-all-done.5 = bf16[16,8,512]{2,1,0:T(8,128)(2,1)S(1)} async-done(((bf16[16,8,512]{2,1,0:T(8,128)(2,1)}), bf16[16,8,512]{2,1,0:T(8,128)(2,1)S(1)}, u32[]{:S(2)}, u32[]{:S(2)}) %all-to-all-start.5) | async-done | bytes 131104 | tf_op jit(solution)/shard_map/all_to_all | solution.py:46
  105.0 3.5 %all-to-all-start.6 = ((bf16[16,8,512]{2,1,0:T(8,128)(2,1)}), bf16[16,8,512]{2,1,0:T(8,128)(2,1)S(1)}, u32[]{:S(2)}, u32[]{:S(2)}) async-start(bf16[16,8,512]{2,1,0:T(8,128)(2,1)} %broadcast_in_dim.41), calls=%async_computation.6 | async-start | bytes 262144 | tf_op jit(solution)/shard_map/all_to_all | solution.py:46
  109.3 4.5 %fusion.27 = f32[8,128,128,1]{2,0,1,3:T(8,128)S(1)} fusion(bf16[1,1,128,128,128]{4,3,2,1,0:T(8,128)(2,1)} %param.11, bf16[128,8,128]{2,1,0:T(8,128)(2,1)S(1)} %gather_fusion.5, f32[128]{0:T(128)S(1)} %compare_convert_fusion, pred[128]{0:T(512)(128)(4,1)S(1)} %get-tuple-element.37), kind=kOutput, calls=%fused_computation.26 | convolution fusion | flops 33816576 | bytes 4981376 | tf_op jit(solution)/shard_map/sut,cst->csu/dot_general | solution.py:81
  114.1 0.8 copy.155
  115.0 2.6 %all-to-all-done.6 = bf16[16,8,512]{2,1,0:T(8,128)(2,1)S(1)} async-done(((bf16[16,8,512]{2,1,0:T(8,128)(2,1)}), bf16[16,8,512]{2,1,0:T(8,128)(2,1)S(1)}, u32[]{:S(2)}, u32[]{:S(2)}) %all-to-all-start.6) | async-done | bytes 131104 | tf_op jit(solution)/shard_map/all_to_all | solution.py:46
  117.5 6.5 %all-to-all-start.7 = ((f32[16,8,512]{2,1,0:T(8,128)}), f32[16,8,512]{2,1,0:T(8,128)S(1)}, u32[]{:S(2)}, u32[]{:S(2)}) async-start(f32[16,8,512]{2,1,0:T(8,128)} %bitcast.227), calls=%async_computation.7 | async-start | bytes 524288 | tf_op jit(solution)/shard_map/all_to_all | solution.py:51
  124.7 3.4 %fusion.33 = f32[8,128,128,1]{2,0,1,3:T(8,128)S(1)} fusion(bf16[1,1,128,128,128]{4,3,2,1,0:T(8,128)(2,1)} %param.11, bf16[128,8,128]{2,1,0:T(8,128)(2,1)S(1)} %gather_fusion.6, f32[128]{0:T(128)S(1)} %compare_select_fusion.1, pred[128]{0:T(512)(128)(4,1)S(1)} %get-tuple-element.29), kind=kOutput, calls=%fused_computation.28 | convolution fusion | flops 33816576 | bytes 4981376 | tf_op jit(solution)/shard_map/sut,csu->cst/dot_general | solution.py:93
  128.5 0.9 copy.154
  129.4 4.2 %all-to-all-done.7 = f32[16,8,512]{2,1,0:T(8,128)S(1)} async-done(((f32[16,8,512]{2,1,0:T(8,128)}), f32[16,8,512]{2,1,0:T(8,128)S(1)}, u32[]{:S(2)}, u32[]{:S(2)}) %all-to-all-start.7) | async-done | bytes 262176 | tf_op jit(solution)/shard_map/all_to_all | solution.py:51
  133.6 6.2 %all-to-all-start.8 = ((f32[16,8,512]{2,1,0:T(8,128)}), f32[16,8,512]{2,1,0:T(8,128)S(1)}, u32[]{:S(2)}, u32[]{:S(2)}) async-start(f32[16,8,512]{2,1,0:T(8,128)} %bitcast.226), calls=%async_computation.8 | async-start | bytes 524288 | tf_op jit(solution)/shard_map/all_to_all | solution.py:51
  140.3 6.9 %all-to-all-done.8 = f32[16,8,512]{2,1,0:T(8,128)S(1)} async-done(((f32[16,8,512]{2,1,0:T(8,128)}), f32[16,8,512]{2,1,0:T(8,128)S(1)}, u32[]{:S(2)}, u32[]{:S(2)}) %all-to-all-start.8) | async-done | bytes 262176 | tf_op jit(solution)/shard_map/all_to_all | solution.py:51
  147.6 0.7 broadcast_in_dim.45
  148.4 6.3 %all-to-all-start.9 = ((f32[256,1,128]{2,1,0:T(1,128)}), f32[256,1,128]{2,1,0:T(1,128)S(1)}, u32[]{:S(2)}, u32[]{:S(2)}) async-start(f32[256,1,128]{2,1,0:T(1,128)} %broadcast_in_dim.45), calls=%async_computation.9 | async-start | bytes 262144 | tf_op jit(solution)/shard_map/all_to_all | solution.py:62
  155.1 12.2 %all-to-all-done.9 = f32[256,1,128]{2,1,0:T(1,128)S(1)} async-done(((f32[256,1,128]{2,1,0:T(1,128)}), f32[256,1,128]{2,1,0:T(1,128)S(1)}, u32[]{:S(2)}, u32[]{:S(2)}) %all-to-all-start.9) | async-done | bytes 131104 | tf_op jit(solution)/shard_map/all_to_all | solution.py:62
  172.3 4.4 %all-to-all-start.10 = ((bf16[16,8,512]{2,1,0:T(8,128)(2,1)}), bf16[16,8,512]{2,1,0:T(8,128)(2,1)S(1)}, u32[]{:S(2)}, u32[]{:S(2)}) async-start(bf16[16,8,512]{2,1,0:T(8,128)(2,1)} %broadcast_in_dim.46), calls=%async_computation.10 | async-start | bytes 262144 | tf_op jit(solution)/shard_map/all_to_all | solution.py:46
  177.1 5.9 %all-to-all-done.10 = bf16[16,8,512]{2,1,0:T(8,128)(2,1)S(1)} async-done(((bf16[16,8,512]{2,1,0:T(8,128)(2,1)}), bf16[16,8,512]{2,1,0:T(8,128)(2,1)S(1)}, u32[]{:S(2)}, u32[]{:S(2)}) %all-to-all-start.10) | async-done | bytes 131104 | tf_op jit(solution)/shard_map/all_to_all | solution.py:46
  182.9 3.5 %all-to-all-start.11 = ((bf16[16,8,512]{2,1,0:T(8,128)(2,1)}), bf16[16,8,512]{2,1,0:T(8,128)(2,1)S(1)}, u32[]{:S(2)}, u32[]{:S(2)}) async-start(bf16[16,8,512]{2,1,0:T(8,128)(2,1)} %broadcast_in_dim.46), calls=%async_computation.11 | async-start | bytes 262144 | tf_op jit(solution)/shard_map/all_to_all | solution.py:46
  187.1 4.5 %fusion.39 = f32[8,128,128,1]{2,0,1,3:T(8,128)S(1)} fusion(bf16[1,1,128,128,128]{4,3,2,1,0:T(8,128)(2,1)} %param.11, bf16[128,8,128]{2,1,0:T(8,128)(2,1)S(1)} %gather_fusion.7, f32[128]{0:T(128)S(1)} %compare_convert_fusion, pred[128]{0:T(512)(128)(4,1)S(1)} %get-tuple-element.37), kind=kOutput, calls=%fused_computation.30 | convolution fusion | flops 33816576 | bytes 4981376 | tf_op jit(solution)/shard_map/sut,cst->csu/dot_general | solution.py:81
  192.0 0.8 copy.153
  192.9 2.6 %all-to-all-done.11 = bf16[16,8,512]{2,1,0:T(8,128)(2,1)S(1)} async-done(((bf16[16,8,512]{2,1,0:T(8,128)(2,1)}), bf16[16,8,512]{2,1,0:T(8,128)(2,1)S(1)}, u32[]{:S(2)}, u32[]{:S(2)}) %all-to-all-start.11) | async-done | bytes 131104 | tf_op jit(solution)/shard_map/all_to_all | solution.py:46
  195.4 6.5 %all-to-all-start.12 = ((f32[16,8,512]{2,1,0:T(8,128)}), f32[16,8,512]{2,1,0:T(8,128)S(1)}, u32[]{:S(2)}, u32[]{:S(2)}) async-start(f32[16,8,512]{2,1,0:T(8,128)} %bitcast.225), calls=%async_computation.12 | async-start | bytes 524288 | tf_op jit(solution)/shard_map/all_to_all | solution.py:51
  202.6 3.4 %fusion.45 = f32[8,128,128,1]{2,0,1,3:T(8,128)S(1)} fusion(bf16[1,1,128,128,128]{4,3,2,1,0:T(8,128)(2,1)} %param.11, bf16[128,8,128]{2,1,0:T(8,128)(2,1)S(1)} %gather_fusion.8, f32[128]{0:T(128)S(1)} %compare_select_fusion.1, pred[128]{0:T(512)(128)(4,1)S(1)} %get-tuple-element.29), kind=kOutput, calls=%fused_computation.32 | convolution fusion | flops 33816576 | bytes 4981376 | tf_op jit(solution)/shard_map/sut,csu->cst/dot_general | solution.py:93
  206.4 0.9 copy.152
  207.3 4.2 %all-to-all-done.12 = f32[16,8,512]{2,1,0:T(8,128)S(1)} async-done(((f32[16,8,512]{2,1,0:T(8,128)}), f32[16,8,512]{2,1,0:T(8,128)S(1)}, u32[]{:S(2)}, u32[]{:S(2)}) %all-to-all-start.12) | async-done | bytes 262176 | tf_op jit(solution)/shard_map/all_to_all | solution.py:51
  211.5 6.3 %all-to-all-start.13 = ((f32[16,8,512]{2,1,0:T(8,128)}), f32[16,8,512]{2,1,0:T(8,128)S(1)}, u32[]{:S(2)}, u32[]{:S(2)}) async-start(f32[16,8,512]{2,1,0:T(8,128)} %bitcast.224), calls=%async_computation.13 | async-start | bytes 524288 | tf_op jit(solution)/shard_map/all_to_all | solution.py:51
  218.1 6.9 %all-to-all-done.13 = f32[16,8,512]{2,1,0:T(8,128)S(1)} async-done(((f32[16,8,512]{2,1,0:T(8,128)}), f32[16,8,512]{2,1,0:T(8,128)S(1)}, u32[]{:S(2)}, u32[]{:S(2)}) %all-to-all-start.13) | async-done | bytes 262176 | tf_op jit(solution)/shard_map/all_to_all | solution.py:51
  225.6 18.8 %all_to_all.78 = f32[256,1,128]{2,1,0:T(1,128)S(1)} all-to-all(f32[256,1,128]{2,1,0:T(1,128)S(1)} %broadcast_in_dim.47), channel_id=1, replica_groups=mesh['row'=16,'col'=16] {'row','col'}, dimensions={0} | all-to-all | bytes 262144 | tf_op jit(solution)/shard_map/all_to_all | solution.py:62
  247.9 0.8 fusion.188
  248.9 0.7 fusion.190
  (133 shorter events, 26.7 us)
Async XLA Ops:
  2.8 13.2 %all-to-all-start = ((bf16[16,36,128]{2,1,0:T(8,128)(2,1)}), bf16[16,36,128]{2,1,0:T(8,128)(2,1)S(1)}, u32[]{:S(2)}, u32[]{:S(2)}) async-start(bf16[16,36,128]{2,1,0:T(8,128)(2,1)} %broadcast_in_dim.38), calls=%async_computation | async-start | bytes 327680 | tf_op jit(solution)/shard_map/all_to_all | solution.py:46
  16.0 19.6 %all-to-all-start.1 = ((bf16[16,36,128]{2,1,0:T(8,128)(2,1)}), bf16[16,36,128]{2,1,0:T(8,128)(2,1)S(1)}, u32[]{:S(2)}, u32[]{:S(2)}) async-start(bf16[16,36,128]{2,1,0:T(8,128)(2,1)} %broadcast_in_dim.38), calls=%async_computation.1 | async-start | bytes 327680 | tf_op jit(solution)/shard_map/all_to_all | solution.py:46
  32.3 11.0 %copy-start.2 = (s32[1,1,2,128]{3,2,1,0:T(2,128)S(1)}, s32[1,1,2,128]{3,2,1,0:T(2,128)}, u32[]{:S(2)}) copy-start(s32[1,1,2,128]{3,2,1,0:T(2,128)} %param.12) | copy-start | bytes 3076
  36.9 17.1 %all-to-all-start.2 = ((f32[16,36,128]{2,1,0:T(8,128)}), f32[16,36,128]{2,1,0:T(8,128)S(1)}, u32[]{:S(2)}, u32[]{:S(2)}) async-start(f32[16,36,128]{2,1,0:T(8,128)} %reshape.309), calls=%async_computation.2 | async-start | bytes 655360 | tf_op jit(solution)/shard_map/all_to_all | solution.py:51
  44.2 17.2 %copy-start = (f32[8,512]{1,0:T(8,128)S(1)}, f32[8,512]{1,0:T(8,128)}, u32[]{:S(2)}) copy-start(f32[8,512]{1,0:T(8,128)} %param.15) | copy-start | bytes 49156
  44.2 32.6 %copy-start.1 = (f32[2,8,24]{2,1,0:T(8,128)S(1)}, f32[2,8,24]{2,1,0:T(8,128)}, u32[]{:S(2)}) copy-start(f32[2,8,24]{2,1,0:T(8,128)} %param.16) | copy-start | bytes 4612
  55.0 14.1 %all-to-all-start.3 = ((f32[16,36,128]{2,1,0:T(8,128)}), f32[16,36,128]{2,1,0:T(8,128)S(1)}, u32[]{:S(2)}, u32[]{:S(2)}) async-start(f32[16,36,128]{2,1,0:T(8,128)} %reshape.313), calls=%async_computation.3 | async-start | bytes 655360 | tf_op jit(solution)/shard_map/all_to_all | solution.py:51
  70.2 19.2 %all-to-all-start.4 = ((f32[256,1,128]{2,1,0:T(1,128)}), f32[256,1,128]{2,1,0:T(1,128)S(1)}, u32[]{:S(2)}, u32[]{:S(2)}) async-start(f32[256,1,128]{2,1,0:T(1,128)} %broadcast_in_dim.39), calls=%async_computation.4 | async-start | bytes 262144 | tf_op jit(solution)/shard_map/all_to_all | solution.py:62
  94.5 10.6 %all-to-all-start.5 = ((bf16[16,8,512]{2,1,0:T(8,128)(2,1)}), bf16[16,8,512]{2,1,0:T(8,128)(2,1)S(1)}, u32[]{:S(2)}, u32[]{:S(2)}) async-start(bf16[16,8,512]{2,1,0:T(8,128)(2,1)} %broadcast_in_dim.41), calls=%async_computation.5 | async-start | bytes 262144 | tf_op jit(solution)/shard_map/all_to_all | solution.py:46
  105.0 12.5 %all-to-all-start.6 = ((bf16[16,8,512]{2,1,0:T(8,128)(2,1)}), bf16[16,8,512]{2,1,0:T(8,128)(2,1)S(1)}, u32[]{:S(2)}, u32[]{:S(2)}) async-start(bf16[16,8,512]{2,1,0:T(8,128)(2,1)} %broadcast_in_dim.41), calls=%async_computation.6 | async-start | bytes 262144 | tf_op jit(solution)/shard_map/all_to_all | solution.py:46
  117.5 16.1 %all-to-all-start.7 = ((f32[16,8,512]{2,1,0:T(8,128)}), f32[16,8,512]{2,1,0:T(8,128)S(1)}, u32[]{:S(2)}, u32[]{:S(2)}) async-start(f32[16,8,512]{2,1,0:T(8,128)} %bitcast.227), calls=%async_computation.7 | async-start | bytes 524288 | tf_op jit(solution)/shard_map/all_to_all | solution.py:51
  133.6 13.5 %all-to-all-start.8 = ((f32[16,8,512]{2,1,0:T(8,128)}), f32[16,8,512]{2,1,0:T(8,128)S(1)}, u32[]{:S(2)}, u32[]{:S(2)}) async-start(f32[16,8,512]{2,1,0:T(8,128)} %bitcast.226), calls=%async_computation.8 | async-start | bytes 524288 | tf_op jit(solution)/shard_map/all_to_all | solution.py:51
  148.4 18.9 %all-to-all-start.9 = ((f32[256,1,128]{2,1,0:T(1,128)}), f32[256,1,128]{2,1,0:T(1,128)S(1)}, u32[]{:S(2)}, u32[]{:S(2)}) async-start(f32[256,1,128]{2,1,0:T(1,128)} %broadcast_in_dim.45), calls=%async_computation.9 | async-start | bytes 262144 | tf_op jit(solution)/shard_map/all_to_all | solution.py:62
  172.3 10.6 %all-to-all-start.10 = ((bf16[16,8,512]{2,1,0:T(8,128)(2,1)}), bf16[16,8,512]{2,1,0:T(8,128)(2,1)S(1)}, u32[]{:S(2)}, u32[]{:S(2)}) async-start(bf16[16,8,512]{2,1,0:T(8,128)(2,1)} %broadcast_in_dim.46), calls=%async_computation.10 | async-start | bytes 262144 | tf_op jit(solution)/shard_map/all_to_all | solution.py:46
  182.9 12.5 %all-to-all-start.11 = ((bf16[16,8,512]{2,1,0:T(8,128)(2,1)}), bf16[16,8,512]{2,1,0:T(8,128)(2,1)S(1)}, u32[]{:S(2)}, u32[]{:S(2)}) async-start(bf16[16,8,512]{2,1,0:T(8,128)(2,1)} %broadcast_in_dim.46), calls=%async_computation.11 | async-start | bytes 262144 | tf_op jit(solution)/shard_map/all_to_all | solution.py:46
  195.4 16.1 %all-to-all-start.12 = ((f32[16,8,512]{2,1,0:T(8,128)}), f32[16,8,512]{2,1,0:T(8,128)S(1)}, u32[]{:S(2)}, u32[]{:S(2)}) async-start(f32[16,8,512]{2,1,0:T(8,128)} %bitcast.225), calls=%async_computation.12 | async-start | bytes 524288 | tf_op jit(solution)/shard_map/all_to_all | solution.py:51
  211.5 13.5 %all-to-all-start.13 = ((f32[16,8,512]{2,1,0:T(8,128)}), f32[16,8,512]{2,1,0:T(8,128)S(1)}, u32[]{:S(2)}, u32[]{:S(2)}) async-start(f32[16,8,512]{2,1,0:T(8,128)} %bitcast.224), calls=%async_computation.13 | async-start | bytes 524288 | tf_op jit(solution)/shard_map/all_to_all | solution.py:51
